TPU v7x, 512 devices: a whole 4x8x8 slice. The times are simulated.
512 devices in a mesh: tm: 32 (over x_hi, y, core), cell: 16 (over z, x_lo).
Axes of the slice: x: 4 (x_hi: 2, x_lo: 2; x = x_hi * 2 + x_lo), y: 8, z: 8, core: 2. Of those that a mesh axis runs over, the one named last changes fastest.
Arguments:
- start_states: float32 [32, 3, 128, 2048], P('tm', None, None, 'cell'), may hold values from -6 to 6
- ocean_mask: int32 [128, 2048], P(None, 'cell'), may hold values 0 or 1
- depth_class: int32 [128, 2048], P(None, 'cell'), may hold values from 0 to 7
- class_depth: float32 [8], replicated, may hold values from 0.2 to 1
- drag_rate: float32 [128, 2048], P(None, 'cell'), may hold values from 0.02 to 0.3
- tide_cos: float32 [128, 2048], P(None, 'cell'), may hold values from -3 to 3
- tide_sin: float32 [128, 2048], P(None, 'cell'), may hold values from -3 to 3
Outputs:
- defect: float32 [32, 3, 128, 2048], P('tm', None, None, 'cell')
- state_grad: float32 [32, 3, 128, 2048], P('tm', None, None, 'cell')
- drag_grad: float32 [128, 2048], P('tm', 'cell')
All inputs are finite; a program needn't handle non-finite values. No bound on the sum of `ocean_mask` on one device may be relied on, other than what follows from the above.
Results may differ from a plain program's by a relative error of at most 0.00002.
Values sent between devices are 32-bit elements; how exact they have to be, the bound alone decides.
No kernel may reach another device: no remote copies, remote signals or barrier semaphores. Data moves between devices by JAX's collectives and lax.ppermute only.
A program may use at most 64 MiB of HBM per device.

v0:
```python
import math

import jax
import jax.numpy as jnp
from jax import lax
from jax.sharding import PartitionSpec as P

STEPS = 8


FLUX_RATE = 0.7
PRESS_RATE = 0.7
ROTATION_RATE = 0.15


def with_halo(block, sides, width):
    for axis, dim in sides:
        count = lax.axis_size(axis)
        forward = [(i, i + 1) for i in range(count - 1)]
        forward.append((count - 1, 0))
        backward = [(target, source) for source, target in forward]
        low = lax.ppermute(
            lax.slice_in_dim(block, block.shape[dim] - width, None, axis=dim), axis, forward
        )
        high = lax.ppermute(lax.slice_in_dim(block, 0, width, axis=dim), axis, backward)
        block = jnp.concatenate([low, block, high], axis=dim)
    return block


def from_behind(value, axis, steps):
    count = lax.axis_size(axis)
    pairs = [(source, (source + steps) % count) for source in range(count)]
    return lax.ppermute(value, axis, pairs)


def cropped(values_in, cut_width):
    if cut_width == 0:
        return values_in
    return values_in[..., cut_width : values_in.shape[-1] - cut_width]


def across_cols(values_in):
    return 0.5 * (values_in[..., 2:] - values_in[..., :-2])


def across_rows(values_in):
    zeros_row = jnp.zeros_like(values_in[..., :1, :])
    upper_rows = jnp.concatenate([values_in[..., 1:, :], zeros_row], axis=-2)
    lower_rows = jnp.concatenate([zeros_row, values_in[..., :-1, :]], axis=-2)
    return 0.5 * (upper_rows - lower_rows)


def coriolis(rows_count):
    latitude = math.pi * ((jnp.arange(rows_count, dtype=jnp.float32) + 0.5) / rows_count - 0.5)
    return (ROTATION_RATE * jnp.sin(latitude))[:, None]


def advance_wide(current, statics, rotation, cosine, sine_now):
    sea_mask, depth_field, retain = (statics[0], statics[1], statics[2])
    height, east_vel, north_vel = (current[0], current[1], current[2])
    spread = across_cols(depth_field * east_vel) + cropped(across_rows(depth_field * north_vel), 1)
    height_new = cropped(sea_mask, 1) * (cropped(height, 1) - FLUX_RATE * spread)
    surface = height_new + cropped(cosine * statics[3] + sine_now * statics[4], 1)
    mask_keep = cropped(sea_mask * retain, 2)
    east_mid = cropped(east_vel, 2)
    north_mid = cropped(north_vel, 2)
    east_new = mask_keep * (east_mid - PRESS_RATE * across_cols(surface) + rotation * north_mid)
    north_new = mask_keep * (
        north_mid - PRESS_RATE * cropped(across_rows(surface), 1) - rotation * east_mid
    )
    return jnp.stack([cropped(height_new, 1), east_new, north_new])


def adjoint_step(adjoint, statics, rotation):
    sea_mask, depth_field, retain = (statics[0], statics[1], statics[2])
    mask_keep = sea_mask * retain
    east_part = mask_keep * adjoint[1]
    north_part = mask_keep * adjoint[2]
    summed = cropped(adjoint[0], 1) + PRESS_RATE * (
        across_cols(east_part) + cropped(across_rows(north_part), 1)
    )
    height_part = cropped(sea_mask, 1) * summed
    depth_flux = FLUX_RATE * cropped(depth_field, 2)
    east_in = (
        cropped(east_part, 2)
        - rotation * cropped(north_part, 2)
        + depth_flux * across_cols(height_part)
    )
    north_in = (
        cropped(north_part, 2)
        + rotation * cropped(east_part, 2)
        + depth_flux * cropped(across_rows(height_part), 1)
    )
    return (jnp.stack([cropped(height_part, 1), east_in, north_in]), east_part, north_part)


def local(start_states, ocean_mask, depth_class, class_depth, drag_rate, tide_cos, tide_sin):
    per_rim = 1
    rim_width = 2 * per_rim
    slice_count = lax.axis_size("tm")
    slice_index = lax.axis_index("tm")
    sea_mask = ocean_mask.astype(jnp.float32)
    classes = jnp.arange(class_depth.shape[0], dtype=jnp.int32)
    depth_field = jnp.sum(
        jnp.where(depth_class[None] == classes[:, None, None], class_depth[:, None, None], 0.0),
        axis=0,
    )
    retain = 1.0 / (1.0 + drag_rate)
    statics = with_halo(
        jnp.stack([sea_mask, depth_field, retain, tide_cos, tide_sin]), (("cell", 2),), rim_width
    )
    rotation = coriolis(sea_mask.shape[0])
    initial = start_states[0]
    current = initial * sea_mask
    phase_unit = 2.0 * math.pi / (slice_count * STEPS)
    stored = []
    for first_step in range(0, STEPS, per_rim):
        widened = with_halo(current, (("cell", 2),), rim_width)
        inner_step = 0
        phase_now = (slice_index * STEPS + first_step + inner_step).astype(jnp.float32) * phase_unit
        widened = advance_wide(
            widened,
            cropped(statics, 2 * inner_step),
            rotation,
            jnp.cos(phase_now),
            jnp.sin(phase_now),
        )
        stored.append(cropped(widened[1:], rim_width - 2 * inner_step - 2))
        current = widened
    arrived = from_behind(current, "tm", 1)
    behind = sea_mask * (arrived - initial)
    defect = from_behind(behind, "tm", -1)
    adjoint = defect
    drag_total = jnp.zeros_like(drag_rate)
    for first_step in range(STEPS - per_rim, -1, -per_rim):
        widened = with_halo(adjoint, (("cell", 2),), rim_width)
        inner_step = 0
        step_number = first_step + per_rim - 1 - inner_step
        margin = rim_width - 2 * inner_step
        widened, east_part, north_part = adjoint_step(
            widened, cropped(statics, 2 * inner_step), rotation
        )
        outputs = stored[step_number]
        drag_total = drag_total - (
            cropped(east_part, margin) * outputs[0] + cropped(north_part, margin) * outputs[1]
        )
        adjoint = widened
    state_grad = sea_mask * adjoint - behind
    summed_rows = lax.psum_scatter(drag_total, "tm", scatter_dimension=0, tiled=True)
    drag_grad = summed_rows / slice_count
    return (defect[None], state_grad[None], drag_grad)


def solution(mesh):
    return jax.shard_map(
        local,
        mesh=mesh,
        in_specs=(
            P("tm", None, None, "cell"),
            P(None, "cell"),
            P(None, "cell"),
            P(),
            P(None, "cell"),
            P(None, "cell"),
            P(None, "cell"),
        ),
        out_specs=(P("tm", None, None, "cell"), P("tm", None, None, "cell"), P("tm", "cell")),
        check_vma=False,
    )
```

profile of v0, /device:TPU:1, one launch (start us, length us, event | category | flops | bytes accessed | tf_op | source)
XLA Modules:
  0.0 551.2 jit_solution(4551584671012178818)
XLA Ops:
  10.9 3.9 collective-permute-start
  14.9 10.4 %collective-permute-start.1 = (f32[5,128,2]{2,1,0:T(8,128)S(1)}, f32[5,128,2]{2,1,0:T(8,128)S(1)}, u32[]{:S(2)}, u32[]{:S(2)}) collective-permute-start(f32[5,128,2]{2,1,0:T(8,128)S(1)} %get-tuple-element.119), channel_id=1, source_target_pairs={{1,0},{2,1},{3,2},{4,3},{5,4},{6,5},{7,6},{8,7},{9,8},{10,9},{11,1... | collective-permute-start | bytes 15368 | tf_op jit(solution)/shard_map/ppermute | solution.py:25
  25.5 1.9 collective-permute-start.2
  27.4 5.5 collective-permute-start.3
  35.8 4.7 collective-permute-done.3
  42.1 1.9 collective-permute-start.4
  44.0 8.8 %collective-permute-start.5 = (f32[3,128,2]{2,1,0:T(8,128)S(1)}, f32[3,128,2]{2,1,0:T(8,128)S(1)}, u32[]{:S(2)}, u32[]{:S(2)}) collective-permute-start(f32[3,128,2]{2,1,0:T(8,128)S(1)} %get-tuple-element.149), channel_id=1, source_target_pairs={{1,0},{2,1},{3,2},{4,3},{5,4},{6,5},{7,6},{8,7},{9,8},{10,9},{11,1... | collective-permute-start | bytes 9224 | tf_op jit(solution)/shard_map/ppermute | solution.py:25
  56.4 1.9 collective-permute-start.6
  58.3 9.3 %collective-permute-start.7 = (f32[3,128,2]{2,1,0:T(8,128)S(1)}, f32[3,128,2]{2,1,0:T(8,128)S(1)}, u32[]{:S(2)}, u32[]{:S(2)}) collective-permute-start(f32[3,128,2]{2,1,0:T(8,128)S(1)} %get-tuple-element.147), channel_id=1, source_target_pairs={{1,0},{2,1},{3,2},{4,3},{5,4},{6,5},{7,6},{8,7},{9,8},{10,9},{11,1... | collective-permute-start | bytes 9224 | tf_op jit(solution)/shard_map/ppermute | solution.py:25
  67.7 2.9 collective-permute-done.6
  72.5 1.9 collective-permute-start.8
  74.4 8.1 %collective-permute-start.9 = (f32[3,128,2]{2,1,0:T(8,128)S(1)}, f32[3,128,2]{2,1,0:T(8,128)S(1)}, u32[]{:S(2)}, u32[]{:S(2)}) collective-permute-start(f32[3,128,2]{2,1,0:T(8,128)S(1)} %get-tuple-element.145), channel_id=1, source_target_pairs={{1,0},{2,1},{3,2},{4,3},{5,4},{6,5},{7,6},{8,7},{9,8},{10,9},{11,1... | collective-permute-start | bytes 9224 | tf_op jit(solution)/shard_map/ppermute | solution.py:25
  82.5 2.9 collective-permute-done.8
  87.4 1.9 collective-permute-start.10
  89.3 8.1 %collective-permute-start.11 = (f32[3,128,2]{2,1,0:T(8,128)S(1)}, f32[3,128,2]{2,1,0:T(8,128)S(1)}, u32[]{:S(2)}, u32[]{:S(2)}) collective-permute-start(f32[3,128,2]{2,1,0:T(8,128)S(1)} %get-tuple-element.143), channel_id=1, source_target_pairs={{1,0},{2,1},{3,2},{4,3},{5,4},{6,5},{7,6},{8,7},{9,8},{10,9},{11,1... | collective-permute-start | bytes 9224 | tf_op jit(solution)/shard_map/ppermute | solution.py:25
  97.4 2.9 collective-permute-done.10
  102.3 1.9 collective-permute-start.12
  104.2 8.1 %collective-permute-start.13 = (f32[3,128,2]{2,1,0:T(8,128)S(1)}, f32[3,128,2]{2,1,0:T(8,128)S(1)}, u32[]{:S(2)}, u32[]{:S(2)}) collective-permute-start(f32[3,128,2]{2,1,0:T(8,128)S(1)} %get-tuple-element.141), channel_id=1, source_target_pairs={{1,0},{2,1},{3,2},{4,3},{5,4},{6,5},{7,6},{8,7},{9,8},{10,9},{11,1... | collective-permute-start | bytes 9224 | tf_op jit(solution)/shard_map/ppermute | solution.py:25
  112.3 2.9 collective-permute-done.12
  117.2 1.9 collective-permute-start.14
  119.1 8.1 %collective-permute-start.15 = (f32[3,128,2]{2,1,0:T(8,128)S(1)}, f32[3,128,2]{2,1,0:T(8,128)S(1)}, u32[]{:S(2)}, u32[]{:S(2)}) collective-permute-start(f32[3,128,2]{2,1,0:T(8,128)S(1)} %get-tuple-element.139), channel_id=1, source_target_pairs={{1,0},{2,1},{3,2},{4,3},{5,4},{6,5},{7,6},{8,7},{9,8},{10,9},{11,1... | collective-permute-start | bytes 9224 | tf_op jit(solution)/shard_map/ppermute | solution.py:25
  127.2 2.9 collective-permute-done.14
  132.1 1.9 collective-permute-start.16
  134.0 8.1 %collective-permute-start.17 = (f32[3,128,2]{2,1,0:T(8,128)S(1)}, f32[3,128,2]{2,1,0:T(8,128)S(1)}, u32[]{:S(2)}, u32[]{:S(2)}) collective-permute-start(f32[3,128,2]{2,1,0:T(8,128)S(1)} %get-tuple-element.137), channel_id=1, source_target_pairs={{1,0},{2,1},{3,2},{4,3},{5,4},{6,5},{7,6},{8,7},{9,8},{10,9},{11,1... | collective-permute-start | bytes 9224 | tf_op jit(solution)/shard_map/ppermute | solution.py:25
  142.1 2.9 collective-permute-done.16
  147.4 4.7 collective-permute-start.18
  152.2 2.6 collective-permute-done.18
  154.8 6.8 %collective-permute-start.19 = (f32[3,128,128]{2,1,0:T(8,128)S(1)}, f32[3,128,128]{2,1,0:T(8,128)S(1)}, u32[]{:S(2)}, u32[]{:S(2)}) collective-permute-start(f32[3,128,128]{2,1,0:T(8,128)S(1)} %fusion.2), channel_id=1, source_target_pairs={{0,496},{16,0},{32,16},{48,32},{64,48},{80,64},{96,80},{112,96},{1... | collective-permute-start | bytes 589832 | tf_op jit(solution)/shard_map/ppermute | solution.py:33
  162.8 1.9 collective-permute-start.20
  164.7 7.0 %collective-permute-start.21 = (f32[3,128,2]{2,1,0:T(8,128)S(1)}, f32[3,128,2]{2,1,0:T(8,128)S(1)}, u32[]{:S(2)}, u32[]{:S(2)}) collective-permute-start(f32[3,128,2]{2,1,0:T(8,128)S(1)} %get-tuple-element.135), channel_id=1, source_target_pairs={{1,0},{2,1},{3,2},{4,3},{5,4},{6,5},{7,6},{8,7},{9,8},{10,9},{11,1... | collective-permute-start | bytes 9224 | tf_op jit(solution)/shard_map/ppermute | solution.py:25
  172.9 3.0 collective-permute-done.21
  176.9 1.9 collective-permute-start.22
  178.8 7.4 %collective-permute-start.23 = (f32[3,128,2]{2,1,0:T(8,128)S(1)}, f32[3,128,2]{2,1,0:T(8,128)S(1)}, u32[]{:S(2)}, u32[]{:S(2)}) collective-permute-start(f32[3,128,2]{2,1,0:T(8,128)S(1)} %get-tuple-element.133), channel_id=1, source_target_pairs={{1,0},{2,1},{3,2},{4,3},{5,4},{6,5},{7,6},{8,7},{9,8},{10,9},{11,1... | collective-permute-start | bytes 9224 | tf_op jit(solution)/shard_map/ppermute | solution.py:25
  186.2 2.3 collective-permute-done.22
  191.2 1.9 collective-permute-start.24
  193.1 8.9 %collective-permute-start.25 = (f32[3,128,2]{2,1,0:T(8,128)S(1)}, f32[3,128,2]{2,1,0:T(8,128)S(1)}, u32[]{:S(2)}, u32[]{:S(2)}) collective-permute-start(f32[3,128,2]{2,1,0:T(8,128)S(1)} %get-tuple-element.131), channel_id=1, source_target_pairs={{1,0},{2,1},{3,2},{4,3},{5,4},{6,5},{7,6},{8,7},{9,8},{10,9},{11,1... | collective-permute-start | bytes 9224 | tf_op jit(solution)/shard_map/ppermute | solution.py:25
  202.0 2.7 collective-permute-done.24
  207.5 1.9 collective-permute-start.26
  209.4 8.1 %collective-permute-start.27 = (f32[3,128,2]{2,1,0:T(8,128)S(1)}, f32[3,128,2]{2,1,0:T(8,128)S(1)}, u32[]{:S(2)}, u32[]{:S(2)}) collective-permute-start(f32[3,128,2]{2,1,0:T(8,128)S(1)} %get-tuple-element.129), channel_id=1, source_target_pairs={{1,0},{2,1},{3,2},{4,3},{5,4},{6,5},{7,6},{8,7},{9,8},{10,9},{11,1... | collective-permute-start | bytes 9224 | tf_op jit(solution)/shard_map/ppermute | solution.py:25
  217.5 2.9 collective-permute-done.26
  225.1 8.1 %collective-permute-start.29 = (f32[3,128,2]{2,1,0:T(8,128)S(1)}, f32[3,128,2]{2,1,0:T(8,128)S(1)}, u32[]{:S(2)}, u32[]{:S(2)}) collective-permute-start(f32[3,128,2]{2,1,0:T(8,128)S(1)} %get-tuple-element.127), channel_id=1, source_target_pairs={{1,0},{2,1},{3,2},{4,3},{5,4},{6,5},{7,6},{8,7},{9,8},{10,9},{11,1... | collective-permute-start | bytes 9224 | tf_op jit(solution)/shard_map/ppermute | solution.py:25
  233.2 2.9 collective-permute-done.28
  240.7 8.1 %collective-permute-start.31 = (f32[3,128,2]{2,1,0:T(8,128)S(1)}, f32[3,128,2]{2,1,0:T(8,128)S(1)}, u32[]{:S(2)}, u32[]{:S(2)}) collective-permute-start(f32[3,128,2]{2,1,0:T(8,128)S(1)} %get-tuple-element.125), channel_id=1, source_target_pairs={{1,0},{2,1},{3,2},{4,3},{5,4},{6,5},{7,6},{8,7},{9,8},{10,9},{11,1... | collective-permute-start | bytes 9224 | tf_op jit(solution)/shard_map/ppermute | solution.py:25
  248.8 2.9 collective-permute-done.30
  256.5 8.5 %collective-permute-start.33 = (f32[3,128,2]{2,1,0:T(8,128)S(1)}, f32[3,128,2]{2,1,0:T(8,128)S(1)}, u32[]{:S(2)}, u32[]{:S(2)}) collective-permute-start(f32[3,128,2]{2,1,0:T(8,128)S(1)} %get-tuple-element.123), channel_id=1, source_target_pairs={{1,0},{2,1},{3,2},{4,3},{5,4},{6,5},{7,6},{8,7},{9,8},{10,9},{11,1... | collective-permute-start | bytes 9224 | tf_op jit(solution)/shard_map/ppermute | solution.py:25
  265.1 2.9 collective-permute-done.32
  274.0 8.2 %collective-permute-start.35 = (f32[3,128,2]{2,1,0:T(8,128)}, f32[3,128,2]{2,1,0:T(8,128)}, u32[]{:S(2)}, u32[]{:S(2)}) collective-permute-start(f32[3,128,2]{2,1,0:T(8,128)} %get-tuple-element.121), channel_id=1, source_target_pairs={{1,0},{2,1},{3,2},{4,3},{5,4},{6,5},{7,6},{8,7},{9,8},{10,9},{11,1... | collective-permute-start | bytes 9224 | tf_op jit(solution)/shard_map/ppermute | solution.py:25
  294.7 247.7 %all-reduce.67.cloned.1.call-done = f32[128,128]{1,0:T(8,128)} async-done(((f32[128,128]{1,0:T(8,128)}), f32[128,128]{1,0:T(8,128)}) %all-reduce.67.cloned.1.call-update) | async-done | bytes 65552
  (227 shorter events, 64.3 us)
Async XLA Ops:
  7.2 0.9 copy-start.14
  7.2 0.9 copy-start.10
  7.2 535.2 %all-reduce.67.cloned.1.call-start = ((), (), s32[]{:S(2)}) async-start(), calls=%async_computation | async-start | bytes 131072
  8.2 0.8 copy-start.11
  9.1 0.8 copy-start.12
  10.7 14.5 %copy-start.9 = (s32[128,128]{1,0:T(8,128)S(1)}, s32[128,128]{1,0:T(8,128)}, u32[]{:S(2)}) copy-start(s32[128,128]{1,0:T(8,128)} %param.8) | copy-start | bytes 196612
  10.7 14.6 %copy-start.2 = (f32[1,3,128,128]{3,2,1,0:T(8,128)S(1)}, f32[1,3,128,128]{3,2,1,0:T(8,128)}, u32[]{:S(2)}) copy-start(f32[1,3,128,128]{3,2,1,0:T(8,128)} %param.7) | copy-start | bytes 589828
  10.9 29.8 %collective-permute-start = (f32[5,128,2]{2,1,0:T(8,128)S(1)}, f32[5,128,2]{2,1,0:T(8,128)S(1)}, u32[]{:S(2)}, u32[]{:S(2)}) collective-permute-start(f32[5,128,2]{2,1,0:T(8,128)S(1)} %get-tuple-element.118), channel_id=1, source_target_pairs={{0,1},{1,2},{2,3},{3,4},{4,5},{5,6},{6,7},{7,8},{8,9},{9,10},{10,1... | collective-permute-start | bytes 15368 | tf_op jit(solution)/shard_map/ppermute | solution.py:22
  14.9 25.9 %collective-permute-start.1 = (f32[5,128,2]{2,1,0:T(8,128)S(1)}, f32[5,128,2]{2,1,0:T(8,128)S(1)}, u32[]{:S(2)}, u32[]{:S(2)}) collective-permute-start(f32[5,128,2]{2,1,0:T(8,128)S(1)} %get-tuple-element.119), channel_id=1, source_target_pairs={{1,0},{2,1},{3,2},{4,3},{5,4},{6,5},{7,6},{8,7},{9,8},{10,9},{11,1... | collective-permute-start | bytes 15368 | tf_op jit(solution)/shard_map/ppermute | solution.py:25
  25.5 10.3 %collective-permute-start.2 = (f32[3,128,2]{2,1,0:T(8,128)S(1)}, f32[3,128,2]{2,1,0:T(8,128)S(1)}, u32[]{:S(2)}, u32[]{:S(2)}) collective-permute-start(f32[3,128,2]{2,1,0:T(8,128)S(1)} %get-tuple-element.150), channel_id=1, source_target_pairs={{0,1},{1,2},{2,3},{3,4},{4,5},{5,6},{6,7},{7,8},{8,9},{9,10},{10,1... | collective-permute-start | bytes 9224 | tf_op jit(solution)/shard_map/ppermute | solution.py:22
  27.4 13.1 %collective-permute-start.3 = (f32[3,128,2]{2,1,0:T(8,128)S(1)}, f32[3,128,2]{2,1,0:T(8,128)S(1)}, u32[]{:S(2)}, u32[]{:S(2)}) collective-permute-start(f32[3,128,2]{2,1,0:T(8,128)S(1)} %get-tuple-element.151), channel_id=1, source_target_pairs={{1,0},{2,1},{3,2},{4,3},{5,4},{6,5},{7,6},{8,7},{9,8},{10,9},{11,1... | collective-permute-start | bytes 9224 | tf_op jit(solution)/shard_map/ppermute | solution.py:25
  41.2 135.3 %copy-start = (f32[128,132]{1,0:T(8,128)}, f32[128,132]{1,0:T(8,128)S(1)}, u32[]{:S(2)}) copy-start(f32[128,132]{1,0:T(8,128)S(1)} %get-tuple-element.35) | copy-start | bytes 202756
  42.1 12.4 %collective-permute-start.4 = (f32[3,128,2]{2,1,0:T(8,128)S(1)}, f32[3,128,2]{2,1,0:T(8,128)S(1)}, u32[]{:S(2)}, u32[]{:S(2)}) collective-permute-start(f32[3,128,2]{2,1,0:T(8,128)S(1)} %get-tuple-element.148), channel_id=1, source_target_pairs={{0,1},{1,2},{2,3},{3,4},{4,5},{5,6},{6,7},{7,8},{8,9},{9,10},{10,1... | collective-permute-start | bytes 9224 | tf_op jit(solution)/shard_map/ppermute | solution.py:22
  44.0 11.4 %collective-permute-start.5 = (f32[3,128,2]{2,1,0:T(8,128)S(1)}, f32[3,128,2]{2,1,0:T(8,128)S(1)}, u32[]{:S(2)}, u32[]{:S(2)}) collective-permute-start(f32[3,128,2]{2,1,0:T(8,128)S(1)} %get-tuple-element.149), channel_id=1, source_target_pairs={{1,0},{2,1},{3,2},{4,3},{5,4},{6,5},{7,6},{8,7},{9,8},{10,9},{11,1... | collective-permute-start | bytes 9224 | tf_op jit(solution)/shard_map/ppermute | solution.py:25
  56.4 14.2 %collective-permute-start.6 = (f32[3,128,2]{2,1,0:T(8,128)S(1)}, f32[3,128,2]{2,1,0:T(8,128)S(1)}, u32[]{:S(2)}, u32[]{:S(2)}) collective-permute-start(f32[3,128,2]{2,1,0:T(8,128)S(1)} %get-tuple-element.146), channel_id=1, source_target_pairs={{0,1},{1,2},{2,3},{3,4},{4,5},{5,6},{6,7},{7,8},{8,9},{9,10},{10,1... | collective-permute-start | bytes 9224 | tf_op jit(solution)/shard_map/ppermute | solution.py:22
  58.3 13.1 %collective-permute-start.7 = (f32[3,128,2]{2,1,0:T(8,128)S(1)}, f32[3,128,2]{2,1,0:T(8,128)S(1)}, u32[]{:S(2)}, u32[]{:S(2)}) collective-permute-start(f32[3,128,2]{2,1,0:T(8,128)S(1)} %get-tuple-element.147), channel_id=1, source_target_pairs={{1,0},{2,1},{3,2},{4,3},{5,4},{6,5},{7,6},{8,7},{9,8},{10,9},{11,1... | collective-permute-start | bytes 9224 | tf_op jit(solution)/shard_map/ppermute | solution.py:25
  72.5 13.0 %collective-permute-start.8 = (f32[3,128,2]{2,1,0:T(8,128)S(1)}, f32[3,128,2]{2,1,0:T(8,128)S(1)}, u32[]{:S(2)}, u32[]{:S(2)}) collective-permute-start(f32[3,128,2]{2,1,0:T(8,128)S(1)} %get-tuple-element.144), channel_id=1, source_target_pairs={{0,1},{1,2},{2,3},{3,4},{4,5},{5,6},{6,7},{7,8},{8,9},{9,10},{10,1... | collective-permute-start | bytes 9224 | tf_op jit(solution)/shard_map/ppermute | solution.py:22
  74.4 11.9 %collective-permute-start.9 = (f32[3,128,2]{2,1,0:T(8,128)S(1)}, f32[3,128,2]{2,1,0:T(8,128)S(1)}, u32[]{:S(2)}, u32[]{:S(2)}) collective-permute-start(f32[3,128,2]{2,1,0:T(8,128)S(1)} %get-tuple-element.145), channel_id=1, source_target_pairs={{1,0},{2,1},{3,2},{4,3},{5,4},{6,5},{7,6},{8,7},{9,8},{10,9},{11,1... | collective-permute-start | bytes 9224 | tf_op jit(solution)/shard_map/ppermute | solution.py:25
  87.4 13.0 %collective-permute-start.10 = (f32[3,128,2]{2,1,0:T(8,128)S(1)}, f32[3,128,2]{2,1,0:T(8,128)S(1)}, u32[]{:S(2)}, u32[]{:S(2)}) collective-permute-start(f32[3,128,2]{2,1,0:T(8,128)S(1)} %get-tuple-element.142), channel_id=1, source_target_pairs={{0,1},{1,2},{2,3},{3,4},{4,5},{5,6},{6,7},{7,8},{8,9},{9,10},{10,1... | collective-permute-start | bytes 9224 | tf_op jit(solution)/shard_map/ppermute | solution.py:22
  89.3 11.9 %collective-permute-start.11 = (f32[3,128,2]{2,1,0:T(8,128)S(1)}, f32[3,128,2]{2,1,0:T(8,128)S(1)}, u32[]{:S(2)}, u32[]{:S(2)}) collective-permute-start(f32[3,128,2]{2,1,0:T(8,128)S(1)} %get-tuple-element.143), channel_id=1, source_target_pairs={{1,0},{2,1},{3,2},{4,3},{5,4},{6,5},{7,6},{8,7},{9,8},{10,9},{11,1... | collective-permute-start | bytes 9224 | tf_op jit(solution)/shard_map/ppermute | solution.py:25
  102.3 13.0 %collective-permute-start.12 = (f32[3,128,2]{2,1,0:T(8,128)S(1)}, f32[3,128,2]{2,1,0:T(8,128)S(1)}, u32[]{:S(2)}, u32[]{:S(2)}) collective-permute-start(f32[3,128,2]{2,1,0:T(8,128)S(1)} %get-tuple-element.140), channel_id=1, source_target_pairs={{0,1},{1,2},{2,3},{3,4},{4,5},{5,6},{6,7},{7,8},{8,9},{9,10},{10,1... | collective-permute-start | bytes 9224 | tf_op jit(solution)/shard_map/ppermute | solution.py:22
  104.2 11.9 %collective-permute-start.13 = (f32[3,128,2]{2,1,0:T(8,128)S(1)}, f32[3,128,2]{2,1,0:T(8,128)S(1)}, u32[]{:S(2)}, u32[]{:S(2)}) collective-permute-start(f32[3,128,2]{2,1,0:T(8,128)S(1)} %get-tuple-element.141), channel_id=1, source_target_pairs={{1,0},{2,1},{3,2},{4,3},{5,4},{6,5},{7,6},{8,7},{9,8},{10,9},{11,1... | collective-permute-start | bytes 9224 | tf_op jit(solution)/shard_map/ppermute | solution.py:25
  117.2 13.0 %collective-permute-start.14 = (f32[3,128,2]{2,1,0:T(8,128)S(1)}, f32[3,128,2]{2,1,0:T(8,128)S(1)}, u32[]{:S(2)}, u32[]{:S(2)}) collective-permute-start(f32[3,128,2]{2,1,0:T(8,128)S(1)} %get-tuple-element.138), channel_id=1, source_target_pairs={{0,1},{1,2},{2,3},{3,4},{4,5},{5,6},{6,7},{7,8},{8,9},{9,10},{10,1... | collective-permute-start | bytes 9224 | tf_op jit(solution)/shard_map/ppermute | solution.py:22
  119.1 11.9 %collective-permute-start.15 = (f32[3,128,2]{2,1,0:T(8,128)S(1)}, f32[3,128,2]{2,1,0:T(8,128)S(1)}, u32[]{:S(2)}, u32[]{:S(2)}) collective-permute-start(f32[3,128,2]{2,1,0:T(8,128)S(1)} %get-tuple-element.139), channel_id=1, source_target_pairs={{1,0},{2,1},{3,2},{4,3},{5,4},{6,5},{7,6},{8,7},{9,8},{10,9},{11,1... | collective-permute-start | bytes 9224 | tf_op jit(solution)/shard_map/ppermute | solution.py:25
  132.1 13.0 %collective-permute-start.16 = (f32[3,128,2]{2,1,0:T(8,128)S(1)}, f32[3,128,2]{2,1,0:T(8,128)S(1)}, u32[]{:S(2)}, u32[]{:S(2)}) collective-permute-start(f32[3,128,2]{2,1,0:T(8,128)S(1)} %get-tuple-element.136), channel_id=1, source_target_pairs={{0,1},{1,2},{2,3},{3,4},{4,5},{5,6},{6,7},{7,8},{8,9},{9,10},{10,1... | collective-permute-start | bytes 9224 | tf_op jit(solution)/shard_map/ppermute | solution.py:22
  134.0 11.9 %collective-permute-start.17 = (f32[3,128,2]{2,1,0:T(8,128)S(1)}, f32[3,128,2]{2,1,0:T(8,128)S(1)}, u32[]{:S(2)}, u32[]{:S(2)}) collective-permute-start(f32[3,128,2]{2,1,0:T(8,128)S(1)} %get-tuple-element.137), channel_id=1, source_target_pairs={{1,0},{2,1},{3,2},{4,3},{5,4},{6,5},{7,6},{8,7},{9,8},{10,9},{11,1... | collective-permute-start | bytes 9224 | tf_op jit(solution)/shard_map/ppermute | solution.py:25
  147.4 7.3 %collective-permute-start.18 = (f32[3,128,128]{2,1,0:T(8,128)S(1)}, f32[3,128,128]{2,1,0:T(8,128)S(1)}, u32[]{:S(2)}, u32[]{:S(2)}) collective-permute-start(f32[3,128,128]{2,1,0:T(8,128)S(1)} %pad_maximum_fusion.24), channel_id=1, source_target_pairs={{0,16},{16,32},{32,48},{48,64},{64,80},{80,96},{96,112},{112,128},... | collective-permute-start | bytes 589832 | tf_op jit(solution)/shard_map/ppermute | solution.py:33
  154.8 8.0 %copy-start.3 = (f32[3,128,128]{2,1,0:T(8,128)}, f32[3,128,128]{2,1,0:T(8,128)S(1)}, u32[]{:S(2)}) copy-start(f32[3,128,128]{2,1,0:T(8,128)S(1)} %fusion.2) | copy-start | bytes 589828
  154.8 7.9 %collective-permute-start.19 = (f32[3,128,128]{2,1,0:T(8,128)S(1)}, f32[3,128,128]{2,1,0:T(8,128)S(1)}, u32[]{:S(2)}, u32[]{:S(2)}) collective-permute-start(f32[3,128,128]{2,1,0:T(8,128)S(1)} %fusion.2), channel_id=1, source_target_pairs={{0,496},{16,0},{32,16},{48,32},{64,48},{80,64},{96,80},{112,96},{1... | collective-permute-start | bytes 589832 | tf_op jit(solution)/shard_map/ppermute | solution.py:33
  162.8 10.1 %collective-permute-start.20 = (f32[3,128,2]{2,1,0:T(8,128)S(1)}, f32[3,128,2]{2,1,0:T(8,128)S(1)}, u32[]{:S(2)}, u32[]{:S(2)}) collective-permute-start(f32[3,128,2]{2,1,0:T(8,128)S(1)} %get-tuple-element.134), channel_id=1, source_target_pairs={{0,1},{1,2},{2,3},{3,4},{4,5},{5,6},{6,7},{7,8},{8,9},{9,10},{10,1... | collective-permute-start | bytes 9224 | tf_op jit(solution)/shard_map/ppermute | solution.py:22
  164.7 11.2 %collective-permute-start.21 = (f32[3,128,2]{2,1,0:T(8,128)S(1)}, f32[3,128,2]{2,1,0:T(8,128)S(1)}, u32[]{:S(2)}, u32[]{:S(2)}) collective-permute-start(f32[3,128,2]{2,1,0:T(8,128)S(1)} %get-tuple-element.135), channel_id=1, source_target_pairs={{1,0},{2,1},{3,2},{4,3},{5,4},{6,5},{7,6},{8,7},{9,8},{10,9},{11,1... | collective-permute-start | bytes 9224 | tf_op jit(solution)/shard_map/ppermute | solution.py:25
  176.9 11.5 %collective-permute-start.22 = (f32[3,128,2]{2,1,0:T(8,128)S(1)}, f32[3,128,2]{2,1,0:T(8,128)S(1)}, u32[]{:S(2)}, u32[]{:S(2)}) collective-permute-start(f32[3,128,2]{2,1,0:T(8,128)S(1)} %get-tuple-element.132), channel_id=1, source_target_pairs={{0,1},{1,2},{2,3},{3,4},{4,5},{5,6},{6,7},{7,8},{8,9},{9,10},{10,1... | collective-permute-start | bytes 9224 | tf_op jit(solution)/shard_map/ppermute | solution.py:22
  178.8 10.5 %collective-permute-start.23 = (f32[3,128,2]{2,1,0:T(8,128)S(1)}, f32[3,128,2]{2,1,0:T(8,128)S(1)}, u32[]{:S(2)}, u32[]{:S(2)}) collective-permute-start(f32[3,128,2]{2,1,0:T(8,128)S(1)} %get-tuple-element.133), channel_id=1, source_target_pairs={{1,0},{2,1},{3,2},{4,3},{5,4},{6,5},{7,6},{8,7},{9,8},{10,9},{11,1... | collective-permute-start | bytes 9224 | tf_op jit(solution)/shard_map/ppermute | solution.py:25
  191.2 13.6 %collective-permute-start.24 = (f32[3,128,2]{2,1,0:T(8,128)S(1)}, f32[3,128,2]{2,1,0:T(8,128)S(1)}, u32[]{:S(2)}, u32[]{:S(2)}) collective-permute-start(f32[3,128,2]{2,1,0:T(8,128)S(1)} %get-tuple-element.130), channel_id=1, source_target_pairs={{0,1},{1,2},{2,3},{3,4},{4,5},{5,6},{6,7},{7,8},{8,9},{9,10},{10,1... | collective-permute-start | bytes 9224 | tf_op jit(solution)/shard_map/ppermute | solution.py:22
  193.1 12.5 %collective-permute-start.25 = (f32[3,128,2]{2,1,0:T(8,128)S(1)}, f32[3,128,2]{2,1,0:T(8,128)S(1)}, u32[]{:S(2)}, u32[]{:S(2)}) collective-permute-start(f32[3,128,2]{2,1,0:T(8,128)S(1)} %get-tuple-element.131), channel_id=1, source_target_pairs={{1,0},{2,1},{3,2},{4,3},{5,4},{6,5},{7,6},{8,7},{9,8},{10,9},{11,1... | collective-permute-start | bytes 9224 | tf_op jit(solution)/shard_map/ppermute | solution.py:25
  207.5 12.9 %collective-permute-start.26 = (f32[3,128,2]{2,1,0:T(8,128)S(1)}, f32[3,128,2]{2,1,0:T(8,128)S(1)}, u32[]{:S(2)}, u32[]{:S(2)}) collective-permute-start(f32[3,128,2]{2,1,0:T(8,128)S(1)} %get-tuple-element.128), channel_id=1, source_target_pairs={{0,1},{1,2},{2,3},{3,4},{4,5},{5,6},{6,7},{7,8},{8,9},{9,10},{10,1... | collective-permute-start | bytes 9224 | tf_op jit(solution)/shard_map/ppermute | solution.py:22
  209.4 11.9 %collective-permute-start.27 = (f32[3,128,2]{2,1,0:T(8,128)S(1)}, f32[3,128,2]{2,1,0:T(8,128)S(1)}, u32[]{:S(2)}, u32[]{:S(2)}) collective-permute-start(f32[3,128,2]{2,1,0:T(8,128)S(1)} %get-tuple-element.129), channel_id=1, source_target_pairs={{1,0},{2,1},{3,2},{4,3},{5,4},{6,5},{7,6},{8,7},{9,8},{10,9},{11,1... | collective-permute-start | bytes 9224 | tf_op jit(solution)/shard_map/ppermute | solution.py:25
  223.1 12.9 %collective-permute-start.28 = (f32[3,128,2]{2,1,0:T(8,128)S(1)}, f32[3,128,2]{2,1,0:T(8,128)S(1)}, u32[]{:S(2)}, u32[]{:S(2)}) collective-permute-start(f32[3,128,2]{2,1,0:T(8,128)S(1)} %get-tuple-element.126), channel_id=1, source_target_pairs={{0,1},{1,2},{2,3},{3,4},{4,5},{5,6},{6,7},{7,8},{8,9},{9,10},{10,1... | collective-permute-start | bytes 9224 | tf_op jit(solution)/shard_map/ppermute | solution.py:22
  225.1 11.9 %collective-permute-start.29 = (f32[3,128,2]{2,1,0:T(8,128)S(1)}, f32[3,128,2]{2,1,0:T(8,128)S(1)}, u32[]{:S(2)}, u32[]{:S(2)}) collective-permute-start(f32[3,128,2]{2,1,0:T(8,128)S(1)} %get-tuple-element.127), channel_id=1, source_target_pairs={{1,0},{2,1},{3,2},{4,3},{5,4},{6,5},{7,6},{8,7},{9,8},{10,9},{11,1... | collective-permute-start | bytes 9224 | tf_op jit(solution)/shard_map/ppermute | solution.py:25
  238.8 13.0 %collective-permute-start.30 = (f32[3,128,2]{2,1,0:T(8,128)S(1)}, f32[3,128,2]{2,1,0:T(8,128)S(1)}, u32[]{:S(2)}, u32[]{:S(2)}) collective-permute-start(f32[3,128,2]{2,1,0:T(8,128)S(1)} %get-tuple-element.124), channel_id=1, source_target_pairs={{0,1},{1,2},{2,3},{3,4},{4,5},{5,6},{6,7},{7,8},{8,9},{9,10},{10,1... | collective-permute-start | bytes 9224 | tf_op jit(solution)/shard_map/ppermute | solution.py:22
  240.7 12.0 %collective-permute-start.31 = (f32[3,128,2]{2,1,0:T(8,128)S(1)}, f32[3,128,2]{2,1,0:T(8,128)S(1)}, u32[]{:S(2)}, u32[]{:S(2)}) collective-permute-start(f32[3,128,2]{2,1,0:T(8,128)S(1)} %get-tuple-element.125), channel_id=1, source_target_pairs={{1,0},{2,1},{3,2},{4,3},{5,4},{6,5},{7,6},{8,7},{9,8},{10,9},{11,1... | collective-permute-start | bytes 9224 | tf_op jit(solution)/shard_map/ppermute | solution.py:25
  254.6 13.4 %collective-permute-start.32 = (f32[3,128,2]{2,1,0:T(8,128)S(1)}, f32[3,128,2]{2,1,0:T(8,128)S(1)}, u32[]{:S(2)}, u32[]{:S(2)}) collective-permute-start(f32[3,128,2]{2,1,0:T(8,128)S(1)} %get-tuple-element.122), channel_id=1, source_target_pairs={{0,1},{1,2},{2,3},{3,4},{4,5},{5,6},{6,7},{7,8},{8,9},{9,10},{10,1... | collective-permute-start | bytes 9224 | tf_op jit(solution)/shard_map/ppermute | solution.py:22
  256.5 13.0 %collective-permute-start.33 = (f32[3,128,2]{2,1,0:T(8,128)S(1)}, f32[3,128,2]{2,1,0:T(8,128)S(1)}, u32[]{:S(2)}, u32[]{:S(2)}) collective-permute-start(f32[3,128,2]{2,1,0:T(8,128)S(1)} %get-tuple-element.123), channel_id=1, source_target_pairs={{1,0},{2,1},{3,2},{4,3},{5,4},{6,5},{7,6},{8,7},{9,8},{10,9},{11,1... | collective-permute-start | bytes 9224 | tf_op jit(solution)/shard_map/ppermute | solution.py:25
  272.1 13.4 %collective-permute-start.34 = (f32[3,128,2]{2,1,0:T(8,128)}, f32[3,128,2]{2,1,0:T(8,128)}, u32[]{:S(2)}, u32[]{:S(2)}) collective-permute-start(f32[3,128,2]{2,1,0:T(8,128)} %get-tuple-element.120), channel_id=1, source_target_pairs={{0,1},{1,2},{2,3},{3,4},{4,5},{5,6},{6,7},{7,8},{8,9},{9,10},{10,1... | collective-permute-start | bytes 9224 | tf_op jit(solution)/shard_map/ppermute | solution.py:22
  274.0 13.1 %collective-permute-start.35 = (f32[3,128,2]{2,1,0:T(8,128)}, f32[3,128,2]{2,1,0:T(8,128)}, u32[]{:S(2)}, u32[]{:S(2)}) collective-permute-start(f32[3,128,2]{2,1,0:T(8,128)} %get-tuple-element.121), channel_id=1, source_target_pairs={{1,0},{2,1},{3,2},{4,3},{5,4},{6,5},{7,6},{8,7},{9,8},{10,9},{11,1... | collective-permute-start | bytes 9224 | tf_op jit(solution)/shard_map/ppermute | solution.py:25
  289.0 0.9 copy-start.8
  292.2 0.9 copy-start.1
  293.1 0.9 copy-start.4
  (4 other events, 2.9 us)
Sparse Core Ops, SparseCore 0:
  291.0 251.3 all-reduce.66
where the time goes:
time: 554 us; the launch traced here: 551 us
  waiting for transfers between devices  313 us (56%)
  starting transfers between devices  185 us (33%)
  other arithmetic  23.5 us (4%)
  between operations  17.4 us (3%)
  local copies, waits for them, and re-layouts  12.4 us (2%)
    unnamed x2, waiting for transfers between devices  248 us
    ppermute x17, starting transfers between devices, with_halo(): lax.ppermute(lax.slice_in_dim(block, 0, width, axis=dim), axis, backward)  139 us
    ppermute x17, waiting for transfers between devices, with_halo(): lax.ppermute(lax.slice_in_dim(block, block.shape[dim] - width, None, axis...  40.2 us
    ppermute x17, starting transfers between devices, with_halo(): lax.ppermute(lax.slice_in_dim(block, block.shape[dim] - width, None, axis...  34.7 us
    ppermute x17, waiting for transfers between devices, with_halo(): lax.ppermute(lax.slice_in_dim(block, 0, width, axis=dim), axis, backward)  21.5 us
    ppermute x2, starting transfers between devices, from_behind(): return lax.ppermute(value, axis, pairs)  11.5 us
  transfers between devices with their start and end apart: 37, of which 35 were waited for; matrix products, arithmetic and copies ran while one was open for 1% of the time, Pallas kernels for 0%

commit v1 on v0

--- a/solution.py
+++ b/solution.py
@@ -13,24 +13,19 @@
 ROTATION_RATE = 0.15
 
 
-def with_halo(block, sides, width):
-    for axis, dim in sides:
-        count = lax.axis_size(axis)
-        forward = [(i, i + 1) for i in range(count - 1)]
-        forward.append((count - 1, 0))
-        backward = [(target, source) for source, target in forward]
-        low = lax.ppermute(
-            lax.slice_in_dim(block, block.shape[dim] - width, None, axis=dim), axis, forward
-        )
-        high = lax.ppermute(lax.slice_in_dim(block, 0, width, axis=dim), axis, backward)
-        block = jnp.concatenate([low, block, high], axis=dim)
-    return block
+def ring_pairs(count, steps):
+    return [(source, (source + steps) % count) for source in range(count)]
+
+
+def with_halo(block, axis, width):
+    count = lax.axis_size(axis)
+    low = lax.ppermute(block[..., block.shape[-1] - width :], axis, ring_pairs(count, 1))
+    high = lax.ppermute(block[..., :width], axis, ring_pairs(count, -1))
+    return jnp.concatenate([low, block, high], axis=-1)
 
 
 def from_behind(value, axis, steps):
-    count = lax.axis_size(axis)
-    pairs = [(source, (source + steps) % count) for source in range(count)]
-    return lax.ppermute(value, axis, pairs)
+    return lax.ppermute(value, axis, ring_pairs(lax.axis_size(axis), steps))
 
 
 def cropped(values_in, cut_width):
@@ -94,9 +89,26 @@
     return (jnp.stack([cropped(height_part, 1), east_in, north_in]), east_part, north_part)
 
 
+def reduce_scatter_rows(value, axis):
+    count = lax.axis_size(axis)
+    bits = count.bit_length() - 1
+    me = lax.axis_index(axis)
+    rows = value.shape[0] // count
+    buf = value.reshape((2,) * bits + (rows, value.shape[1]))
+    for bit in range(bits):
+        at = bits - 1 - bit
+        mine = ((me >> bit) & 1) == 1
+        low = lax.index_in_dim(buf, 0, axis=at, keepdims=False)
+        high = lax.index_in_dim(buf, 1, axis=at, keepdims=False)
+        keep = jnp.where(mine, high, low)
+        send = jnp.where(mine, low, high)
+        pairs = [(source, source ^ (1 << bit)) for source in range(count)]
+        buf = keep + lax.ppermute(send, axis, pairs)
+    return buf
+
+
 def local(start_states, ocean_mask, depth_class, class_depth, drag_rate, tide_cos, tide_sin):
-    per_rim = 1
-    rim_width = 2 * per_rim
+    halo = 2 * STEPS
     slice_count = lax.axis_size("tm")
     slice_index = lax.axis_index("tm")
     sea_mask = ocean_mask.astype(jnp.float32)
@@ -106,48 +118,40 @@
         axis=0,
     )
     retain = 1.0 / (1.0 + drag_rate)
-    statics = with_halo(
-        jnp.stack([sea_mask, depth_field, retain, tide_cos, tide_sin]), (("cell", 2),), rim_width
+    initial = start_states[0]
+    following = from_behind(initial, "tm", -1)
+    wide = with_halo(
+        jnp.concatenate(
+            [initial, jnp.stack([sea_mask, depth_field, retain, tide_cos, tide_sin])], axis=0
+        ),
+        "cell",
+        halo,
     )
+    statics = wide[3:]
     rotation = coriolis(sea_mask.shape[0])
-    initial = start_states[0]
-    current = initial * sea_mask
+    current = wide[:3] * statics[0]
     phase_unit = 2.0 * math.pi / (slice_count * STEPS)
     stored = []
-    for first_step in range(0, STEPS, per_rim):
-        widened = with_halo(current, (("cell", 2),), rim_width)
-        inner_step = 0
-        phase_now = (slice_index * STEPS + first_step + inner_step).astype(jnp.float32) * phase_unit
-        widened = advance_wide(
-            widened,
-            cropped(statics, 2 * inner_step),
-            rotation,
-            jnp.cos(phase_now),
-            jnp.sin(phase_now),
+    for step_number in range(STEPS):
+        phase_now = (slice_index * STEPS + step_number).astype(jnp.float32) * phase_unit
+        current = advance_wide(
+            current, cropped(statics, 2 * step_number), rotation, jnp.cos(phase_now), jnp.sin(phase_now)
         )
-        stored.append(cropped(widened[1:], rim_width - 2 * inner_step - 2))
-        current = widened
-    arrived = from_behind(current, "tm", 1)
-    behind = sea_mask * (arrived - initial)
-    defect = from_behind(behind, "tm", -1)
-    adjoint = defect
+        stored.append(cropped(current[1:], halo - 2 * (step_number + 1)))
+    defect = sea_mask * (current - following)
+    behind = from_behind(defect, "tm", 1)
+    adjoint = with_halo(defect, "cell", halo)
     drag_total = jnp.zeros_like(drag_rate)
-    for first_step in range(STEPS - per_rim, -1, -per_rim):
-        widened = with_halo(adjoint, (("cell", 2),), rim_width)
-        inner_step = 0
-        step_number = first_step + per_rim - 1 - inner_step
-        margin = rim_width - 2 * inner_step
-        widened, east_part, north_part = adjoint_step(
-            widened, cropped(statics, 2 * inner_step), rotation
-        )
+    for back in range(STEPS):
+        step_number = STEPS - 1 - back
+        margin = halo - 2 * back
+        adjoint, east_part, north_part = adjoint_step(adjoint, cropped(statics, 2 * back), rotation)
         outputs = stored[step_number]
         drag_total = drag_total - (
             cropped(east_part, margin) * outputs[0] + cropped(north_part, margin) * outputs[1]
         )
-        adjoint = widened
     state_grad = sea_mask * adjoint - behind
-    summed_rows = lax.psum_scatter(drag_total, "tm", scatter_dimension=0, tiled=True)
-    drag_grad = summed_rows / slice_count
+    drag_grad = reduce_scatter_rows(drag_total, "tm") / slice_count
     return (defect[None], state_grad[None], drag_grad)
 
 

time: 554 us -> 115 us (0.21)
  the two profiles are of different devices: /device:TPU:1 before, /device:TPU:254 now
where the time goes in v1:
time: 115 us
  waiting for transfers between devices  42.7 us (37%)
  starting transfers between devices  33.5 us (29%)
  other arithmetic  22.5 us (20%)
  local copies, waits for them, and re-layouts  13.1 us (11%)
  between operations  2.79 us (2%)
    ppermute x5, waiting for transfers between devices, reduce_scatter_rows(): buf = keep + lax.ppermute(send, axis, pairs)  18.4 us
    ppermute x2, waiting for transfers between devices, with_halo(): lax.ppermute(block[..., block.shape[-1] - width:], axis, ring_pairs(count...  18.1 us
    ppermute x2, starting transfers between devices, with_halo(): lax.ppermute(block[..., block.shape[-1] - width:], axis, ring_pairs(count...  13.6 us
    ppermute x5, starting transfers between devices, reduce_scatter_rows(): buf = keep + lax.ppermute(send, axis, pairs)  11.5 us
    unnamed x59, local copies, waits for them, and re-layouts  11.3 us
    squeeze x8, other arithmetic, advance_wide(): sea_mask, depth_field, retain = (statics[0], statics[1], statics[2])  6.6 us
    ppermute x2, waiting for transfers between devices, with_halo(): high = lax.ppermute(block[..., :width], axis, ring_pairs(count, -1))  6.19 us
    ppermute x2, starting transfers between devices, from_behind(): return lax.ppermute(value, axis, ring_pairs(lax.axis_size(axis), steps))  4.52 us
  transfers between devices with their start and end apart: 11, of which 7 were waited for; matrix products, arithmetic and copies ran while one was open for 19% of the time, Pallas kernels for 0%

profile of v1, /device:TPU:254, one launch (start us, length us, event | category | flops | bytes accessed | tf_op | source)
XLA Modules:
  0.0 114.6 jit_solution(11195628452631316412)
XLA Ops:
  0.6 1.0 constant_dynamic-update-slice_fusion
  1.7 0.8 copy-done.23
  2.6 0.8 copy-done.24
  3.5 0.8 copy-done.25
  4.3 0.8 copy-done.26
  5.3 5.8 %collective-permute-start = (f32[8,128,16]{2,1,0:T(8,128)S(1)}, f32[8,128,16]{2,1,0:T(8,128)S(1)}, u32[]{:S(2)}, u32[]{:S(2)}) collective-permute-start(f32[8,128,16]{2,1,0:T(8,128)S(1)} %get-tuple-element.111), channel_id=1, source_target_pairs={{0,1},{1,2},{2,3},{3,4},{4,5},{5,6},{6,7},{7,8},{8,9},{9,10},{10,1... | collective-permute-start | bytes 196616 | tf_op jit(solution)/shard_map/ppermute | solution.py:22
  11.1 1.9 %collective-permute-start.1 = (f32[8,128,16]{2,1,0:T(8,128)S(1)}, f32[8,128,16]{2,1,0:T(8,128)S(1)}, u32[]{:S(2)}, u32[]{:S(2)}) collective-permute-start(f32[8,128,16]{2,1,0:T(8,128)S(1)} %get-tuple-element.112), channel_id=1, source_target_pairs={{0,15},{1,0},{2,1},{3,2},{4,3},{5,4},{6,5},{7,6},{8,7},{9,8},{10,9... | collective-permute-start | bytes 196616 | tf_op jit(solution)/shard_map/ppermute | solution.py:23
  13.0 2.4 %collective-permute-start.2 = (f32[3,128,128]{2,1,0:T(8,128)}, f32[3,128,128]{2,1,0:T(8,128)}, u32[]{:S(2)}, u32[]{:S(2)}) collective-permute-start(f32[3,128,128]{2,1,0:T(8,128)} %bitcast), channel_id=1, source_target_pairs={{0,496},{16,0},{32,16},{48,32},{64,48},{80,64},{96,80},{112,96},{1... | collective-permute-start | bytes 589832 | tf_op jit(solution)/shard_map/ppermute | solution.py:28
  16.8 17.5 %collective-permute-done = f32[8,128,16]{2,1,0:T(8,128)S(1)} collective-permute-done((f32[8,128,16]{2,1,0:T(8,128)S(1)}, f32[8,128,16]{2,1,0:T(8,128)S(1)}, u32[]{:S(2)}, u32[]{:S(2)}) %collective-permute-start) | collective-permute-done | bytes 65568 | tf_op jit(solution)/shard_map/ppermute | solution.py:22
  34.2 0.5 pad_maximum_fusion
  34.7 0.7 slice_bitcast_fusion.20
  36.3 0.9 slice_bitcast_fusion.17
  37.8 0.8 slice_bitcast_fusion.15
  39.0 0.4 fusion.307
  39.4 0.8 slice_bitcast_fusion.13
  41.0 0.8 slice_bitcast_fusion.11
  42.6 0.8 slice_bitcast_fusion.9
  44.2 0.8 slice_bitcast_fusion.7
  45.8 0.8 slice_bitcast_fusion.5
  47.2 1.0 fusion
  48.2 0.8 fusion.339
  49.0 7.9 %collective-permute-start.3 = (f32[3,128,16]{2,1,0:T(8,128)}, f32[3,128,16]{2,1,0:T(8,128)}, u32[]{:S(2)}, u32[]{:S(2)}) collective-permute-start(f32[3,128,16]{2,1,0:T(8,128)} %get-tuple-element.120), channel_id=1, source_target_pairs={{0,1},{1,2},{2,3},{3,4},{4,5},{5,6},{6,7},{7,8},{8,9},{9,10},{10,1... | collective-permute-start | bytes 73736 | tf_op jit(solution)/shard_map/ppermute | solution.py:22
  56.9 1.9 %collective-permute-start.4 = (f32[3,128,16]{2,1,0:T(8,128)}, f32[3,128,16]{2,1,0:T(8,128)}, u32[]{:S(2)}, u32[]{:S(2)}) collective-permute-start(f32[3,128,16]{2,1,0:T(8,128)} %get-tuple-element.121), channel_id=1, source_target_pairs={{0,15},{1,0},{2,1},{3,2},{4,3},{5,4},{6,5},{7,6},{8,7},{9,8},{10,9... | collective-permute-start | bytes 73736 | tf_op jit(solution)/shard_map/ppermute | solution.py:23
  58.8 2.1 %collective-permute-start.5 = (f32[3,128,128]{2,1,0:T(8,128)S(1)}, f32[3,128,128]{2,1,0:T(8,128)S(1)}, u32[]{:S(2)}, u32[]{:S(2)}) collective-permute-start(f32[3,128,128]{2,1,0:T(8,128)S(1)} %fusion), channel_id=1, source_target_pairs={{0,16},{16,32},{32,48},{48,64},{64,80},{80,96},{96,112},{112,128},... | collective-permute-start | bytes 589832 | tf_op jit(solution)/shard_map/ppermute | solution.py:28
  60.9 0.6 collective-permute-done.3
  61.6 6.2 %collective-permute-done.4 = f32[3,128,16]{2,1,0:T(8,128)} collective-permute-done((f32[3,128,16]{2,1,0:T(8,128)}, f32[3,128,16]{2,1,0:T(8,128)}, u32[]{:S(2)}, u32[]{:S(2)}) %collective-permute-start.4) | collective-permute-done | bytes 24608 | tf_op jit(solution)/shard_map/ppermute | solution.py:23
  67.8 1.2 %pad_maximum_fusion.1 = f32[3,128,160]{2,1,0:T(8,128)S(1)} fusion(f32[3,128,16]{2,1,0:T(8,128)} %collective-permute-done.4, f32[3,128,128]{2,1,0:T(8,128)S(1)} %fusion, f32[3,128,16]{2,1,0:T(8,128)} %collective-permute-done.3), kind=kLoop, calls=%fused_computation.4 | loop fusion | flops 122880 | bytes 491520 | tf_op jit(solution)/shard_map/concatenate | solution.py:24
  69.4 0.9 copy-done.14
  70.8 0.9 copy-done.15
  72.3 0.9 copy-done.16
  73.8 0.9 copy-done.17
  75.3 0.9 copy-done.18
  76.8 0.9 copy-done.19
  78.3 0.9 copy-done.7
  79.5 0.6 copy-done.1
  80.4 0.6 fusion.246
  81.0 1.9 %collective-permute-start.6 = (f32[2,2,2,2,4,128]{5,4,3,2,1,0:T(4,128)S(1)}, f32[2,2,2,2,4,128]{5,4,3,2,1,0:T(4,128)S(1)}, u32[]{:S(2)}, u32[]{:S(2)}) collective-permute-start(f32[2,2,2,2,4,128]{5,4,3,2,1,0:T(4,128)S(1)} %select_bitcast_fusion), channel_id=1, source_target_pairs={{0,16},{16,0},{32,48},{48,32},{64,80},{80,64},{96,112},{112,96},{1... | collective-permute-start | bytes 98312 | tf_op jit(solution)/shard_map/ppermute | solution.py:106
  82.9 1.6 %fusion.372 = f32[1,3,128,128]{3,2,1,0:T(8,128)} fusion(f32[3,128,128]{2,1,0:T(8,128)} %collective-permute-done.2, f32[1,128,128]{2,1,0:T(8,128)S(1)} %bitcast.380, f32[1,128,128]{2,1,0:T(8,128)S(1)} %bitcast.378, f32[1,128,128]{2,1,0:T(8,128)S(1)} %copy-done.9, f32[128,128]{1,0:T(8,128)S(1)} %convert_element_type.27), kind=kLoop, calls=%fused_computation.518 | loop fusion | flops 196608 | bytes 655360 | tf_op jit(solution)/shard_map/broadcast_in_dim | solution.py:155
  84.6 1.9 %collective-permute-start.7 = (f32[2,2,2,4,128]{4,3,2,1,0:T(4,128)S(1)}, f32[2,2,2,4,128]{4,3,2,1,0:T(4,128)S(1)}, u32[]{:S(2)}, u32[]{:S(2)}) collective-permute-start(f32[2,2,2,4,128]{4,3,2,1,0:T(4,128)S(1)} %select_bitcast_fusion.1), channel_id=1, source_target_pairs={{0,32},{16,48},{32,0},{48,16},{64,96},{80,112},{96,64},{112,80},{1... | collective-permute-start | bytes 49160 | tf_op jit(solution)/shard_map/ppermute | solution.py:106
  86.6 3.7 %collective-permute-done.7 = f32[2,2,2,4,128]{4,3,2,1,0:T(4,128)S(1)} collective-permute-done((f32[2,2,2,4,128]{4,3,2,1,0:T(4,128)S(1)}, f32[2,2,2,4,128]{4,3,2,1,0:T(4,128)S(1)}, u32[]{:S(2)}, u32[]{:S(2)}) %collective-permute-start.7) | collective-permute-done | bytes 16416 | tf_op jit(solution)/shard_map/ppermute | solution.py:106
  90.3 1.9 %collective-permute-start.8 = (f32[2,2,4,128]{3,2,1,0:T(4,128)S(1)}, f32[2,2,4,128]{3,2,1,0:T(4,128)S(1)}, u32[]{:S(2)}, u32[]{:S(2)}) collective-permute-start(f32[2,2,4,128]{3,2,1,0:T(4,128)S(1)} %select_bitcast_fusion.2), channel_id=1, source_target_pairs={{0,64},{16,80},{32,96},{48,112},{64,0},{80,16},{96,32},{112,48},{1... | collective-permute-start | bytes 24584 | tf_op jit(solution)/shard_map/ppermute | solution.py:106
  92.5 4.3 %collective-permute-done.8 = f32[2,2,4,128]{3,2,1,0:T(4,128)S(1)} collective-permute-done((f32[2,2,4,128]{3,2,1,0:T(4,128)S(1)}, f32[2,2,4,128]{3,2,1,0:T(4,128)S(1)}, u32[]{:S(2)}, u32[]{:S(2)}) %collective-permute-start.8) | collective-permute-done | bytes 8224 | tf_op jit(solution)/shard_map/ppermute | solution.py:106
  96.7 2.7 %collective-permute-start.9 = (f32[2,4,128]{2,1,0:T(4,128)S(1)}, f32[2,4,128]{2,1,0:T(4,128)S(1)}, u32[]{:S(2)}, u32[]{:S(2)}) collective-permute-start(f32[2,4,128]{2,1,0:T(4,128)S(1)} %select_bitcast_fusion.3), channel_id=1, source_target_pairs={{0,128},{16,144},{32,160},{48,176},{64,192},{80,208},{96,224},{112... | collective-permute-start | bytes 12296 | tf_op jit(solution)/shard_map/ppermute | solution.py:106
  99.5 6.8 %collective-permute-done.9 = f32[2,4,128]{2,1,0:T(4,128)S(1)} collective-permute-done((f32[2,4,128]{2,1,0:T(4,128)S(1)}, f32[2,4,128]{2,1,0:T(4,128)S(1)}, u32[]{:S(2)}, u32[]{:S(2)}) %collective-permute-start.9) | collective-permute-done | bytes 4128 | tf_op jit(solution)/shard_map/ppermute | solution.py:106
  106.3 3.0 %collective-permute-start.10 = (f32[4,128]{1,0:T(4,128)S(1)}, f32[4,128]{1,0:T(4,128)S(1)}, u32[]{:S(2)}, u32[]{:S(2)}) collective-permute-start(f32[4,128]{1,0:T(4,128)S(1)} %select_bitcast_fusion.4), channel_id=1, source_target_pairs={{0,256},{16,272},{32,288},{48,304},{64,320},{80,336},{96,352},{112... | collective-permute-start | bytes 6152 | tf_op jit(solution)/shard_map/ppermute | solution.py:106
  109.5 3.7 %collective-permute-done.10 = f32[4,128]{1,0:T(4,128)S(1)} collective-permute-done((f32[4,128]{1,0:T(4,128)S(1)}, f32[4,128]{1,0:T(4,128)S(1)}, u32[]{:S(2)}, u32[]{:S(2)}) %collective-permute-start.10) | collective-permute-done | bytes 2080 | tf_op jit(solution)/shard_map/ppermute | solution.py:106
  113.3 0.6 fusion.299
  113.9 0.7 fusion.2
  (135 shorter events, 10.7 us)
Async XLA Ops:
  0.6 1.0 copy-start.22
  1.6 0.8 copy-start.23
  1.6 0.8 copy-start.27
  2.6 0.8 copy-start.24
  3.4 0.8 copy-start.25
  4.3 0.8 copy-start.26
  5.3 28.9 %collective-permute-start = (f32[8,128,16]{2,1,0:T(8,128)S(1)}, f32[8,128,16]{2,1,0:T(8,128)S(1)}, u32[]{:S(2)}, u32[]{:S(2)}) collective-permute-start(f32[8,128,16]{2,1,0:T(8,128)S(1)} %get-tuple-element.111), channel_id=1, source_target_pairs={{0,1},{1,2},{2,3},{3,4},{4,5},{5,6},{6,7},{7,8},{8,9},{9,10},{10,1... | collective-permute-start | bytes 196616 | tf_op jit(solution)/shard_map/ppermute | solution.py:22
  11.1 23.1 %collective-permute-start.1 = (f32[8,128,16]{2,1,0:T(8,128)S(1)}, f32[8,128,16]{2,1,0:T(8,128)S(1)}, u32[]{:S(2)}, u32[]{:S(2)}) collective-permute-start(f32[8,128,16]{2,1,0:T(8,128)S(1)} %get-tuple-element.112), channel_id=1, source_target_pairs={{0,15},{1,0},{2,1},{3,2},{4,3},{5,4},{6,5},{7,6},{8,7},{9,8},{10,9... | collective-permute-start | bytes 196616 | tf_op jit(solution)/shard_map/ppermute | solution.py:23
  13.0 34.2 %collective-permute-start.2 = (f32[3,128,128]{2,1,0:T(8,128)}, f32[3,128,128]{2,1,0:T(8,128)}, u32[]{:S(2)}, u32[]{:S(2)}) collective-permute-start(f32[3,128,128]{2,1,0:T(8,128)} %bitcast), channel_id=1, source_target_pairs={{0,496},{16,0},{32,16},{48,32},{64,48},{80,64},{96,80},{112,96},{1... | collective-permute-start | bytes 589832 | tf_op jit(solution)/shard_map/ppermute | solution.py:28
  42.5 1.2 %copy-start = (f32[128,140]{1,0:T(8,128)}, f32[128,140]{1,0:T(8,128)S(1)}, u32[]{:S(2)}) copy-start(f32[128,140]{1,0:T(8,128)S(1)} %get-tuple-element.52) | copy-start | bytes 215044
  44.1 1.2 %copy-start.2 = (f32[128,136]{1,0:T(8,128)}, f32[128,136]{1,0:T(8,128)S(1)}, u32[]{:S(2)}) copy-start(f32[128,136]{1,0:T(8,128)S(1)} %get-tuple-element.14) | copy-start | bytes 208900
  44.1 1.2 %copy-start.4 = (f32[128,136]{1,0:T(8,128)}, f32[128,136]{1,0:T(8,128)S(1)}, u32[]{:S(2)}) copy-start(f32[128,136]{1,0:T(8,128)S(1)} %get-tuple-element.50) | copy-start | bytes 208900
  45.7 1.2 %copy-start.6 = (f32[128,132]{1,0:T(8,128)}, f32[128,132]{1,0:T(8,128)S(1)}, u32[]{:S(2)}) copy-start(f32[128,132]{1,0:T(8,128)S(1)} %get-tuple-element.87) | copy-start | bytes 202756
  45.7 1.2 %copy-start.10 = (f32[128,132]{1,0:T(8,128)}, f32[128,132]{1,0:T(8,128)S(1)}, u32[]{:S(2)}) copy-start(f32[128,132]{1,0:T(8,128)S(1)} %get-tuple-element.6) | copy-start | bytes 202756
  45.7 1.2 %copy-start.12 = (f32[128,132]{1,0:T(8,128)}, f32[128,132]{1,0:T(8,128)S(1)}, u32[]{:S(2)}) copy-start(f32[128,132]{1,0:T(8,128)S(1)} %get-tuple-element.48) | copy-start | bytes 202756
  47.2 1.0 copy-start.8
  49.0 12.5 %collective-permute-start.3 = (f32[3,128,16]{2,1,0:T(8,128)}, f32[3,128,16]{2,1,0:T(8,128)}, u32[]{:S(2)}, u32[]{:S(2)}) collective-permute-start(f32[3,128,16]{2,1,0:T(8,128)} %get-tuple-element.120), channel_id=1, source_target_pairs={{0,1},{1,2},{2,3},{3,4},{4,5},{5,6},{6,7},{7,8},{8,9},{9,10},{10,1... | collective-permute-start | bytes 73736 | tf_op jit(solution)/shard_map/ppermute | solution.py:22
  56.9 10.9 %collective-permute-start.4 = (f32[3,128,16]{2,1,0:T(8,128)}, f32[3,128,16]{2,1,0:T(8,128)}, u32[]{:S(2)}, u32[]{:S(2)}) collective-permute-start(f32[3,128,16]{2,1,0:T(8,128)} %get-tuple-element.121), channel_id=1, source_target_pairs={{0,15},{1,0},{2,1},{3,2},{4,3},{5,4},{6,5},{7,6},{8,7},{9,8},{10,9... | collective-permute-start | bytes 73736 | tf_op jit(solution)/shard_map/ppermute | solution.py:23
  58.8 55.0 %collective-permute-start.5 = (f32[3,128,128]{2,1,0:T(8,128)S(1)}, f32[3,128,128]{2,1,0:T(8,128)S(1)}, u32[]{:S(2)}, u32[]{:S(2)}) collective-permute-start(f32[3,128,128]{2,1,0:T(8,128)S(1)} %fusion), channel_id=1, source_target_pairs={{0,16},{16,32},{32,48},{48,64},{64,80},{80,96},{96,112},{112,128},... | collective-permute-start | bytes 589832 | tf_op jit(solution)/shard_map/ppermute | solution.py:28
  69.3 0.9 copy-start.14
  70.8 0.9 copy-start.15
  72.3 0.9 copy-start.16
  73.8 0.9 copy-start.17
  75.3 0.9 copy-start.18
  76.7 0.9 copy-start.19
  78.2 0.9 copy-start.7
  78.2 1.0 copy-start.20
  79.2 0.9 copy-start.1
  79.2 1.0 copy-start.3
  79.2 1.0 copy-start.5
  79.2 1.1 copy-start.11
  79.2 1.2 %copy-start.13 = (f32[128,132]{1,0:T(8,128)S(1)}, f32[128,132]{1,0:T(8,128)}, u32[]{:S(2)}) copy-start(f32[128,132]{1,0:T(8,128)} %copy-done.12) | copy-start | bytes 202756
  81.0 2.0 %copy-start.9 = (f32[1,128,128]{2,1,0:T(8,128)S(1)}, f32[1,128,128]{2,1,0:T(8,128)}, u32[]{:S(2)}) copy-start(f32[1,128,128]{2,1,0:T(8,128)} %copy-done.8) | copy-start | bytes 196612
  81.0 3.6 %collective-permute-start.6 = (f32[2,2,2,2,4,128]{5,4,3,2,1,0:T(4,128)S(1)}, f32[2,2,2,2,4,128]{5,4,3,2,1,0:T(4,128)S(1)}, u32[]{:S(2)}, u32[]{:S(2)}) collective-permute-start(f32[2,2,2,2,4,128]{5,4,3,2,1,0:T(4,128)S(1)} %select_bitcast_fusion), channel_id=1, source_target_pairs={{0,16},{16,0},{32,48},{48,32},{64,80},{80,64},{96,112},{112,96},{1... | collective-permute-start | bytes 98312 | tf_op jit(solution)/shard_map/ppermute | solution.py:106
  84.6 5.6 %collective-permute-start.7 = (f32[2,2,2,4,128]{4,3,2,1,0:T(4,128)S(1)}, f32[2,2,2,4,128]{4,3,2,1,0:T(4,128)S(1)}, u32[]{:S(2)}, u32[]{:S(2)}) collective-permute-start(f32[2,2,2,4,128]{4,3,2,1,0:T(4,128)S(1)} %select_bitcast_fusion.1), channel_id=1, source_target_pairs={{0,32},{16,48},{32,0},{48,16},{64,96},{80,112},{96,64},{112,80},{1... | collective-permute-start | bytes 49160 | tf_op jit(solution)/shard_map/ppermute | solution.py:106
  90.3 6.4 %collective-permute-start.8 = (f32[2,2,4,128]{3,2,1,0:T(4,128)S(1)}, f32[2,2,4,128]{3,2,1,0:T(4,128)S(1)}, u32[]{:S(2)}, u32[]{:S(2)}) collective-permute-start(f32[2,2,4,128]{3,2,1,0:T(4,128)S(1)} %select_bitcast_fusion.2), channel_id=1, source_target_pairs={{0,64},{16,80},{32,96},{48,112},{64,0},{80,16},{96,32},{112,48},{1... | collective-permute-start | bytes 24584 | tf_op jit(solution)/shard_map/ppermute | solution.py:106
  96.7 12.6 %copy-start.21 = (f32[128,132]{1,0:T(8,128)S(1)}, f32[128,132]{1,0:T(8,128)}, u32[]{:S(2)}) copy-start(f32[128,132]{1,0:T(8,128)} %get-tuple-element.63) | copy-start | bytes 202756
  96.7 9.5 %collective-permute-start.9 = (f32[2,4,128]{2,1,0:T(4,128)S(1)}, f32[2,4,128]{2,1,0:T(4,128)S(1)}, u32[]{:S(2)}, u32[]{:S(2)}) collective-permute-start(f32[2,4,128]{2,1,0:T(4,128)S(1)} %select_bitcast_fusion.3), channel_id=1, source_target_pairs={{0,128},{16,144},{32,160},{48,176},{64,192},{80,208},{96,224},{112... | collective-permute-start | bytes 12296 | tf_op jit(solution)/shard_map/ppermute | solution.py:106
  106.3 7.0 %collective-permute-start.10 = (f32[4,128]{1,0:T(4,128)S(1)}, f32[4,128]{1,0:T(4,128)S(1)}, u32[]{:S(2)}, u32[]{:S(2)}) collective-permute-start(f32[4,128]{1,0:T(4,128)S(1)} %select_bitcast_fusion.4), channel_id=1, source_target_pairs={{0,256},{16,272},{32,288},{48,304},{64,320},{80,336},{96,352},{112... | collective-permute-start | bytes 6152 | tf_op jit(solution)/shard_map/ppermute | solution.py:106

commit v2 on v1

--- a/solution.py
+++ b/solution.py
@@ -17,11 +17,16 @@
     return [(source, (source + steps) % count) for source in range(count)]
 
 
-def with_halo(block, axis, width):
-    count = lax.axis_size(axis)
-    low = lax.ppermute(block[..., block.shape[-1] - width :], axis, ring_pairs(count, 1))
-    high = lax.ppermute(block[..., :width], axis, ring_pairs(count, -1))
-    return jnp.concatenate([low, block, high], axis=-1)
+def grid_pairs(slices, cells, slice_steps, cell_steps):
+    return [
+        (t * cells + c, ((t + slice_steps) % slices) * cells + (c + cell_steps) % cells)
+        for t in range(slices)
+        for c in range(cells)
+    ]
+
+
+def lane_dense(strip):
+    return jnp.swapaxes(strip, -1, -2)
 
 
 def from_behind(value, axis, steps):
@@ -91,20 +96,8 @@
 
 def reduce_scatter_rows(value, axis):
     count = lax.axis_size(axis)
-    bits = count.bit_length() - 1
-    me = lax.axis_index(axis)
-    rows = value.shape[0] // count
-    buf = value.reshape((2,) * bits + (rows, value.shape[1]))
-    for bit in range(bits):
-        at = bits - 1 - bit
-        mine = ((me >> bit) & 1) == 1
-        low = lax.index_in_dim(buf, 0, axis=at, keepdims=False)
-        high = lax.index_in_dim(buf, 1, axis=at, keepdims=False)
-        keep = jnp.where(mine, high, low)
-        send = jnp.where(mine, low, high)
-        pairs = [(source, source ^ (1 << bit)) for source in range(count)]
-        buf = keep + lax.ppermute(send, axis, pairs)
-    return buf
+    pieces = value.reshape((count, value.shape[0] // count, value.shape[1]))
+    return jnp.sum(lax.all_to_all(pieces, axis, 0, 0, tiled=True), axis=0)
 
 
 def local(start_states, ocean_mask, depth_class, class_depth, drag_rate, tide_cos, tide_sin):
@@ -119,15 +112,22 @@
     )
     retain = 1.0 / (1.0 + drag_rate)
     initial = start_states[0]
+    slices, cells = slice_count, lax.axis_size("cell")
+    own = jnp.concatenate(
+        [initial, jnp.stack([sea_mask, depth_field, retain, tide_cos, tide_sin])], axis=0
+    )
+    width = own.shape[-1]
+    grid = ("tm", "cell")
+    from_left = lax.ppermute(lane_dense(own[..., width - 2 * halo :]), "cell", ring_pairs(cells, 1))
+    from_right = lax.ppermute(lane_dense(own[..., : 2 * halo]), "cell", ring_pairs(cells, -1))
+    next_left = lax.ppermute(
+        lane_dense(initial[..., width - halo :]), grid, grid_pairs(slices, cells, -1, 1)
+    )
+    next_right = lax.ppermute(lane_dense(initial[..., :halo]), grid, grid_pairs(slices, cells, -1, -1))
     following = from_behind(initial, "tm", -1)
-    wide = with_halo(
-        jnp.concatenate(
-            [initial, jnp.stack([sea_mask, depth_field, retain, tide_cos, tide_sin])], axis=0
-        ),
-        "cell",
-        halo,
-    )
+    wide = jnp.concatenate([lane_dense(from_left), own, lane_dense(from_right)], axis=-1)
     statics = wide[3:]
+    following = jnp.concatenate([lane_dense(next_left), following, lane_dense(next_right)], axis=-1)
     rotation = coriolis(sea_mask.shape[0])
     current = wide[:3] * statics[0]
     phase_unit = 2.0 * math.pi / (slice_count * STEPS)
@@ -137,15 +137,17 @@
         current = advance_wide(
             current, cropped(statics, 2 * step_number), rotation, jnp.cos(phase_now), jnp.sin(phase_now)
         )
-        stored.append(cropped(current[1:], halo - 2 * (step_number + 1)))
-    defect = sea_mask * (current - following)
+        stored.append(cropped(current[1:], 2 * halo - 2 * (step_number + 1)))
+    adjoint = cropped(statics[0], halo) * (current - following)
+    defect = cropped(adjoint, halo)
     behind = from_behind(defect, "tm", 1)
-    adjoint = with_halo(defect, "cell", halo)
     drag_total = jnp.zeros_like(drag_rate)
     for back in range(STEPS):
         step_number = STEPS - 1 - back
         margin = halo - 2 * back
-        adjoint, east_part, north_part = adjoint_step(adjoint, cropped(statics, 2 * back), rotation)
+        adjoint, east_part, north_part = adjoint_step(
+            adjoint, cropped(statics, halo + 2 * back), rotation
+        )
         outputs = stored[step_number]
         drag_total = drag_total - (
             cropped(east_part, margin) * outputs[0] + cropped(north_part, margin) * outputs[1]

time: 115 us -> 83.1 us (0.72)
  the two profiles are of different devices: /device:TPU:254 before, /device:TPU:1 now
where the time goes in v2:
time: 83.1 us; the launch traced here: 82.6 us
  starting transfers between devices  47.9 us (58%)
  other arithmetic  16 us (19%)
  waiting for transfers between devices  8.93 us (11%)
  local copies, waits for them, and re-layouts  7.17 us (9%)
  between operations  2.61 us (3%)
    all_to_all x1, starting transfers between devices, reduce_scatter_rows(): return jnp.sum(lax.all_to_all(pieces, axis, 0, 0, tiled=True), axis=0)  15.9 us
    ppermute x1, starting transfers between devices, local(): lax.ppermute(lane_dense(own[..., :2 * halo]), 'cell', ring_pairs(cells, -1))  10.4 us
    ppermute x1, starting transfers between devices, local(): lax.ppermute(lane_dense(initial[..., :halo]), grid, grid_pairs(slices, ce...  9.32 us
    ppermute x2, starting transfers between devices, from_behind(): return lax.ppermute(value, axis, ring_pairs(lax.axis_size(axis), steps))  6.4 us
    all_to_all x1, waiting for transfers between devices, reduce_scatter_rows(): return jnp.sum(lax.all_to_all(pieces, axis, 0, 0, tiled=True), axis=0)  5.55 us
    unnamed x17, local copies, waits for them, and re-layouts  4.28 us
    ppermute x1, starting transfers between devices, local(): lax.ppermute(lane_dense(own[..., width - 2 * halo:]), 'cell', ring_pairs(...  3.95 us
    ppermute x1, waiting for transfers between devices, local(): lax.ppermute(lane_dense(own[..., :2 * halo]), 'cell', ring_pairs(cells, -1))  3.36 us
  transfers between devices with their start and end apart: 7, of which 2 were waited for; matrix products, arithmetic and copies ran while one was open for 12% of the time, Pallas kernels for 0%

profile of v2, /device:TPU:1, one launch (start us, length us, event | category | flops | bytes accessed | tf_op | source)
XLA Modules:
  0.0 82.6 jit_solution(11089324630556255294)
XLA Ops:
  0.6 1.0 %constant_dynamic-update-slice_fusion = f32[8,128,128]{2,1,0:T(8,128)S(1)} fusion(f32[1,3,128,128]{3,2,1,0:T(8,128)} %param.7), kind=kLoop, calls=%fused_computation.502 | loop fusion | bytes 393216
  1.7 0.8 copy-done.2
  2.6 0.8 copy-done.3
  3.5 0.8 copy-done.4
  4.3 0.8 %copy-done.5 = f32[128,128]{1,0:T(8,128)S(1)} copy-done((f32[128,128]{1,0:T(8,128)S(1)}, f32[128,128]{1,0:T(8,128)}, u32[]{:S(2)}) %copy-start.5) | copy-done | bytes 65560
  5.3 3.9 %collective-permute-start = (f32[8,32,128]{1,2,0:T(8,128)S(1)}, f32[8,32,128]{1,2,0:T(8,128)S(1)}, u32[]{:S(2)}, u32[]{:S(2)}) collective-permute-start(f32[8,32,128]{1,2,0:T(8,128)S(1)} %get-tuple-element.121), channel_id=1, source_target_pairs={{0,1},{1,2},{2,3},{3,4},{4,5},{5,6},{6,7},{7,8},{8,9},{9,10},{10,1... | collective-permute-start | bytes 393224 | tf_op jit(solution)/shard_map/ppermute | solution.py:121
  9.3 10.4 %collective-permute-start.1 = (f32[8,32,128]{1,2,0:T(8,128)S(1)}, f32[8,32,128]{1,2,0:T(8,128)S(1)}, u32[]{:S(2)}, u32[]{:S(2)}) collective-permute-start(f32[8,32,128]{1,2,0:T(8,128)S(1)} %get-tuple-element.122), channel_id=1, source_target_pairs={{0,15},{1,0},{2,1},{3,2},{4,3},{5,4},{6,5},{7,6},{8,7},{9,8},{10,9... | collective-permute-start | bytes 393224 | tf_op jit(solution)/shard_map/ppermute | solution.py:122
  19.7 2.9 %collective-permute-start.3 = (f32[3,128,128]{2,1,0:T(8,128)S(1)}, f32[3,128,128]{2,1,0:T(8,128)S(1)}, u32[]{:S(2)}, u32[]{:S(2)}) collective-permute-start(f32[3,128,128]{2,1,0:T(8,128)S(1)} %bitcast.425), channel_id=1, source_target_pairs={{0,496},{16,0},{32,16},{48,32},{64,48},{80,64},{96,80},{112,96},{1... | collective-permute-start | bytes 589832 | tf_op jit(solution)/shard_map/ppermute | solution.py:33
  22.7 1.9 %collective-permute-start.2 = (f32[3,16,128]{1,2,0:T(8,128)S(1)}, f32[3,16,128]{1,2,0:T(8,128)}, u32[]{:S(2)}, u32[]{:S(2)}) collective-permute-start(f32[3,16,128]{1,2,0:T(8,128)S(1)} %get-tuple-element.130), channel_id=1, source_target_pairs={{0,497},{1,498},{2,499},{3,500},{4,501},{5,502},{6,503},{7,504},{8... | collective-permute-start | bytes 73736 | tf_op jit(solution)/shard_map/ppermute | solution.py:123
  24.6 9.3 %collective-permute-start.4 = (f32[3,16,128]{1,2,0:T(8,128)S(1)}, f32[3,16,128]{1,2,0:T(8,128)}, u32[]{:S(2)}, u32[]{:S(2)}) collective-permute-start(f32[3,16,128]{1,2,0:T(8,128)S(1)} %get-tuple-element.131), channel_id=1, source_target_pairs={{0,511},{1,496},{2,497},{3,498},{4,499},{5,500},{6,501},{7,502},{8... | collective-permute-start | bytes 73736 | tf_op jit(solution)/shard_map/ppermute | solution.py:126
  35.3 3.4 %collective-permute-done.1 = f32[8,32,128]{1,2,0:T(8,128)S(1)} collective-permute-done((f32[8,32,128]{1,2,0:T(8,128)S(1)}, f32[8,32,128]{1,2,0:T(8,128)S(1)}, u32[]{:S(2)}, u32[]{:S(2)}) %collective-permute-start.1) | collective-permute-done | bytes 131104 | tf_op jit(solution)/shard_map/ppermute | solution.py:122
  38.6 0.5 pad_maximum_fusion
  40.2 0.3 slice_add_fusion.7
  40.5 0.4 fusion.258
  41.1 0.3 slice_add_fusion.6
  41.5 0.4 fusion.259
  42.0 0.3 slice_add_fusion.5
  42.4 0.4 fusion.262
  43.0 0.3 slice_add_fusion.4
  43.3 0.4 fusion.263
  43.9 0.3 slice_add_fusion.3
  44.2 0.4 fusion.266
  44.8 0.3 slice_add_fusion.2
  45.1 0.4 fusion.267
  45.7 0.3 slice_add_fusion.1
  46.0 0.4 fusion.270
  46.6 0.3 slice_add_fusion
  46.9 0.4 fusion.127
  47.5 1.2 %fusion = f32[3,128,160]{2,1,0:T(8,128)S(1)} fusion(f32[1,128,160]{2,1,0:T(8,128)S(1)} %get-tuple-element.120, f32[1,128,160]{2,1,0:T(8,128)S(1)} %get-tuple-element.119, f32[1,128,160]{2,1,0:T(8,128)S(1)} %get-tuple-element.197, f32[3,128,16]{2,1,0:T(8,128)} %bitcast.51, f32[3,128,128]{2,1,0:T(8,128)S(1)} %collective-permute-done.3, ...), kind=kLoop, calls=%fused_computation.7 | loop fusion | flops 368640 | bytes 819200 | tf_op jit(solution)/shard_map/mul | solution.py:141
  48.9 0.8 fusion.333
  49.7 0.2 fusion.112
  50.0 0.4 fusion.106
  50.4 0.2 fusion.97
  50.7 0.4 fusion.91
  51.1 0.2 fusion.82
  51.4 0.4 fusion.76
  51.8 0.2 fusion.67
  52.0 0.4 fusion.61
  52.7 0.4 fusion.46
  53.1 0.2 fusion.37
  53.4 0.4 fusion.31
  54.0 0.4 fusion.16
  54.4 1.3 %fusion.273 = f32[128,128]{1,0:T(8,128)} fusion(f32[1,128,188]{2,1,0:T(8,128)S(1)} %bitcast.428, f32[1,128,188]{2,1,0:T(8,128)S(1)} %bitcast.427, f32[1,128,184]{2,1,0:T(8,128)S(1)} %bitcast.429, f32[128,136]{1,0:T(8,128)S(1)} %get-tuple-element.64, f32[1,128,184]{2,1,0:T(8,128)S(1)} %bitcast.430, f32[128,136]{1,0:T(8,128)S(1)} %get-tuple-element.63, ...), kind=kLoop, calls=%fused_computation.440 | loop fusion | flops 524288 | bytes 2162688 | tf_op jit(solution)/shard_map/sub | solution.py:152
  55.7 15.9 %all-to-all-start = ((f32[32,4,128]{2,1,0:T(4,128)}), f32[32,4,128]{2,1,0:T(4,128)S(1)}, u32[]{:S(2)}, u32[]{:S(2)}) async-start(f32[32,4,128]{2,1,0:T(4,128)} %bitcast.114), calls=%async_computation | async-start | bytes 131072 | tf_op jit(solution)/shard_map/all_to_all | solution.py:100
  71.9 3.5 %collective-permute-start.5 = (f32[3,128,128]{2,1,0:T(8,128)S(1)}, f32[3,128,128]{2,1,0:T(8,128)S(1)}, u32[]{:S(2)}, u32[]{:S(2)}) collective-permute-start(f32[3,128,128]{2,1,0:T(8,128)S(1)} %get-tuple-element.125), channel_id=1, source_target_pairs={{0,16},{16,32},{32,48},{48,64},{64,80},{80,96},{96,112},{112,128},... | collective-permute-start | bytes 589832 | tf_op jit(solution)/shard_map/ppermute | solution.py:33
  75.7 5.6 %all-to-all-done = f32[32,4,128]{2,1,0:T(4,128)S(1)} async-done(((f32[32,4,128]{2,1,0:T(4,128)}), f32[32,4,128]{2,1,0:T(4,128)S(1)}, u32[]{:S(2)}, u32[]{:S(2)}) %all-to-all-start) | async-done | bytes 65568 | tf_op jit(solution)/shard_map/all_to_all | solution.py:100
  81.3 0.6 broadcast_multiply_fusion
  81.9 0.7 fusion.2
  (84 shorter events, 4.9 us)
Async XLA Ops:
  0.6 1.0 %copy-start.1 = (s32[128,128]{1,0:T(8,128)S(1)}, s32[128,128]{1,0:T(8,128)}, u32[]{:S(2)}) copy-start(s32[128,128]{1,0:T(8,128)} %param.8) | copy-start | bytes 196612
  1.6 0.8 %copy-start.2 = (s32[128,128]{1,0:T(8,128)S(1)}, s32[128,128]{1,0:T(8,128)}, u32[]{:S(2)}) copy-start(s32[128,128]{1,0:T(8,128)} %param.9) | copy-start | bytes 196612
  1.6 0.8 %copy-start.6 = (f32[8]{0:T(128)S(1)}, f32[8]{0:T(128)}, u32[]{:S(2)}) copy-start(f32[8]{0:T(128)} %param.10) | copy-start | bytes 100
  2.6 0.8 %copy-start.3 = (f32[128,128]{1,0:T(8,128)S(1)}, f32[128,128]{1,0:T(8,128)}, u32[]{:S(2)}) copy-start(f32[128,128]{1,0:T(8,128)} %param.11) | copy-start | bytes 196612
  3.4 0.8 %copy-start.4 = (f32[128,128]{1,0:T(8,128)S(1)}, f32[128,128]{1,0:T(8,128)}, u32[]{:S(2)}) copy-start(f32[128,128]{1,0:T(8,128)} %param.12) | copy-start | bytes 196612
  4.3 0.8 %copy-start.5 = (f32[128,128]{1,0:T(8,128)S(1)}, f32[128,128]{1,0:T(8,128)}, u32[]{:S(2)}) copy-start(f32[128,128]{1,0:T(8,128)} %param.13) | copy-start | bytes 196612
  5.1 14.6 %copy-start = (f32[1,3,128,128]{3,2,1,0:T(8,128)S(1)}, f32[1,3,128,128]{3,2,1,0:T(8,128)}, u32[]{:S(2)}) copy-start(f32[1,3,128,128]{3,2,1,0:T(8,128)} %param.7) | copy-start | bytes 589828
  5.3 29.9 %collective-permute-start = (f32[8,32,128]{1,2,0:T(8,128)S(1)}, f32[8,32,128]{1,2,0:T(8,128)S(1)}, u32[]{:S(2)}, u32[]{:S(2)}) collective-permute-start(f32[8,32,128]{1,2,0:T(8,128)S(1)} %get-tuple-element.121), channel_id=1, source_target_pairs={{0,1},{1,2},{2,3},{3,4},{4,5},{5,6},{6,7},{7,8},{8,9},{9,10},{10,1... | collective-permute-start | bytes 393224 | tf_op jit(solution)/shard_map/ppermute | solution.py:121
  9.3 29.3 %collective-permute-start.1 = (f32[8,32,128]{1,2,0:T(8,128)S(1)}, f32[8,32,128]{1,2,0:T(8,128)S(1)}, u32[]{:S(2)}, u32[]{:S(2)}) collective-permute-start(f32[8,32,128]{1,2,0:T(8,128)S(1)} %get-tuple-element.122), channel_id=1, source_target_pairs={{0,15},{1,0},{2,1},{3,2},{4,3},{5,4},{6,5},{7,6},{8,7},{9,8},{10,9... | collective-permute-start | bytes 393224 | tf_op jit(solution)/shard_map/ppermute | solution.py:122
  19.7 27.8 %collective-permute-start.3 = (f32[3,128,128]{2,1,0:T(8,128)S(1)}, f32[3,128,128]{2,1,0:T(8,128)S(1)}, u32[]{:S(2)}, u32[]{:S(2)}) collective-permute-start(f32[3,128,128]{2,1,0:T(8,128)S(1)} %bitcast.425), channel_id=1, source_target_pairs={{0,496},{16,0},{32,16},{48,32},{64,48},{80,64},{96,80},{112,96},{1... | collective-permute-start | bytes 589832 | tf_op jit(solution)/shard_map/ppermute | solution.py:33
  22.7 24.8 %collective-permute-start.2 = (f32[3,16,128]{1,2,0:T(8,128)S(1)}, f32[3,16,128]{1,2,0:T(8,128)}, u32[]{:S(2)}, u32[]{:S(2)}) collective-permute-start(f32[3,16,128]{1,2,0:T(8,128)S(1)} %get-tuple-element.130), channel_id=1, source_target_pairs={{0,497},{1,498},{2,499},{3,500},{4,501},{5,502},{6,503},{7,504},{8... | collective-permute-start | bytes 73736 | tf_op jit(solution)/shard_map/ppermute | solution.py:123
  24.6 22.9 %collective-permute-start.4 = (f32[3,16,128]{1,2,0:T(8,128)S(1)}, f32[3,16,128]{1,2,0:T(8,128)}, u32[]{:S(2)}, u32[]{:S(2)}) collective-permute-start(f32[3,16,128]{1,2,0:T(8,128)S(1)} %get-tuple-element.131), channel_id=1, source_target_pairs={{0,511},{1,496},{2,497},{3,498},{4,499},{5,500},{6,501},{7,502},{8... | collective-permute-start | bytes 73736 | tf_op jit(solution)/shard_map/ppermute | solution.py:126
  55.7 25.5 %all-to-all-start = ((f32[32,4,128]{2,1,0:T(4,128)}), f32[32,4,128]{2,1,0:T(4,128)S(1)}, u32[]{:S(2)}, u32[]{:S(2)}) async-start(f32[32,4,128]{2,1,0:T(4,128)} %bitcast.114), calls=%async_computation | async-start | bytes 131072 | tf_op jit(solution)/shard_map/all_to_all | solution.py:100
  71.9 9.9 %collective-permute-start.5 = (f32[3,128,128]{2,1,0:T(8,128)S(1)}, f32[3,128,128]{2,1,0:T(8,128)S(1)}, u32[]{:S(2)}, u32[]{:S(2)}) collective-permute-start(f32[3,128,128]{2,1,0:T(8,128)S(1)} %get-tuple-element.125), channel_id=1, source_target_pairs={{0,16},{16,32},{32,48},{48,64},{64,80},{80,96},{96,112},{112,128},... | collective-permute-start | bytes 589832 | tf_op jit(solution)/shard_map/ppermute | solution.py:33

commit v3 on v2

--- a/solution.py
+++ b/solution.py
@@ -15,14 +15,6 @@
 
 def ring_pairs(count, steps):
     return [(source, (source + steps) % count) for source in range(count)]
-
-
-def grid_pairs(slices, cells, slice_steps, cell_steps):
-    return [
-        (t * cells + c, ((t + slice_steps) % slices) * cells + (c + cell_steps) % cells)
-        for t in range(slices)
-        for c in range(cells)
-    ]
 
 
 def lane_dense(strip):
@@ -117,17 +109,26 @@
         [initial, jnp.stack([sea_mask, depth_field, retain, tide_cos, tide_sin])], axis=0
     )
     width = own.shape[-1]
-    grid = ("tm", "cell")
-    from_left = lax.ppermute(lane_dense(own[..., width - 2 * halo :]), "cell", ring_pairs(cells, 1))
-    from_right = lax.ppermute(lane_dense(own[..., : 2 * halo]), "cell", ring_pairs(cells, -1))
-    next_left = lax.ppermute(
-        lane_dense(initial[..., width - halo :]), grid, grid_pairs(slices, cells, -1, 1)
-    )
-    next_right = lax.ppermute(lane_dense(initial[..., :halo]), grid, grid_pairs(slices, cells, -1, -1))
     following = from_behind(initial, "tm", -1)
-    wide = jnp.concatenate([lane_dense(from_left), own, lane_dense(from_right)], axis=-1)
+    fields, lanes = own.shape[0], own.shape[1]
+
+    def strips(at_right):
+        mine = own[..., width - 2 * halo :] if at_right else own[..., : 2 * halo]
+        theirs = following[..., width - halo :] if at_right else following[..., :halo]
+        return jnp.concatenate(
+            [lane_dense(mine).reshape(-1, lanes), lane_dense(theirs).reshape(-1, lanes)], axis=0
+        )
+
+    def unpacked(packed):
+        mine = lane_dense(packed[: fields * 2 * halo].reshape(fields, 2 * halo, lanes))
+        theirs = lane_dense(packed[fields * 2 * halo :].reshape(3, halo, lanes))
+        return mine, theirs
+
+    left_own, left_next = unpacked(lax.ppermute(strips(True), "cell", ring_pairs(cells, 1)))
+    right_own, right_next = unpacked(lax.ppermute(strips(False), "cell", ring_pairs(cells, -1)))
+    wide = jnp.concatenate([left_own, own, right_own], axis=-1)
     statics = wide[3:]
-    following = jnp.concatenate([lane_dense(next_left), following, lane_dense(next_right)], axis=-1)
+    following = jnp.concatenate([left_next, following, right_next], axis=-1)
     rotation = coriolis(sea_mask.shape[0])
     current = wide[:3] * statics[0]
     phase_unit = 2.0 * math.pi / (slice_count * STEPS)

time: 83.1 us -> 57.8 us (0.70)
  starting transfers between devices: 47.9 us -> 32.4 us
  other arithmetic: 16 us -> 5.16 us
  local copies, waits for them, and re-layouts: 7.17 us -> 12 us
  waiting for transfers between devices: 8.93 us -> 5.12 us
    ppermute x4 -> x2, starting transfers between devices: 25.6 us -> 8.91 us  [the longest x1 6.99 us: local(): lax.ppermute(strips(False), 'cell', ring_pairs(cells, -1))]
    ppermute x2, starting transfers between devices: 6.4 us -> 12.5 us  [from_behind(): return lax.ppermute(value, axis, ring_pairs(lax.axis_size(axis), steps))]
    all_to_all x1, starting transfers between devices: 15.9 us -> 11 us  [reduce_scatter_rows(): return jnp.sum(lax.all_to_all(pieces, axis, 0, 0, tiled=True), axis=0)]
    ppermute x4 -> x2, waiting for transfers between devices: 3.37 us -> 0.17 us  [the longest x1 0.17 us: local(): lax.ppermute(strips(False), 'cell', ring_pairs(cells, -1))]
    unnamed x17 -> x24, local copies, waits for them, and re-layouts: 4.28 us -> 6.68 us
    slice x32, local copies, waits for them, and re-layouts: 0.62 us -> 2.64 us  [across_rows(): upper_rows = jnp.concatenate([values_in[..., 1:, :], zeros_row], axis=-2)]
    mul x8, other arithmetic: 2.71 us -> 0.74 us  [adjoint_step(): east_part = mask_keep * adjoint[1]]
    slice x0 -> x8, local copies, waits for them, and re-layouts: none -> 1.65 us  [the longest x3 0.9 us: unpacked(): packed[:fields * 2 * halo].reshape(fields, 2 * halo, lanes)]
  transfers between devices with their start and end apart: 7 -> 5, of which waited for: 2 -> 2; matrix products, arithmetic and copies ran while one was open for 12% -> 4% of each run, Pallas kernels for 0% -> 0%
where the time goes in v3:
time: 57.8 us; the launch traced here: 57.2 us
  starting transfers between devices  32.4 us (56%)
  local copies, waits for them, and re-layouts  12 us (21%)
  other arithmetic  5.16 us (9%)
  waiting for transfers between devices  5.12 us (9%)
  between operations  2.62 us (5%)
    ppermute x2, starting transfers between devices, from_behind(): return lax.ppermute(value, axis, ring_pairs(lax.axis_size(axis), steps))  12.5 us
    all_to_all x1, starting transfers between devices, reduce_scatter_rows(): return jnp.sum(lax.all_to_all(pieces, axis, 0, 0, tiled=True), axis=0)  11 us
    ppermute x1, starting transfers between devices, local(): lax.ppermute(strips(False), 'cell', ring_pairs(cells, -1))  6.99 us
    unnamed x24, local copies, waits for them, and re-layouts  6.68 us
    all_to_all x1, waiting for transfers between devices, reduce_scatter_rows(): return jnp.sum(lax.all_to_all(pieces, axis, 0, 0, tiled=True), axis=0)  4.95 us
    slice x32, local copies, waits for them, and re-layouts, across_rows(): upper_rows = jnp.concatenate([values_in[..., 1:, :], zeros_row], axis=-2)  2.64 us
    ppermute x1, starting transfers between devices, local(): lax.ppermute(strips(True), 'cell', ring_pairs(cells, 1))  1.92 us
  transfers between devices with their start and end apart: 5, of which 2 were waited for; matrix products, arithmetic and copies ran while one was open for 4% of the time, Pallas kernels for 0%

profile of v3, /device:TPU:1, one launch (start us, length us, event | category | flops | bytes accessed | tf_op | source)
XLA Modules:
  0.0 57.2 jit_solution(4259444149812670650)
XLA Ops:
  0.6 1.1 %copy.25 = f32[1,3,128,128]{2,3,1,0:T(8,128)S(1)} copy(f32[1,3,128,128]{3,2,1,0:T(8,128)} %param.7) | data formatting | bytes 393216 | tf_op args[0]
  1.7 8.9 %collective-permute-start = (f32[3,128,128]{1,2,0:T(8,128)S(1)}, f32[3,128,128]{1,2,0:T(8,128)S(1)}, u32[]{:S(2)}, u32[]{:S(2)}) collective-permute-start(f32[3,128,128]{1,2,0:T(8,128)S(1)} %bitcast.436), channel_id=1, source_target_pairs={{0,496},{16,0},{32,16},{48,32},{64,48},{80,64},{96,80},{112,96},{1... | collective-permute-start | bytes 589832 | tf_op jit(solution)/shard_map/ppermute | solution.py:25
  10.8 0.7 %copy-done.2 = s32[128,128]{1,0:T(8,128)S(1)} copy-done((s32[128,128]{1,0:T(8,128)S(1)}, s32[128,128]{1,0:T(8,128)}, u32[]{:S(2)}) %copy-start.2) | copy-done | bytes 65560
  11.5 0.1 select_reduce_fusion
  11.7 0.7 %copy-done.3 = f32[128,128]{1,0:T(8,128)S(1)} copy-done((f32[128,128]{1,0:T(8,128)S(1)}, f32[128,128]{1,0:T(8,128)}, u32[]{:S(2)}) %copy-start.3) | copy-done | bytes 65560
  12.6 0.7 %copy-done.4 = f32[128,128]{1,0:T(8,128)S(1)} copy-done((f32[128,128]{1,0:T(8,128)S(1)}, f32[128,128]{1,0:T(8,128)}, u32[]{:S(2)}) %copy-start.4) | copy-done | bytes 65560
  13.4 0.7 %copy-done.5 = f32[128,128]{1,0:T(8,128)S(1)} copy-done((f32[128,128]{1,0:T(8,128)S(1)}, f32[128,128]{1,0:T(8,128)}, u32[]{:S(2)}) %copy-start.5) | copy-done | bytes 65560
  14.4 1.9 %collective-permute-start.1 = (f32[304,128]{1,0:T(8,128)S(1)}, f32[304,128]{1,0:T(8,128)S(1)}, u32[]{:S(2)}, u32[]{:S(2)}) collective-permute-start(f32[304,128]{1,0:T(8,128)S(1)} %pad_maximum_fusion.1), channel_id=1, source_target_pairs={{0,1},{1,2},{2,3},{3,4},{4,5},{5,6},{6,7},{7,8},{8,9},{9,10},{10,1... | collective-permute-start | bytes 466952 | tf_op jit(solution)/shard_map/ppermute | solution.py:127
  16.3 7.0 %collective-permute-start.2 = (f32[304,128]{1,0:T(8,128)S(1)}, f32[304,128]{1,0:T(8,128)S(1)}, u32[]{:S(2)}, u32[]{:S(2)}) collective-permute-start(f32[304,128]{1,0:T(8,128)S(1)} %pad_maximum_fusion.2), channel_id=1, source_target_pairs={{0,15},{1,0},{2,1},{3,2},{4,3},{5,4},{6,5},{7,6},{8,7},{9,8},{10,9... | collective-permute-start | bytes 466952 | tf_op jit(solution)/shard_map/ppermute | solution.py:128
  24.7 0.7 %copy-done = f32[304,128]{1,0:T(8,128)} copy-done((f32[304,128]{1,0:T(8,128)}, f32[304,128]{1,0:T(8,128)S(1)}, u32[]{:S(2)}) %copy-start) | copy-done | bytes 155672
  25.3 0.2 collective-permute-done.2
  25.5 0.9 %slice-done = f32[256,128]{1,0:T(8,128)S(1)} async-done(((f32[304,128]{1,0:T(8,128)}), f32[256,128]{1,0:T(8,128)S(1)}, s32[]{:S(2)}) %slice-start) | async-done | bytes 131096 | tf_op jit(solution)/shard_map/slice | solution.py:123
  26.7 0.1 slice_add_fusion.1
  26.9 0.1 fusion.65
  27.2 0.1 slice_add_fusion
  27.4 0.1 fusion.100
  27.7 0.1 slice_add_fusion.3
  27.9 0.1 fusion.103
  28.1 0.1 slice_add_fusion.2
  28.4 0.1 fusion.138
  28.6 0.1 slice_add_fusion.5
  28.8 0.1 fusion.141
  29.1 0.1 slice_add_fusion.4
  29.3 0.1 fusion.177
  29.5 0.1 slice_add_fusion.7
  29.7 0.1 fusion.180
  30.0 0.1 slice_add_fusion.6
  30.2 0.1 fusion.176
  30.4 0.7 %slice-done.1 = f32[48,128]{1,0:T(8,128)S(1)} async-done(((f32[304,128]{1,0:T(8,128)}), f32[48,128]{1,0:T(8,128)S(1)}, s32[]{:S(2)}) %slice-start.1) | async-done | bytes 24600 | tf_op jit(solution)/shard_map/slice | solution.py:124
  31.5 0.1 fusion.161
  31.8 0.1 fusion.146
  32.0 0.1 fusion.209
  32.2 0.1 fusion.200
  32.4 0.1 fusion.194
  32.6 0.1 fusion.185
  33.0 0.1 fusion.230
  33.2 0.1 fusion.224
  33.4 0.1 fusion.215
  33.6 0.1 fusion.269
  33.8 0.1 fusion.260
  34.2 0.2 fusion.273
  34.4 0.7 %copy.31 = f32[128,128]{1,0:T(8,128)} copy(f32[128,128]{0,1:T(8,128)S(1)} %fusion.273) | data formatting | bytes 131072 | tf_op jit(solution)/shard_map/sub | solution.py:153
  35.2 11.0 %all-to-all-start = ((f32[32,4,128]{2,1,0:T(4,128)}), f32[32,4,128]{2,1,0:T(4,128)S(1)}, u32[]{:S(2)}, u32[]{:S(2)}) async-start(f32[32,4,128]{2,1,0:T(4,128)} %bitcast.122), calls=%async_computation | async-start | bytes 131072 | tf_op jit(solution)/shard_map/all_to_all | solution.py:92
  46.4 3.5 %collective-permute-start.3 = (f32[3,128,128]{1,2,0:T(8,128)S(1)}, f32[3,128,128]{1,2,0:T(8,128)S(1)}, u32[]{:S(2)}, u32[]{:S(2)}) collective-permute-start(f32[3,128,128]{1,2,0:T(8,128)S(1)} %get-tuple-element.135), channel_id=1, source_target_pairs={{0,16},{16,32},{32,48},{48,64},{64,80},{80,96},{96,112},{112,128},... | collective-permute-start | bytes 589832 | tf_op jit(solution)/shard_map/ppermute | solution.py:25
  49.9 0.8 %copy.32 = f32[1,3,128,128]{3,2,1,0:T(8,128)} copy(f32[1,3,128,128]{2,3,1,0:T(8,128)S(1)} %get-tuple-element.136) | data formatting | bytes 393216
  50.8 4.9 %all-to-all-done = f32[32,4,128]{2,1,0:T(4,128)S(1)} async-done(((f32[32,4,128]{2,1,0:T(4,128)}), f32[32,4,128]{2,1,0:T(4,128)S(1)}, u32[]{:S(2)}, u32[]{:S(2)}) %all-to-all-start) | async-done | bytes 65568 | tf_op jit(solution)/shard_map/all_to_all | solution.py:92
  55.8 0.6 %broadcast_multiply_fusion = f32[4,128]{1,0:T(4,128)} fusion(f32[4,128]{1,0:T(4,128)S(1)} %reduce_sum.19), kind=kLoop, calls=%fused_computation.501 | loop fusion | flops 512 | bytes 4096 | tf_op jit(solution)/shard_map/div | solution.py:157
  56.4 0.8 %copy.33 = f32[1,3,128,128]{3,2,1,0:T(8,128)} copy(f32[1,3,128,128]{2,3,1,0:T(8,128)S(1)} %fusion.2) | data formatting | bytes 393216
  (97 shorter events, 4.5 us)
Async XLA Ops:
  1.7 9.0 %copy-start.1 = (s32[128,128]{1,0:T(8,128)S(1)}, s32[128,128]{1,0:T(8,128)}, u32[]{:S(2)}) copy-start(s32[128,128]{1,0:T(8,128)} %param.8) | copy-start | bytes 196612
  1.7 12.7 %collective-permute-start = (f32[3,128,128]{1,2,0:T(8,128)S(1)}, f32[3,128,128]{1,2,0:T(8,128)S(1)}, u32[]{:S(2)}, u32[]{:S(2)}) collective-permute-start(f32[3,128,128]{1,2,0:T(8,128)S(1)} %bitcast.436), channel_id=1, source_target_pairs={{0,496},{16,0},{32,16},{48,32},{64,48},{80,64},{96,80},{112,96},{1... | collective-permute-start | bytes 589832 | tf_op jit(solution)/shard_map/ppermute | solution.py:25
  10.7 0.8 %copy-start.2 = (s32[128,128]{1,0:T(8,128)S(1)}, s32[128,128]{1,0:T(8,128)}, u32[]{:S(2)}) copy-start(s32[128,128]{1,0:T(8,128)} %param.9) | copy-start | bytes 196612
  10.7 0.8 %copy-start.6 = (f32[8]{0:T(128)S(1)}, f32[8]{0:T(128)}, u32[]{:S(2)}) copy-start(f32[8]{0:T(128)} %param.10) | copy-start | bytes 100
  11.6 0.8 %copy-start.3 = (f32[128,128]{1,0:T(8,128)S(1)}, f32[128,128]{1,0:T(8,128)}, u32[]{:S(2)}) copy-start(f32[128,128]{1,0:T(8,128)} %param.11) | copy-start | bytes 196612
  12.5 0.8 %copy-start.4 = (f32[128,128]{1,0:T(8,128)S(1)}, f32[128,128]{1,0:T(8,128)}, u32[]{:S(2)}) copy-start(f32[128,128]{1,0:T(8,128)} %param.12) | copy-start | bytes 196612
  13.3 0.8 %copy-start.5 = (f32[128,128]{1,0:T(8,128)S(1)}, f32[128,128]{1,0:T(8,128)}, u32[]{:S(2)}) copy-start(f32[128,128]{1,0:T(8,128)} %param.13) | copy-start | bytes 196612
  14.4 10.3 %collective-permute-start.1 = (f32[304,128]{1,0:T(8,128)S(1)}, f32[304,128]{1,0:T(8,128)S(1)}, u32[]{:S(2)}, u32[]{:S(2)}) collective-permute-start(f32[304,128]{1,0:T(8,128)S(1)} %pad_maximum_fusion.1), channel_id=1, source_target_pairs={{0,1},{1,2},{2,3},{3,4},{4,5},{5,6},{6,7},{7,8},{8,9},{9,10},{10,1... | collective-permute-start | bytes 466952 | tf_op jit(solution)/shard_map/ppermute | solution.py:127
  16.3 9.2 %collective-permute-start.2 = (f32[304,128]{1,0:T(8,128)S(1)}, f32[304,128]{1,0:T(8,128)S(1)}, u32[]{:S(2)}, u32[]{:S(2)}) collective-permute-start(f32[304,128]{1,0:T(8,128)S(1)} %pad_maximum_fusion.2), channel_id=1, source_target_pairs={{0,15},{1,0},{2,1},{3,2},{4,3},{5,4},{6,5},{7,6},{8,7},{9,8},{10,9... | collective-permute-start | bytes 466952 | tf_op jit(solution)/shard_map/ppermute | solution.py:128
  24.7 0.7 %copy-start = (f32[304,128]{1,0:T(8,128)}, f32[304,128]{1,0:T(8,128)S(1)}, u32[]{:S(2)}) copy-start(f32[304,128]{1,0:T(8,128)S(1)} %collective-permute-done.1) | copy-start | bytes 466948
  25.5 0.9 %slice-start = ((f32[304,128]{1,0:T(8,128)}), f32[256,128]{1,0:T(8,128)S(1)}, s32[]{:S(2)}) async-start(f32[304,128]{1,0:T(8,128)} %copy-done), calls=%async_computation.1 | async-start | bytes 262144 | tf_op jit(solution)/shard_map/slice | solution.py:123
  30.3 0.7 %slice-start.1 = ((f32[304,128]{1,0:T(8,128)}), f32[48,128]{1,0:T(8,128)S(1)}, s32[]{:S(2)}) async-start(f32[304,128]{1,0:T(8,128)} %copy-done), calls=%async_computation.2 | async-start | bytes 49152 | tf_op jit(solution)/shard_map/slice | solution.py:124
  35.2 20.6 %all-to-all-start = ((f32[32,4,128]{2,1,0:T(4,128)}), f32[32,4,128]{2,1,0:T(4,128)S(1)}, u32[]{:S(2)}, u32[]{:S(2)}) async-start(f32[32,4,128]{2,1,0:T(4,128)} %bitcast.122), calls=%async_computation | async-start | bytes 131072 | tf_op jit(solution)/shard_map/all_to_all | solution.py:92
  46.4 10.0 %collective-permute-start.3 = (f32[3,128,128]{1,2,0:T(8,128)S(1)}, f32[3,128,128]{1,2,0:T(8,128)S(1)}, u32[]{:S(2)}, u32[]{:S(2)}) collective-permute-start(f32[3,128,128]{1,2,0:T(8,128)S(1)} %get-tuple-element.135), channel_id=1, source_target_pairs={{0,16},{16,32},{32,48},{48,64},{64,80},{80,96},{96,112},{112,128},... | collective-permute-start | bytes 589832 | tf_op jit(solution)/shard_map/ppermute | solution.py:25

commit v4 on v3

v4 whole, which is shorter than its diff:
```python
import math

import jax
import jax.numpy as jnp
from jax import lax
from jax.experimental import pallas as pl
from jax.experimental.pallas import tpu as pltpu
from jax.sharding import PartitionSpec as P

STEPS = 8


FLUX_RATE = 0.7
PRESS_RATE = 0.7
ROTATION_RATE = 0.15


def ring_pairs(count, steps):
    return [(source, (source + steps) % count) for source in range(count)]


def lane_dense(strip):
    return jnp.swapaxes(strip, -1, -2)


def from_behind(value, axis, steps):
    return lax.ppermute(value, axis, ring_pairs(lax.axis_size(axis), steps))


def coriolis(rows_count):
    latitude = math.pi * ((jnp.arange(rows_count, dtype=jnp.float32) + 0.5) / rows_count - 0.5)
    return (ROTATION_RATE * jnp.sin(latitude))[:, None]


def shooting_kernel(trig_ref, rot_ref, wide_ref, next_ref, defect_ref, pulled_ref, drag_ref, stored_ref):
    rows, lanes = wide_ref.shape[-2], wide_ref.shape[-1]
    tile = defect_ref.shape[-1]
    row = lax.broadcasted_iota(jnp.int32, (rows, lanes), 0)
    first, last = row == 0, row == rows - 1

    def across_cols(q):
        return 0.5 * (pltpu.roll(q, lanes - 1, 1) - pltpu.roll(q, 1, 1))

    def across_rows(q):
        upper = jnp.where(last, 0.0, pltpu.roll(q, rows - 1, 0))
        lower = jnp.where(first, 0.0, pltpu.roll(q, 1, 0))
        return 0.5 * (upper - lower)

    sea, depth, retain = wide_ref[3], wide_ref[4], wide_ref[5]
    rot = rot_ref[...]
    keep = sea * retain
    height, east, north = wide_ref[0] * sea, wide_ref[1] * sea, wide_ref[2] * sea
    for step in range(STEPS):
        force = trig_ref[step] * wide_ref[6] + trig_ref[STEPS + step] * wide_ref[7]
        spread = across_cols(depth * east) + across_rows(depth * north)
        height = sea * (height - FLUX_RATE * spread)
        surface = height + force
        east, north = (
            keep * (east - PRESS_RATE * across_cols(surface) + rot * north),
            keep * (north - PRESS_RATE * across_rows(surface) - rot * east),
        )
        stored_ref[step, 0] = east[:, :tile]
        stored_ref[step, 1] = north[:, :tile]
    height = sea * (height - next_ref[0])
    east = sea * (east - next_ref[1])
    north = sea * (north - next_ref[2])
    defect_ref[0] = height[:, :tile]
    defect_ref[1] = east[:, :tile]
    defect_ref[2] = north[:, :tile]
    depth_flux = FLUX_RATE * depth
    drag = jnp.zeros((rows, tile), jnp.float32)
    for back in range(STEPS):
        step = STEPS - 1 - back
        east_part = keep * east
        north_part = keep * north
        height = sea * (height + PRESS_RATE * (across_cols(east_part) + across_rows(north_part)))
        east = east_part - rot * north_part + depth_flux * across_cols(height)
        north = north_part + rot * east_part + depth_flux * across_rows(height)
        drag = drag - (
            east_part[:, :tile] * stored_ref[step, 0] + north_part[:, :tile] * stored_ref[step, 1]
        )
    sea_tile = sea[:, :tile]
    pulled_ref[0] = sea_tile * height[:, :tile]
    pulled_ref[1] = sea_tile * east[:, :tile]
    pulled_ref[2] = sea_tile * north[:, :tile]
    drag_ref[...] = drag


def shooting(trig, rotation, wide, following, tile):
    rows, lanes = wide.shape[-2], wide.shape[-1]
    vmem = pl.BlockSpec(memory_space=pltpu.VMEM)
    state = jax.ShapeDtypeStruct((3, rows, tile), jnp.float32)
    return pl.pallas_call(
        shooting_kernel,
        out_shape=(state, state, jax.ShapeDtypeStruct((rows, tile), jnp.float32)),
        in_specs=[pl.BlockSpec(memory_space=pltpu.SMEM), vmem, vmem, vmem],
        out_specs=(vmem, vmem, vmem),
        scratch_shapes=[pltpu.VMEM((STEPS, 2, rows, tile), jnp.float32)],
        cost_estimate=pl.CostEstimate(
            flops=2 * STEPS * 60 * rows * lanes, transcendentals=0, bytes_accessed=4 * rows * (11 * lanes + 7 * tile)
        ),
    )(trig, rotation, wide, following)


def reduce_scatter_rows(value, axis):
    count = lax.axis_size(axis)
    pieces = value.reshape((count, value.shape[0] // count, value.shape[1]))
    return jnp.sum(lax.all_to_all(pieces, axis, 0, 0, tiled=True), axis=0)


def local(start_states, ocean_mask, depth_class, class_depth, drag_rate, tide_cos, tide_sin):
    halo = 2 * STEPS
    slice_count = lax.axis_size("tm")
    slice_index = lax.axis_index("tm")
    sea_mask = ocean_mask.astype(jnp.float32)
    classes = jnp.arange(class_depth.shape[0], dtype=jnp.int32)
    depth_field = jnp.sum(
        jnp.where(depth_class[None] == classes[:, None, None], class_depth[:, None, None], 0.0),
        axis=0,
    )
    retain = 1.0 / (1.0 + drag_rate)
    initial = start_states[0]
    cells = lax.axis_size("cell")
    own = jnp.concatenate(
        [initial, jnp.stack([sea_mask, depth_field, retain, tide_cos, tide_sin])], axis=0
    )
    fields, rows, width = own.shape
    following = from_behind(initial, "tm", -1)

    def strips(at_right):
        mine = own[..., width - 2 * halo :] if at_right else own[..., : 2 * halo]
        theirs = following[..., width - halo :] if at_right else following[..., :halo]
        return jnp.concatenate(
            [lane_dense(mine).reshape(-1, rows), lane_dense(theirs).reshape(-1, rows)], axis=0
        )

    def unpacked(packed):
        mine = lane_dense(packed[: fields * 2 * halo].reshape(fields, 2 * halo, rows))
        theirs = lane_dense(packed[fields * 2 * halo :].reshape(3, halo, rows))
        return mine, theirs

    left_own, left_next = unpacked(lax.ppermute(strips(True), "cell", ring_pairs(cells, 1)))
    right_own, right_next = unpacked(lax.ppermute(strips(False), "cell", ring_pairs(cells, -1)))
    lanes = 2 * width

    def circular(middle, right, left):
        gap = jnp.zeros(middle.shape[:-1] + (lanes - width - right.shape[-1] - left.shape[-1],), middle.dtype)
        return jnp.concatenate([middle, right, gap, left], axis=-1)

    phase_unit = 2.0 * math.pi / (slice_count * STEPS)
    phases = (slice_index * STEPS + jnp.arange(STEPS)).astype(jnp.float32) * phase_unit
    trig = jnp.concatenate([jnp.cos(phases), jnp.sin(phases)])
    defect, pulled, drag_total = shooting(
        trig,
        coriolis(rows),
        circular(own, right_own, left_own),
        circular(following, right_next, left_next),
        width,
    )
    behind = from_behind(defect, "tm", 1)
    state_grad = pulled - behind
    drag_grad = reduce_scatter_rows(drag_total, "tm") / slice_count
    return (defect[None], state_grad[None], drag_grad)


def solution(mesh):
    return jax.shard_map(
        local,
        mesh=mesh,
        in_specs=(
            P("tm", None, None, "cell"),
            P(None, "cell"),
            P(None, "cell"),
            P(),
            P(None, "cell"),
            P(None, "cell"),
            P(None, "cell"),
        ),
        out_specs=(P("tm", None, None, "cell"), P("tm", None, None, "cell"), P("tm", "cell")),
        check_vma=False,
    )
```

time: 57.8 us -> 62.2 us (1.076)
  Pallas kernels: 0 us -> 6.88 us
  local copies, waits for them, and re-layouts: 12 us -> 5.91 us
  waiting for transfers between devices: 5.12 us -> 10.4 us
  between operations: 2.62 us -> 0.85 us
    pallas_call x0 -> x1, Pallas kernels: none -> 6.88 us  [shooting(): pl.pallas_call(shooting_kernel, out_shape=(state, state, jax.ShapeDtypeSt...]
    ppermute x1, waiting for transfers between devices: 0.01 us -> 4.4 us  [local(): lax.ppermute(strips(True), 'cell', ring_pairs(cells, 1))]
    slice x42 -> x4, local copies, waits for them, and re-layouts: 4.32 us -> 0.03 us  [the longest x2 0.02 us: unpacked(): packed[:fields * 2 * halo].reshape(fields, 2 * halo, rows)]
    concatenate x3 -> x5, other arithmetic: 0.08 us -> 2.74 us  [the longest x2 2.09 us: circular(): return jnp.concatenate([middle, right, gap, left], axis=-1)]
    mul x26 -> x0, other arithmetic: 2.57 us -> none  [the longest x8 0.85 us: adjoint_step(): height_part = cropped(sea_mask, 1) * summed]
    unnamed x24 -> x17, local copies, waits for them, and re-layouts: 6.68 us -> 4.24 us
    all_to_all x1, waiting for transfers between devices: 4.95 us -> 6.03 us  [reduce_scatter_rows(): return jnp.sum(lax.all_to_all(pieces, axis, 0, 0, tiled=True), axis=0)]
    add x8 -> x0, other arithmetic: 0.92 us -> none  [advance_wide(): height_new + cropped(cosine * statics[3] + sine_now * statics[4], 1)]
  transfers between devices with their start and end apart: 5 -> 5, of which waited for: 2 -> 2; matrix products, arithmetic and copies ran while one was open for 4% -> 7% of each run, Pallas kernels for 0% -> 0%
where the time goes in v4:
time: 62.2 us; the launch traced here: 61.7 us
  starting transfers between devices  32.5 us (52%)
  waiting for transfers between devices  10.4 us (17%)
  Pallas kernels  6.88 us (11%)
  local copies, waits for them, and re-layouts  5.91 us (10%)
  other arithmetic  5.12 us (8%)
  between operations  0.85 us (1%)
    ppermute x2, starting transfers between devices, from_behind(): return lax.ppermute(value, axis, ring_pairs(lax.axis_size(axis), steps))  12.5 us
    all_to_all x1, starting transfers between devices, reduce_scatter_rows(): return jnp.sum(lax.all_to_all(pieces, axis, 0, 0, tiled=True), axis=0)  11.9 us
    pallas_call x1, Pallas kernels, shooting(): pl.pallas_call(shooting_kernel, out_shape=(state, state, jax.ShapeDtypeSt...  6.88 us
    ppermute x1, starting transfers between devices, local(): lax.ppermute(strips(False), 'cell', ring_pairs(cells, -1))  6.22 us
    all_to_all x1, waiting for transfers between devices, reduce_scatter_rows(): return jnp.sum(lax.all_to_all(pieces, axis, 0, 0, tiled=True), axis=0)  6.03 us
    ppermute x1, waiting for transfers between devices, local(): lax.ppermute(strips(True), 'cell', ring_pairs(cells, 1))  4.4 us
    unnamed x17, local copies, waits for them, and re-layouts  4.24 us
    concatenate x2, other arithmetic, circular(): return jnp.concatenate([middle, right, gap, left], axis=-1)  2.09 us
  transfers between devices with their start and end apart: 5, of which 2 were waited for; matrix products, arithmetic and copies ran while one was open for 7% of the time, Pallas kernels for 0%

profile of v4, /device:TPU:1, one launch (start us, length us, event | category | flops | bytes accessed | tf_op | source)
XLA Modules:
  0.0 61.7 jit_solution(14166495257486484034)
XLA Ops:
  0.6 0.0 copy-start.1
  0.6 8.9 %collective-permute-start = (f32[3,128,128]{2,1,0:T(8,128)}, f32[3,128,128]{2,1,0:T(8,128)S(1)}, u32[]{:S(2)}, u32[]{:S(2)}) collective-permute-start(f32[3,128,128]{2,1,0:T(8,128)} %bitcast.44), channel_id=1, source_target_pairs={{0,496},{16,0},{32,16},{48,32},{64,48},{80,64},{96,80},{112,96},{1... | collective-permute-start | bytes 589832 | tf_op jit(solution)/shard_map/ppermute | solution.py:27
  9.6 0.9 %constant_dynamic-update-slice_fusion = f32[8,128,128]{2,1,0:T(8,128)S(1)} fusion(f32[1,3,128,128]{3,2,1,0:T(8,128)} %param.7), kind=kLoop, calls=%fused_computation.17 | loop fusion | bytes 393216
  10.5 0.0 copy-done.1
  10.5 0.0 copy-start.2
  10.5 0.0 copy-start.6
  10.6 0.8 %copy-done.2 = s32[128,128]{1,0:T(8,128)S(1)} copy-done((s32[128,128]{1,0:T(8,128)S(1)}, s32[128,128]{1,0:T(8,128)}, u32[]{:S(2)}) %copy-start.2) | copy-done | bytes 65560
  11.4 0.0 copy-done.6
  11.4 0.1 select_reduce_fusion
  11.5 0.0 copy-start.3
  11.5 0.8 %copy-done.3 = f32[128,128]{1,0:T(8,128)S(1)} copy-done((f32[128,128]{1,0:T(8,128)S(1)}, f32[128,128]{1,0:T(8,128)}, u32[]{:S(2)}) %copy-start.3) | copy-done | bytes 65560
  12.3 0.0 copy-start.4
  12.3 0.8 %copy-done.4 = f32[128,128]{1,0:T(8,128)S(1)} copy-done((f32[128,128]{1,0:T(8,128)S(1)}, f32[128,128]{1,0:T(8,128)}, u32[]{:S(2)}) %copy-start.4) | copy-done | bytes 65560
  13.2 0.0 copy-start.5
  13.2 0.8 %copy-done.5 = f32[128,128]{1,0:T(8,128)S(1)} copy-done((f32[128,128]{1,0:T(8,128)S(1)}, f32[128,128]{1,0:T(8,128)}, u32[]{:S(2)}) %copy-start.5) | copy-done | bytes 65560
  14.0 0.2 slice_bitcast_fusion.1
  14.2 0.2 copy.27
  14.4 0.2 copy.30
  14.6 0.0 collective-permute-done
  14.6 0.1 slice_bitcast_fusion.3
  14.7 0.1 copy.28
  14.9 6.2 %collective-permute-start.1 = (f32[304,128]{1,0:T(8,128)S(1)}, f32[304,128]{1,0:T(8,128)S(1)}, u32[]{:S(2)}, u32[]{:S(2)}) collective-permute-start(f32[304,128]{1,0:T(8,128)S(1)} %pad_maximum_fusion.2), channel_id=1, source_target_pairs={{0,15},{1,0},{2,1},{3,2},{4,3},{5,4},{6,5},{7,6},{8,7},{9,8},{10,9... | collective-permute-start | bytes 466952 | tf_op jit(solution)/shard_map/ppermute | solution.py:143
  21.1 0.1 copy.31
  21.2 1.9 %collective-permute-start.2 = (f32[304,128]{1,0:T(8,128)S(1)}, f32[304,128]{1,0:T(8,128)S(1)}, u32[]{:S(2)}, u32[]{:S(2)}) collective-permute-start(f32[304,128]{1,0:T(8,128)S(1)} %pad_maximum_fusion.3), channel_id=1, source_target_pairs={{0,1},{1,2},{2,3},{3,4},{4,5},{5,6},{6,7},{7,8},{8,9},{9,10},{10,1... | collective-permute-start | bytes 466952 | tf_op jit(solution)/shard_map/ppermute | solution.py:142
  23.2 0.6 pad_maximum_fusion.4.trig_ref
  23.7 0.1 pad.2.clone
  23.8 0.1 pad.6.clone
  23.9 0.9 %sine_multiply_fusion.rot_ref = f32[128,1]{1,0:T(8,128)} fusion(), kind=kLoop, calls=%fused_computation.16 | loop fusion | flops 640 | bytes 512 | tf_op jit(solution)/shard_map/mul | solution.py:32
  24.8 0.0 collective-permute-done.1
  24.8 0.1 copy.33
  24.9 4.4 %collective-permute-done.2 = f32[304,128]{1,0:T(8,128)S(1)} collective-permute-done((f32[304,128]{1,0:T(8,128)S(1)}, f32[304,128]{1,0:T(8,128)S(1)}, u32[]{:S(2)}, u32[]{:S(2)}) %collective-permute-start.2) | collective-permute-done | bytes 155680 | tf_op jit(solution)/shard_map/ppermute | solution.py:142
  29.3 0.1 copy.34
  29.5 0.2 copy.29
  29.7 0.2 copy.32
  29.9 1.2 %pad_maximum_fusion.wide_ref = f32[8,128,256]{2,1,0:T(8,128)} fusion(f32[8,128,32]{2,1,0:T(8,128)S(1)} %bitcast.37, f32[8,128,32]{2,1,0:T(8,128)S(1)} %bitcast.36, f32[8,128,128]{2,1,0:T(8,128)S(1)} %bitcast_dynamic-update-slice_fusion, f32[256]{0:T(256)S(1)} %pad.6.clone), kind=kLoop, calls=%fused_computation | loop fusion | flops 786432 | bytes 1836032 | tf_op jit(solution)/shard_map/concatenate | solution.py:148
  31.1 0.9 %pad_maximum_fusion.1.next_ref = f32[3,128,256]{2,1,0:T(8,128)} fusion(f32[3,128,16]{2,1,0:T(8,128)S(1)} %bitcast.39, f32[3,128,16]{2,1,0:T(8,128)S(1)} %bitcast.38, f32[3,128,128]{2,1,0:T(8,128)S(1)} %collective-permute-done, f32[256]{0:T(256)S(1)} %pad.2.clone), kind=kLoop, calls=%fused_computation.5 | loop fusion | flops 294912 | bytes 640000 | tf_op jit(solution)/shard_map/concatenate | solution.py:148
  32.0 6.9 %shard_map.94 = (f32[3,128,128]{2,1,0:T(8,128)}, f32[3,128,128]{2,1,0:T(8,128)}, f32[128,128]{1,0:T(8,128)}) custom-call(f32[16]{0:T(128)} %pad_maximum_fusion.4.trig_ref, f32[128,1]{1,0:T(8,128)} %sine_multiply_fusion.rot_ref, f32[8,128,256]{2,1,0:T(8,128)} %pad_maximum_fusion.wide_ref, f32[3,128,256]{2,1,0:T(8,128)} %pad_maximum_fusion.1.next_ref), custom_call_target="tpu_custom_call" | custom-call | flops 31457280 | bytes 1900544 | tf_op jit(solution)/shard_map/pallas_call | solution.py:93
  38.9 0.0 copy-start
  38.9 11.9 %all-to-all-start = ((f32[32,4,128]{2,1,0:T(4,128)}), f32[32,4,128]{2,1,0:T(4,128)S(1)}, u32[]{:S(2)}, u32[]{:S(2)}) async-start(f32[32,4,128]{2,1,0:T(4,128)} %bitcast.49), calls=%async_computation | async-start | bytes 131072 | tf_op jit(solution)/shard_map/all_to_all | solution.py:108
  50.8 3.5 %collective-permute-start.3 = (f32[3,128,128]{2,1,0:T(8,128)}, f32[3,128,128]{2,1,0:T(8,128)S(1)}, u32[]{:S(2)}, u32[]{:S(2)}) collective-permute-start(f32[3,128,128]{2,1,0:T(8,128)} %get-tuple-element.6), channel_id=1, source_target_pairs={{0,16},{16,32},{32,48},{48,64},{64,80},{80,96},{96,112},{112,128},... | collective-permute-start | bytes 589832 | tf_op jit(solution)/shard_map/ppermute | solution.py:27
  54.3 6.0 %all-to-all-done = f32[32,4,128]{2,1,0:T(4,128)S(1)} async-done(((f32[32,4,128]{2,1,0:T(4,128)}), f32[32,4,128]{2,1,0:T(4,128)S(1)}, u32[]{:S(2)}, u32[]{:S(2)}) %all-to-all-start) | async-done | bytes 65568 | tf_op jit(solution)/shard_map/all_to_all | solution.py:108
  60.4 0.6 broadcast_multiply_fusion
  61.0 0.0 collective-permute-done.3
  61.0 0.0 copy-done
  61.0 0.7 %subtract_bitcast_fusion = f32[1,3,128,128]{3,2,1,0:T(8,128)} fusion(f32[3,128,128]{2,1,0:T(8,128)S(1)} %copy-done, f32[3,128,128]{2,1,0:T(8,128)S(1)} %collective-permute-done.3), kind=kLoop, calls=%fused_computation.8 | loop fusion | flops 49152 | bytes 589824 | tf_op jit(solution)/shard_map/broadcast_in_dim | solution.py:163
  (15 shorter events, 0.2 us)
Async XLA Ops:
  0.6 9.9 %copy-start.1 = (s32[128,128]{1,0:T(8,128)S(1)}, s32[128,128]{1,0:T(8,128)}, u32[]{:S(2)}) copy-start(s32[128,128]{1,0:T(8,128)} %param.8) | copy-start | bytes 196612
  0.6 14.0 %collective-permute-start = (f32[3,128,128]{2,1,0:T(8,128)}, f32[3,128,128]{2,1,0:T(8,128)S(1)}, u32[]{:S(2)}, u32[]{:S(2)}) collective-permute-start(f32[3,128,128]{2,1,0:T(8,128)} %bitcast.44), channel_id=1, source_target_pairs={{0,496},{16,0},{32,16},{48,32},{64,48},{80,64},{96,80},{112,96},{1... | collective-permute-start | bytes 589832 | tf_op jit(solution)/shard_map/ppermute | solution.py:27
  10.5 0.8 %copy-start.2 = (s32[128,128]{1,0:T(8,128)S(1)}, s32[128,128]{1,0:T(8,128)}, u32[]{:S(2)}) copy-start(s32[128,128]{1,0:T(8,128)} %param.9) | copy-start | bytes 196612
  10.5 0.8 %copy-start.6 = (f32[8]{0:T(128)S(1)}, f32[8]{0:T(128)}, u32[]{:S(2)}) copy-start(f32[8]{0:T(128)} %param.10) | copy-start | bytes 100
  11.5 0.8 %copy-start.3 = (f32[128,128]{1,0:T(8,128)S(1)}, f32[128,128]{1,0:T(8,128)}, u32[]{:S(2)}) copy-start(f32[128,128]{1,0:T(8,128)} %param.11) | copy-start | bytes 196612
  12.3 0.8 %copy-start.4 = (f32[128,128]{1,0:T(8,128)S(1)}, f32[128,128]{1,0:T(8,128)}, u32[]{:S(2)}) copy-start(f32[128,128]{1,0:T(8,128)} %param.12) | copy-start | bytes 196612
  13.2 0.8 %copy-start.5 = (f32[128,128]{1,0:T(8,128)S(1)}, f32[128,128]{1,0:T(8,128)}, u32[]{:S(2)}) copy-start(f32[128,128]{1,0:T(8,128)} %param.13) | copy-start | bytes 196612
  14.9 9.9 %collective-permute-start.1 = (f32[304,128]{1,0:T(8,128)S(1)}, f32[304,128]{1,0:T(8,128)S(1)}, u32[]{:S(2)}, u32[]{:S(2)}) collective-permute-start(f32[304,128]{1,0:T(8,128)S(1)} %pad_maximum_fusion.2), channel_id=1, source_target_pairs={{0,15},{1,0},{2,1},{3,2},{4,3},{5,4},{6,5},{7,6},{8,7},{9,8},{10,9... | collective-permute-start | bytes 466952 | tf_op jit(solution)/shard_map/ppermute | solution.py:143
  21.2 8.1 %collective-permute-start.2 = (f32[304,128]{1,0:T(8,128)S(1)}, f32[304,128]{1,0:T(8,128)S(1)}, u32[]{:S(2)}, u32[]{:S(2)}) collective-permute-start(f32[304,128]{1,0:T(8,128)S(1)} %pad_maximum_fusion.3), channel_id=1, source_target_pairs={{0,1},{1,2},{2,3},{3,4},{4,5},{5,6},{6,7},{7,8},{8,9},{9,10},{10,1... | collective-permute-start | bytes 466952 | tf_op jit(solution)/shard_map/ppermute | solution.py:142
  38.9 22.1 %copy-start = (f32[3,128,128]{2,1,0:T(8,128)S(1)}, f32[3,128,128]{2,1,0:T(8,128)}, u32[]{:S(2)}) copy-start(f32[3,128,128]{2,1,0:T(8,128)} %get-tuple-element.7) | copy-start | bytes 589828
  38.9 21.5 %all-to-all-start = ((f32[32,4,128]{2,1,0:T(4,128)}), f32[32,4,128]{2,1,0:T(4,128)S(1)}, u32[]{:S(2)}, u32[]{:S(2)}) async-start(f32[32,4,128]{2,1,0:T(4,128)} %bitcast.49), calls=%async_computation | async-start | bytes 131072 | tf_op jit(solution)/shard_map/all_to_all | solution.py:108
  50.8 10.2 %collective-permute-start.3 = (f32[3,128,128]{2,1,0:T(8,128)}, f32[3,128,128]{2,1,0:T(8,128)S(1)}, u32[]{:S(2)}, u32[]{:S(2)}) collective-permute-start(f32[3,128,128]{2,1,0:T(8,128)} %get-tuple-element.6), channel_id=1, source_target_pairs={{0,16},{16,32},{32,48},{48,64},{64,80},{80,96},{96,112},{112,128},... | collective-permute-start | bytes 589832 | tf_op jit(solution)/shard_map/ppermute | solution.py:27

commit v5 on v4

--- a/solution.py
+++ b/solution.py
@@ -1,3 +1,4 @@
+import functools
 import math
 
 import jax
@@ -32,12 +33,29 @@
     return (ROTATION_RATE * jnp.sin(latitude))[:, None]
 
 
-def shooting_kernel(trig_ref, rot_ref, wide_ref, next_ref, defect_ref, pulled_ref, drag_ref, stored_ref):
-    rows, lanes = wide_ref.shape[-2], wide_ref.shape[-1]
-    tile = defect_ref.shape[-1]
+def shooting_kernel(
+    trig_ref, rot_ref, own_ref, next_ref, left_ref, right_ref,
+    defect_ref, pulled_ref, drag_ref, wide_ref, ahead_ref, stored_ref, *, halo, scale
+):
+    rows, tile = own_ref.shape[-2], own_ref.shape[-1]
+    lanes = wide_ref.shape[-1]
+
+    def circular(middle, right, left):
+        gap = jnp.zeros((tile - right.shape[0] - left.shape[0], rows), jnp.float32)
+        rim = jnp.transpose(jnp.concatenate([right, gap, left], axis=0))
+        return jnp.concatenate([middle, rim], axis=1)
+
+    fields = own_ref.shape[0]
+    wide = 2 * halo
+    for field in range(fields):
+        strip = slice(field * wide, (field + 1) * wide)
+        wide_ref[field] = circular(own_ref[field], right_ref[strip, :], left_ref[strip, :])
+    for field in range(next_ref.shape[0]):
+        strip = slice(fields * wide + field * halo, fields * wide + (field + 1) * halo)
+        ahead_ref[field] = circular(next_ref[field], right_ref[strip, :], left_ref[strip, :])
+
     row = lax.broadcasted_iota(jnp.int32, (rows, lanes), 0)
     first, last = row == 0, row == rows - 1
-
     def across_cols(q):
         return 0.5 * (pltpu.roll(q, lanes - 1, 1) - pltpu.roll(q, 1, 1))
 
@@ -61,9 +79,9 @@
         )
         stored_ref[step, 0] = east[:, :tile]
         stored_ref[step, 1] = north[:, :tile]
-    height = sea * (height - next_ref[0])
-    east = sea * (east - next_ref[1])
-    north = sea * (north - next_ref[2])
+    height = sea * (height - ahead_ref[0])
+    east = sea * (east - ahead_ref[1])
+    north = sea * (north - ahead_ref[2])
     defect_ref[0] = height[:, :tile]
     defect_ref[1] = east[:, :tile]
     defect_ref[2] = north[:, :tile]
@@ -83,23 +101,28 @@
     pulled_ref[0] = sea_tile * height[:, :tile]
     pulled_ref[1] = sea_tile * east[:, :tile]
     pulled_ref[2] = sea_tile * north[:, :tile]
-    drag_ref[...] = drag
+    drag_ref[...] = drag * scale
 
 
-def shooting(trig, rotation, wide, following, tile):
-    rows, lanes = wide.shape[-2], wide.shape[-1]
+def shooting(trig, rotation, own, following, from_left, from_right, halo, scale):
+    fields, rows, tile = own.shape
     vmem = pl.BlockSpec(memory_space=pltpu.VMEM)
     state = jax.ShapeDtypeStruct((3, rows, tile), jnp.float32)
+    lanes = 2 * tile
     return pl.pallas_call(
-        shooting_kernel,
+        functools.partial(shooting_kernel, halo=halo, scale=scale),
         out_shape=(state, state, jax.ShapeDtypeStruct((rows, tile), jnp.float32)),
-        in_specs=[pl.BlockSpec(memory_space=pltpu.SMEM), vmem, vmem, vmem],
+        in_specs=[pl.BlockSpec(memory_space=pltpu.SMEM)] + [vmem] * 5,
         out_specs=(vmem, vmem, vmem),
-        scratch_shapes=[pltpu.VMEM((STEPS, 2, rows, tile), jnp.float32)],
+        scratch_shapes=[
+            pltpu.VMEM((fields, rows, lanes), jnp.float32),
+            pltpu.VMEM((3, rows, lanes), jnp.float32),
+            pltpu.VMEM((STEPS, 2, rows, tile), jnp.float32),
+        ],
         cost_estimate=pl.CostEstimate(
-            flops=2 * STEPS * 60 * rows * lanes, transcendentals=0, bytes_accessed=4 * rows * (11 * lanes + 7 * tile)
+            flops=2 * STEPS * 60 * rows * lanes, transcendentals=0, bytes_accessed=4 * rows * 24 * tile
         ),
-    )(trig, rotation, wide, following)
+    )(trig, rotation, own, following, from_left, from_right)
 
 
 def reduce_scatter_rows(value, axis):
@@ -134,32 +157,17 @@
             [lane_dense(mine).reshape(-1, rows), lane_dense(theirs).reshape(-1, rows)], axis=0
         )
 
-    def unpacked(packed):
-        mine = lane_dense(packed[: fields * 2 * halo].reshape(fields, 2 * halo, rows))
-        theirs = lane_dense(packed[fields * 2 * halo :].reshape(3, halo, rows))
-        return mine, theirs
-
-    left_own, left_next = unpacked(lax.ppermute(strips(True), "cell", ring_pairs(cells, 1)))
-    right_own, right_next = unpacked(lax.ppermute(strips(False), "cell", ring_pairs(cells, -1)))
-    lanes = 2 * width
-
-    def circular(middle, right, left):
-        gap = jnp.zeros(middle.shape[:-1] + (lanes - width - right.shape[-1] - left.shape[-1],), middle.dtype)
-        return jnp.concatenate([middle, right, gap, left], axis=-1)
-
+    from_left = lax.ppermute(strips(True), "cell", ring_pairs(cells, 1))
+    from_right = lax.ppermute(strips(False), "cell", ring_pairs(cells, -1))
     phase_unit = 2.0 * math.pi / (slice_count * STEPS)
     phases = (slice_index * STEPS + jnp.arange(STEPS)).astype(jnp.float32) * phase_unit
     trig = jnp.concatenate([jnp.cos(phases), jnp.sin(phases)])
-    defect, pulled, drag_total = shooting(
-        trig,
-        coriolis(rows),
-        circular(own, right_own, left_own),
-        circular(following, right_next, left_next),
-        width,
+    defect, pulled, drag_grad = shooting(
+        trig, coriolis(rows), own, following, from_left, from_right, halo, 1.0 / slice_count
     )
     behind = from_behind(defect, "tm", 1)
     state_grad = pulled - behind
-    drag_grad = reduce_scatter_rows(drag_total, "tm") / slice_count
+    drag_grad = reduce_scatter_rows(drag_grad, "tm")
     return (defect[None], state_grad[None], drag_grad)
 
 

time: 62.2 us -> 59.1 us (0.950)
  blocking collectives: 0 us -> 18.5 us
  starting transfers between devices: 32.5 us -> 22.1 us
  waiting for transfers between devices: 10.4 us -> 0.93 us
  other arithmetic: 5.12 us -> 3.04 us
  local copies, waits for them, and re-layouts: 5.91 us -> 6.88 us
    all_to_all x0 -> x1, blocking collectives: none -> 18.5 us  [reduce_scatter_rows(): return jnp.sum(lax.all_to_all(pieces, axis, 0, 0, tiled=True), axis=0)]
    all_to_all x1 -> x0, starting transfers between devices: 11.9 us -> none  [reduce_scatter_rows(): return jnp.sum(lax.all_to_all(pieces, axis, 0, 0, tiled=True), axis=0)]
    all_to_all x1 -> x0, waiting for transfers between devices: 6.03 us -> none  [reduce_scatter_rows(): return jnp.sum(lax.all_to_all(pieces, axis, 0, 0, tiled=True), axis=0)]
    ppermute x2, waiting for transfers between devices: 4.4 us -> 0.93 us  [the longest x1 0.92 us: local(): from_right = lax.ppermute(strips(False), 'cell', ring_pairs(cells, -1))]
    concatenate x2 -> x0, other arithmetic: 2.09 us -> none  [circular(): return jnp.concatenate([middle, right, gap, left], axis=-1)]
    unnamed x17 -> x25, local copies, waits for them, and re-layouts: 4.24 us -> 6.05 us
    ppermute x2, starting transfers between devices: 12.5 us -> 13.9 us  [from_behind(): return lax.ppermute(value, axis, ring_pairs(lax.axis_size(axis), steps))]
    reshape x4 -> x0, local copies, waits for them, and re-layouts: 0.65 us -> none  [the longest x2 0.4 us: unpacked(): packed[:fields * 2 * halo].reshape(fields, 2 * halo, rows)]
  transfers between devices with their start and end apart: 5 -> 4, of which waited for: 2 -> 1; matrix products, arithmetic and copies ran while one was open for 7% -> 7% of each run, Pallas kernels for 0% -> 0%
where the time goes in v5:
time: 59.1 us; the launch traced here: 58.6 us
  starting transfers between devices  22.1 us (37%)
  blocking collectives  18.5 us (31%)
  local copies, waits for them, and re-layouts  6.88 us (12%)
  Pallas kernels  6.4 us (11%)
  other arithmetic  3.04 us (5%)
  waiting for transfers between devices  0.93 us (2%)
  between operations  0.8 us (1%)
    all_to_all x1, blocking collectives, reduce_scatter_rows(): return jnp.sum(lax.all_to_all(pieces, axis, 0, 0, tiled=True), axis=0)  18.5 us
    ppermute x2, starting transfers between devices, from_behind(): return lax.ppermute(value, axis, ring_pairs(lax.axis_size(axis), steps))  13.9 us
    pallas_call x1, Pallas kernels, shooting(): pl.pallas_call(functools.partial(shooting_kernel, halo=halo, scale=scale)...  6.4 us
    ppermute x1, starting transfers between devices, local(): from_right = lax.ppermute(strips(False), 'cell', ring_pairs(cells, -1))  6.22 us
    unnamed x25, local copies, waits for them, and re-layouts  6.05 us
    ppermute x1, starting transfers between devices, local(): from_left = lax.ppermute(strips(True), 'cell', ring_pairs(cells, 1))  1.92 us
  transfers between devices with their start and end apart: 4, of which 1 were waited for; matrix products, arithmetic and copies ran while one was open for 7% of the time, Pallas kernels for 0%

profile of v5, /device:TPU:1, one launch (start us, length us, event | category | flops | bytes accessed | tf_op | source)
XLA Modules:
  0.0 58.6 jit_solution(5230395731764561802)
XLA Ops:
  0.6 0.0 copy-start.5
  0.6 8.9 %collective-permute-start = (f32[3,128,128]{2,1,0:T(8,128)}, f32[3,128,128]{2,1,0:T(8,128)S(1)}, u32[]{:S(2)}, u32[]{:S(2)}) collective-permute-start(f32[3,128,128]{2,1,0:T(8,128)} %bitcast.30), channel_id=1, source_target_pairs={{0,496},{16,0},{32,16},{48,32},{64,48},{80,64},{96,80},{112,96},{1... | collective-permute-start | bytes 589832 | tf_op jit(solution)/shard_map/ppermute | solution.py:28
  9.6 0.9 %constant_dynamic-update-slice_fusion = f32[8,128,128]{2,1,0:T(8,128)S(1)} fusion(f32[1,3,128,128]{3,2,1,0:T(8,128)} %param.7), kind=kLoop, calls=%fused_computation.15 | loop fusion | bytes 393216
  10.5 0.0 copy-done.5
  10.5 0.0 copy-start.6
  10.5 0.0 copy-start.10
  10.6 0.8 %copy-done.6 = s32[128,128]{1,0:T(8,128)S(1)} copy-done((s32[128,128]{1,0:T(8,128)S(1)}, s32[128,128]{1,0:T(8,128)}, u32[]{:S(2)}) %copy-start.6) | copy-done | bytes 65560
  11.4 0.0 copy-done.10
  11.4 0.1 select_reduce_fusion
  11.5 0.0 copy-start.7
  11.5 0.8 %copy-done.7 = f32[128,128]{1,0:T(8,128)S(1)} copy-done((f32[128,128]{1,0:T(8,128)S(1)}, f32[128,128]{1,0:T(8,128)}, u32[]{:S(2)}) %copy-start.7) | copy-done | bytes 65560
  12.3 0.0 copy-start.8
  12.3 0.8 %copy-done.8 = f32[128,128]{1,0:T(8,128)S(1)} copy-done((f32[128,128]{1,0:T(8,128)S(1)}, f32[128,128]{1,0:T(8,128)}, u32[]{:S(2)}) %copy-start.8) | copy-done | bytes 65560
  13.2 0.0 copy-start.9
  13.2 0.8 %copy-done.9 = f32[128,128]{1,0:T(8,128)S(1)} copy-done((f32[128,128]{1,0:T(8,128)S(1)}, f32[128,128]{1,0:T(8,128)}, u32[]{:S(2)}) %copy-start.9) | copy-done | bytes 65560
  14.0 0.0 copy-start
  14.0 0.2 slice_bitcast_fusion
  14.2 0.6 %copy-done = f32[8,128,128]{2,1,0:T(8,128)} copy-done((f32[8,128,128]{2,1,0:T(8,128)}, f32[8,128,128]{2,1,0:T(8,128)S(1)}, u32[]{:S(2)}) %copy-start) | copy-done | bytes 524312
  14.8 0.2 copy.19
  15.0 0.2 copy.21
  15.2 0.0 collective-permute-done.next_ref
  15.2 0.0 copy-start.1
  15.2 0.1 slice_bitcast_fusion.2
  15.3 0.6 copy-done.1
  15.9 0.1 copy.20
  16.0 1.9 %collective-permute-start.1 = (f32[304,128]{1,0:T(8,128)S(1)}, f32[304,128]{1,0:T(8,128)S(1)}, u32[]{:S(2)}, u32[]{:S(2)}) collective-permute-start(f32[304,128]{1,0:T(8,128)S(1)} %pad_maximum_fusion), channel_id=1, source_target_pairs={{0,1},{1,2},{2,3},{3,4},{4,5},{5,6},{6,7},{7,8},{8,9},{9,10},{10,1... | collective-permute-start | bytes 466952 | tf_op jit(solution)/shard_map/ppermute | solution.py:160
  17.9 0.1 copy.22
  18.1 6.2 %collective-permute-start.2 = (f32[304,128]{1,0:T(8,128)S(1)}, f32[304,128]{1,0:T(8,128)S(1)}, u32[]{:S(2)}, u32[]{:S(2)}) collective-permute-start(f32[304,128]{1,0:T(8,128)S(1)} %pad_maximum_fusion.1), channel_id=1, source_target_pairs={{0,15},{1,0},{2,1},{3,2},{4,3},{5,4},{6,5},{7,6},{8,7},{9,8},{10,9... | collective-permute-start | bytes 466952 | tf_op jit(solution)/shard_map/ppermute | solution.py:161
  24.3 0.6 pad_maximum_fusion.2.trig_ref
  24.9 0.9 %sine_multiply_fusion.rot_ref = f32[128,1]{1,0:T(8,128)} fusion(), kind=kLoop, calls=%fused_computation.14 | loop fusion | flops 640 | bytes 512 | tf_op jit(solution)/shard_map/mul | solution.py:33
  25.8 0.0 collective-permute-done.1.left_ref
  25.8 0.0 copy-start.3
  25.8 0.9 %collective-permute-done.2.right_ref = f32[304,128]{1,0:T(8,128)S(1)} collective-permute-done((f32[304,128]{1,0:T(8,128)S(1)}, f32[304,128]{1,0:T(8,128)S(1)}, u32[]{:S(2)}, u32[]{:S(2)}) %collective-permute-start.2) | collective-permute-done | bytes 155680 | tf_op jit(solution)/shard_map/ppermute | solution.py:161
  26.7 0.0 copy-done.3
  26.7 0.0 copy-start.4
  26.7 0.7 %copy-done.4 = f32[304,128]{1,0:T(8,128)} copy-done((f32[304,128]{1,0:T(8,128)}, f32[304,128]{1,0:T(8,128)S(1)}, u32[]{:S(2)}) %copy-start.4) | copy-done | bytes 155672
  27.4 6.4 %shard_map.94 = (f32[3,128,128]{2,1,0:T(8,128)}, f32[3,128,128]{2,1,0:T(8,128)}, f32[128,128]{1,0:T(8,128)}) custom-call(f32[16]{0:T(128)} %pad_maximum_fusion.2.trig_ref, f32[128,1]{1,0:T(8,128)} %sine_multiply_fusion.rot_ref, f32[8,128,128]{2,1,0:T(8,128)} %copy-done, f32[3,128,128]{2,1,0:T(8,128)} %copy-done.1, f32[304,128]{1,0:T(8,128)} %copy-done.3, ...), custom_call_target="tpu_custom_call" | custom-call | flops 31457280 | bytes 1572864 | tf_op jit(solution)/shard_map/pallas_call | solution.py:112
  33.8 0.0 copy-start.2
  33.8 5.0 %collective-permute-start.3 = (f32[3,128,128]{2,1,0:T(8,128)}, f32[3,128,128]{2,1,0:T(8,128)S(1)}, u32[]{:S(2)}, u32[]{:S(2)}) collective-permute-start(f32[3,128,128]{2,1,0:T(8,128)} %get-tuple-element.6), channel_id=1, source_target_pairs={{0,16},{16,32},{32,48},{48,64},{64,80},{80,96},{96,112},{112,128},... | collective-permute-start | bytes 589832 | tf_op jit(solution)/shard_map/ppermute | solution.py:28
  38.8 18.5 %all_to_all.5 = f32[32,4,128]{2,1,0:T(4,128)S(1)} all-to-all(f32[32,4,128]{2,1,0:T(4,128)} %bitcast.33), channel_id=1, replica_groups=mesh['tm'=32,'cell'=16] {'tm'}, dimensions={0} | all-to-all | bytes 131072 | tf_op jit(solution)/shard_map/all_to_all | solution.py:131
  57.3 0.6 %reduce_sum.19 = f32[4,128]{1,0:T(4,128)} reduce(f32[32,4,128]{2,1,0:T(4,128)S(1)} %all_to_all.5, f32[]{:T(128)} %constant.23.clone.1), dimensions={0}, to_apply=%region_1.2 | reduce | flops 15872 | bytes 67588 | tf_op jit(solution)/shard_map/reduce_sum | solution.py:131
  57.9 0.0 collective-permute-done.3
  57.9 0.0 copy-done.2
  57.9 0.7 %subtract_bitcast_fusion = f32[1,3,128,128]{3,2,1,0:T(8,128)} fusion(f32[3,128,128]{2,1,0:T(8,128)S(1)} %copy-done.2, f32[3,128,128]{2,1,0:T(8,128)S(1)} %collective-permute-done.3), kind=kLoop, calls=%fused_computation.6 | loop fusion | flops 49152 | bytes 589824 | tf_op jit(solution)/shard_map/broadcast_in_dim | solution.py:171
  (8 shorter events, 0.2 us)
Async XLA Ops:
  0.6 9.9 %copy-start.5 = (s32[128,128]{1,0:T(8,128)S(1)}, s32[128,128]{1,0:T(8,128)}, u32[]{:S(2)}) copy-start(s32[128,128]{1,0:T(8,128)} %param.8) | copy-start | bytes 196612
  0.6 14.6 %collective-permute-start = (f32[3,128,128]{2,1,0:T(8,128)}, f32[3,128,128]{2,1,0:T(8,128)S(1)}, u32[]{:S(2)}, u32[]{:S(2)}) collective-permute-start(f32[3,128,128]{2,1,0:T(8,128)} %bitcast.30), channel_id=1, source_target_pairs={{0,496},{16,0},{32,16},{48,32},{64,48},{80,64},{96,80},{112,96},{1... | collective-permute-start | bytes 589832 | tf_op jit(solution)/shard_map/ppermute | solution.py:28
  10.5 0.8 %copy-start.6 = (s32[128,128]{1,0:T(8,128)S(1)}, s32[128,128]{1,0:T(8,128)}, u32[]{:S(2)}) copy-start(s32[128,128]{1,0:T(8,128)} %param.9) | copy-start | bytes 196612
  10.5 0.8 %copy-start.10 = (f32[8]{0:T(128)S(1)}, f32[8]{0:T(128)}, u32[]{:S(2)}) copy-start(f32[8]{0:T(128)} %param.10) | copy-start | bytes 100
  11.5 0.8 %copy-start.7 = (f32[128,128]{1,0:T(8,128)S(1)}, f32[128,128]{1,0:T(8,128)}, u32[]{:S(2)}) copy-start(f32[128,128]{1,0:T(8,128)} %param.11) | copy-start | bytes 196612
  12.3 0.8 %copy-start.8 = (f32[128,128]{1,0:T(8,128)S(1)}, f32[128,128]{1,0:T(8,128)}, u32[]{:S(2)}) copy-start(f32[128,128]{1,0:T(8,128)} %param.12) | copy-start | bytes 196612
  13.2 0.8 %copy-start.9 = (f32[128,128]{1,0:T(8,128)S(1)}, f32[128,128]{1,0:T(8,128)}, u32[]{:S(2)}) copy-start(f32[128,128]{1,0:T(8,128)} %param.13) | copy-start | bytes 196612
  14.0 0.8 %copy-start = (f32[8,128,128]{2,1,0:T(8,128)}, f32[8,128,128]{2,1,0:T(8,128)S(1)}, u32[]{:S(2)}) copy-start(f32[8,128,128]{2,1,0:T(8,128)S(1)} %bitcast_dynamic-update-slice_fusion.own_ref) | copy-start | bytes 1572868
  15.2 0.7 %copy-start.1 = (f32[3,128,128]{2,1,0:T(8,128)}, f32[3,128,128]{2,1,0:T(8,128)S(1)}, u32[]{:S(2)}) copy-start(f32[3,128,128]{2,1,0:T(8,128)S(1)} %collective-permute-done.next_ref) | copy-start | bytes 589828
  16.0 9.8 %collective-permute-start.1 = (f32[304,128]{1,0:T(8,128)S(1)}, f32[304,128]{1,0:T(8,128)S(1)}, u32[]{:S(2)}, u32[]{:S(2)}) collective-permute-start(f32[304,128]{1,0:T(8,128)S(1)} %pad_maximum_fusion), channel_id=1, source_target_pairs={{0,1},{1,2},{2,3},{3,4},{4,5},{5,6},{6,7},{7,8},{8,9},{9,10},{10,1... | collective-permute-start | bytes 466952 | tf_op jit(solution)/shard_map/ppermute | solution.py:160
  18.1 8.6 %collective-permute-start.2 = (f32[304,128]{1,0:T(8,128)S(1)}, f32[304,128]{1,0:T(8,128)S(1)}, u32[]{:S(2)}, u32[]{:S(2)}) collective-permute-start(f32[304,128]{1,0:T(8,128)S(1)} %pad_maximum_fusion.1), channel_id=1, source_target_pairs={{0,15},{1,0},{2,1},{3,2},{4,3},{5,4},{6,5},{7,6},{8,7},{9,8},{10,9... | collective-permute-start | bytes 466952 | tf_op jit(solution)/shard_map/ppermute | solution.py:161
  25.8 0.9 %copy-start.3 = (f32[304,128]{1,0:T(8,128)}, f32[304,128]{1,0:T(8,128)S(1)}, u32[]{:S(2)}) copy-start(f32[304,128]{1,0:T(8,128)S(1)} %collective-permute-done.1.left_ref) | copy-start | bytes 466948
  26.7 0.7 %copy-start.4 = (f32[304,128]{1,0:T(8,128)}, f32[304,128]{1,0:T(8,128)S(1)}, u32[]{:S(2)}) copy-start(f32[304,128]{1,0:T(8,128)S(1)} %collective-permute-done.2.right_ref) | copy-start | bytes 466948
  33.8 24.1 %copy-start.2 = (f32[3,128,128]{2,1,0:T(8,128)S(1)}, f32[3,128,128]{2,1,0:T(8,128)}, u32[]{:S(2)}) copy-start(f32[3,128,128]{2,1,0:T(8,128)} %get-tuple-element.7) | copy-start | bytes 589828
  33.8 24.1 %collective-permute-start.3 = (f32[3,128,128]{2,1,0:T(8,128)}, f32[3,128,128]{2,1,0:T(8,128)S(1)}, u32[]{:S(2)}, u32[]{:S(2)}) collective-permute-start(f32[3,128,128]{2,1,0:T(8,128)} %get-tuple-element.6), channel_id=1, source_target_pairs={{0,16},{16,32},{32,48},{48,64},{64,80},{80,96},{96,112},{112,128},... | collective-permute-start | bytes 589832 | tf_op jit(solution)/shard_map/ppermute | solution.py:28

commit v6 on v5

--- a/solution.py
+++ b/solution.py
@@ -56,26 +56,27 @@
 
     row = lax.broadcasted_iota(jnp.int32, (rows, lanes), 0)
     first, last = row == 0, row == rows - 1
-    def across_cols(q):
-        return 0.5 * (pltpu.roll(q, lanes - 1, 1) - pltpu.roll(q, 1, 1))
+    def cols_diff(q):
+        return pltpu.roll(q, lanes - 1, 1) - pltpu.roll(q, 1, 1)
 
-    def across_rows(q):
+    def rows_diff(q):
         upper = jnp.where(last, 0.0, pltpu.roll(q, rows - 1, 0))
         lower = jnp.where(first, 0.0, pltpu.roll(q, 1, 0))
-        return 0.5 * (upper - lower)
+        return upper - lower
 
+    half_flux, half_press = 0.5 * FLUX_RATE, 0.5 * PRESS_RATE
     sea, depth, retain = wide_ref[3], wide_ref[4], wide_ref[5]
     rot = rot_ref[...]
     keep = sea * retain
     height, east, north = wide_ref[0] * sea, wide_ref[1] * sea, wide_ref[2] * sea
     for step in range(STEPS):
         force = trig_ref[step] * wide_ref[6] + trig_ref[STEPS + step] * wide_ref[7]
-        spread = across_cols(depth * east) + across_rows(depth * north)
-        height = sea * (height - FLUX_RATE * spread)
+        spread = cols_diff(depth * east) + rows_diff(depth * north)
+        height = sea * (height - half_flux * spread)
         surface = height + force
         east, north = (
-            keep * (east - PRESS_RATE * across_cols(surface) + rot * north),
-            keep * (north - PRESS_RATE * across_rows(surface) - rot * east),
+            keep * (east - half_press * cols_diff(surface) + rot * north),
+            keep * (north - half_press * rows_diff(surface) - rot * east),
         )
         stored_ref[step, 0] = east[:, :tile]
         stored_ref[step, 1] = north[:, :tile]
@@ -85,15 +86,15 @@
     defect_ref[0] = height[:, :tile]
     defect_ref[1] = east[:, :tile]
     defect_ref[2] = north[:, :tile]
-    depth_flux = FLUX_RATE * depth
+    half_depth_flux = 0.5 * (FLUX_RATE * depth)
     drag = jnp.zeros((rows, tile), jnp.float32)
     for back in range(STEPS):
         step = STEPS - 1 - back
         east_part = keep * east
         north_part = keep * north
-        height = sea * (height + PRESS_RATE * (across_cols(east_part) + across_rows(north_part)))
-        east = east_part - rot * north_part + depth_flux * across_cols(height)
-        north = north_part + rot * east_part + depth_flux * across_rows(height)
+        height = sea * (height + half_press * (cols_diff(east_part) + rows_diff(north_part)))
+        east = east_part - rot * north_part + half_depth_flux * cols_diff(height)
+        north = north_part + rot * east_part + half_depth_flux * rows_diff(height)
         drag = drag - (
             east_part[:, :tile] * stored_ref[step, 0] + north_part[:, :tile] * stored_ref[step, 1]
         )

time: 59.1 us -> 59.2 us (level)
  no operation moved by 1% of the time
where the time goes in v6:
time: 59.2 us; the launch traced here: 58.7 us
  starting transfers between devices  22.1 us (37%)
  blocking collectives  18.5 us (31%)
  local copies, waits for them, and re-layouts  6.88 us (12%)
  Pallas kernels  6.49 us (11%)
  other arithmetic  3.04 us (5%)
  waiting for transfers between devices  0.93 us (2%)
  between operations  0.8 us (1%)
    all_to_all x1, blocking collectives, reduce_scatter_rows(): return jnp.sum(lax.all_to_all(pieces, axis, 0, 0, tiled=True), axis=0)  18.5 us
    ppermute x2, starting transfers between devices, from_behind(): return lax.ppermute(value, axis, ring_pairs(lax.axis_size(axis), steps))  13.9 us
    pallas_call x1, Pallas kernels, shooting(): pl.pallas_call(functools.partial(shooting_kernel, halo=halo, scale=scale)...  6.49 us
    ppermute x1, starting transfers between devices, local(): from_right = lax.ppermute(strips(False), 'cell', ring_pairs(cells, -1))  6.22 us
    unnamed x25, local copies, waits for them, and re-layouts  6.05 us
    ppermute x1, starting transfers between devices, local(): from_left = lax.ppermute(strips(True), 'cell', ring_pairs(cells, 1))  1.92 us
  transfers between devices with their start and end apart: 4, of which 1 were waited for; matrix products, arithmetic and copies ran while one was open for 7% of the time, Pallas kernels for 0%

profile of v6, /device:TPU:1, one launch (start us, length us, event | category | flops | bytes accessed | tf_op | source)
XLA Modules:
  0.0 58.7 jit_solution(17264488785372076104)
XLA Ops:
  0.6 0.0 copy-start.5
  0.6 8.9 %collective-permute-start = (f32[3,128,128]{2,1,0:T(8,128)}, f32[3,128,128]{2,1,0:T(8,128)S(1)}, u32[]{:S(2)}, u32[]{:S(2)}) collective-permute-start(f32[3,128,128]{2,1,0:T(8,128)} %bitcast.30), channel_id=1, source_target_pairs={{0,496},{16,0},{32,16},{48,32},{64,48},{80,64},{96,80},{112,96},{1... | collective-permute-start | bytes 589832 | tf_op jit(solution)/shard_map/ppermute | solution.py:28
  9.6 0.9 %constant_dynamic-update-slice_fusion = f32[8,128,128]{2,1,0:T(8,128)S(1)} fusion(f32[1,3,128,128]{3,2,1,0:T(8,128)} %param.7), kind=kLoop, calls=%fused_computation.15 | loop fusion | bytes 393216
  10.5 0.0 copy-done.5
  10.5 0.0 copy-start.6
  10.5 0.0 copy-start.10
  10.6 0.8 %copy-done.6 = s32[128,128]{1,0:T(8,128)S(1)} copy-done((s32[128,128]{1,0:T(8,128)S(1)}, s32[128,128]{1,0:T(8,128)}, u32[]{:S(2)}) %copy-start.6) | copy-done | bytes 65560
  11.4 0.0 copy-done.10
  11.4 0.1 select_reduce_fusion
  11.5 0.0 copy-start.7
  11.5 0.8 %copy-done.7 = f32[128,128]{1,0:T(8,128)S(1)} copy-done((f32[128,128]{1,0:T(8,128)S(1)}, f32[128,128]{1,0:T(8,128)}, u32[]{:S(2)}) %copy-start.7) | copy-done | bytes 65560
  12.3 0.0 copy-start.8
  12.3 0.8 %copy-done.8 = f32[128,128]{1,0:T(8,128)S(1)} copy-done((f32[128,128]{1,0:T(8,128)S(1)}, f32[128,128]{1,0:T(8,128)}, u32[]{:S(2)}) %copy-start.8) | copy-done | bytes 65560
  13.2 0.0 copy-start.9
  13.2 0.8 %copy-done.9 = f32[128,128]{1,0:T(8,128)S(1)} copy-done((f32[128,128]{1,0:T(8,128)S(1)}, f32[128,128]{1,0:T(8,128)}, u32[]{:S(2)}) %copy-start.9) | copy-done | bytes 65560
  14.0 0.0 copy-start
  14.0 0.2 slice_bitcast_fusion
  14.2 0.6 %copy-done = f32[8,128,128]{2,1,0:T(8,128)} copy-done((f32[8,128,128]{2,1,0:T(8,128)}, f32[8,128,128]{2,1,0:T(8,128)S(1)}, u32[]{:S(2)}) %copy-start) | copy-done | bytes 524312
  14.8 0.2 copy.19
  15.0 0.2 copy.21
  15.2 0.0 collective-permute-done.next_ref
  15.2 0.0 copy-start.1
  15.2 0.1 slice_bitcast_fusion.2
  15.3 0.6 copy-done.1
  15.9 0.1 copy.20
  16.0 1.9 %collective-permute-start.1 = (f32[304,128]{1,0:T(8,128)S(1)}, f32[304,128]{1,0:T(8,128)S(1)}, u32[]{:S(2)}, u32[]{:S(2)}) collective-permute-start(f32[304,128]{1,0:T(8,128)S(1)} %pad_maximum_fusion), channel_id=1, source_target_pairs={{0,1},{1,2},{2,3},{3,4},{4,5},{5,6},{6,7},{7,8},{8,9},{9,10},{10,1... | collective-permute-start | bytes 466952 | tf_op jit(solution)/shard_map/ppermute | solution.py:161
  17.9 0.1 copy.22
  18.1 6.2 %collective-permute-start.2 = (f32[304,128]{1,0:T(8,128)S(1)}, f32[304,128]{1,0:T(8,128)S(1)}, u32[]{:S(2)}, u32[]{:S(2)}) collective-permute-start(f32[304,128]{1,0:T(8,128)S(1)} %pad_maximum_fusion.1), channel_id=1, source_target_pairs={{0,15},{1,0},{2,1},{3,2},{4,3},{5,4},{6,5},{7,6},{8,7},{9,8},{10,9... | collective-permute-start | bytes 466952 | tf_op jit(solution)/shard_map/ppermute | solution.py:162
  24.3 0.6 pad_maximum_fusion.2.trig_ref
  24.9 0.9 %sine_multiply_fusion.rot_ref = f32[128,1]{1,0:T(8,128)} fusion(), kind=kLoop, calls=%fused_computation.14 | loop fusion | flops 640 | bytes 512 | tf_op jit(solution)/shard_map/mul | solution.py:33
  25.8 0.0 collective-permute-done.1.left_ref
  25.8 0.0 copy-start.3
  25.8 0.9 %collective-permute-done.2.right_ref = f32[304,128]{1,0:T(8,128)S(1)} collective-permute-done((f32[304,128]{1,0:T(8,128)S(1)}, f32[304,128]{1,0:T(8,128)S(1)}, u32[]{:S(2)}, u32[]{:S(2)}) %collective-permute-start.2) | collective-permute-done | bytes 155680 | tf_op jit(solution)/shard_map/ppermute | solution.py:162
  26.7 0.0 copy-done.3
  26.7 0.0 copy-start.4
  26.7 0.7 %copy-done.4 = f32[304,128]{1,0:T(8,128)} copy-done((f32[304,128]{1,0:T(8,128)}, f32[304,128]{1,0:T(8,128)S(1)}, u32[]{:S(2)}) %copy-start.4) | copy-done | bytes 155672
  27.4 6.5 %shard_map.94 = (f32[3,128,128]{2,1,0:T(8,128)}, f32[3,128,128]{2,1,0:T(8,128)}, f32[128,128]{1,0:T(8,128)}) custom-call(f32[16]{0:T(128)} %pad_maximum_fusion.2.trig_ref, f32[128,1]{1,0:T(8,128)} %sine_multiply_fusion.rot_ref, f32[8,128,128]{2,1,0:T(8,128)} %copy-done, f32[3,128,128]{2,1,0:T(8,128)} %copy-done.1, f32[304,128]{1,0:T(8,128)} %copy-done.3, ...), custom_call_target="tpu_custom_call" | custom-call | flops 31457280 | bytes 1572864 | tf_op jit(solution)/shard_map/pallas_call | solution.py:113
  33.9 0.0 copy-start.2
  33.9 5.0 %collective-permute-start.3 = (f32[3,128,128]{2,1,0:T(8,128)}, f32[3,128,128]{2,1,0:T(8,128)S(1)}, u32[]{:S(2)}, u32[]{:S(2)}) collective-permute-start(f32[3,128,128]{2,1,0:T(8,128)} %get-tuple-element.6), channel_id=1, source_target_pairs={{0,16},{16,32},{32,48},{48,64},{64,80},{80,96},{96,112},{112,128},... | collective-permute-start | bytes 589832 | tf_op jit(solution)/shard_map/ppermute | solution.py:28
  38.9 18.5 %all_to_all.5 = f32[32,4,128]{2,1,0:T(4,128)S(1)} all-to-all(f32[32,4,128]{2,1,0:T(4,128)} %bitcast.33), channel_id=1, replica_groups=mesh['tm'=32,'cell'=16] {'tm'}, dimensions={0} | all-to-all | bytes 131072 | tf_op jit(solution)/shard_map/all_to_all | solution.py:132
  57.4 0.6 %reduce_sum.19 = f32[4,128]{1,0:T(4,128)} reduce(f32[32,4,128]{2,1,0:T(4,128)S(1)} %all_to_all.5, f32[]{:T(128)} %constant.23.clone.1), dimensions={0}, to_apply=%region_1.2 | reduce | flops 15872 | bytes 67588 | tf_op jit(solution)/shard_map/reduce_sum | solution.py:132
  58.0 0.0 collective-permute-done.3
  58.0 0.0 copy-done.2
  58.0 0.7 %subtract_bitcast_fusion = f32[1,3,128,128]{3,2,1,0:T(8,128)} fusion(f32[3,128,128]{2,1,0:T(8,128)S(1)} %copy-done.2, f32[3,128,128]{2,1,0:T(8,128)S(1)} %collective-permute-done.3), kind=kLoop, calls=%fused_computation.6 | loop fusion | flops 49152 | bytes 589824 | tf_op jit(solution)/shard_map/broadcast_in_dim | solution.py:172
  (8 shorter events, 0.2 us)
Async XLA Ops:
  0.6 9.9 %copy-start.5 = (s32[128,128]{1,0:T(8,128)S(1)}, s32[128,128]{1,0:T(8,128)}, u32[]{:S(2)}) copy-start(s32[128,128]{1,0:T(8,128)} %param.8) | copy-start | bytes 196612
  0.6 14.6 %collective-permute-start = (f32[3,128,128]{2,1,0:T(8,128)}, f32[3,128,128]{2,1,0:T(8,128)S(1)}, u32[]{:S(2)}, u32[]{:S(2)}) collective-permute-start(f32[3,128,128]{2,1,0:T(8,128)} %bitcast.30), channel_id=1, source_target_pairs={{0,496},{16,0},{32,16},{48,32},{64,48},{80,64},{96,80},{112,96},{1... | collective-permute-start | bytes 589832 | tf_op jit(solution)/shard_map/ppermute | solution.py:28
  10.5 0.8 %copy-start.6 = (s32[128,128]{1,0:T(8,128)S(1)}, s32[128,128]{1,0:T(8,128)}, u32[]{:S(2)}) copy-start(s32[128,128]{1,0:T(8,128)} %param.9) | copy-start | bytes 196612
  10.5 0.8 %copy-start.10 = (f32[8]{0:T(128)S(1)}, f32[8]{0:T(128)}, u32[]{:S(2)}) copy-start(f32[8]{0:T(128)} %param.10) | copy-start | bytes 100
  11.5 0.8 %copy-start.7 = (f32[128,128]{1,0:T(8,128)S(1)}, f32[128,128]{1,0:T(8,128)}, u32[]{:S(2)}) copy-start(f32[128,128]{1,0:T(8,128)} %param.11) | copy-start | bytes 196612
  12.3 0.8 %copy-start.8 = (f32[128,128]{1,0:T(8,128)S(1)}, f32[128,128]{1,0:T(8,128)}, u32[]{:S(2)}) copy-start(f32[128,128]{1,0:T(8,128)} %param.12) | copy-start | bytes 196612
  13.2 0.8 %copy-start.9 = (f32[128,128]{1,0:T(8,128)S(1)}, f32[128,128]{1,0:T(8,128)}, u32[]{:S(2)}) copy-start(f32[128,128]{1,0:T(8,128)} %param.13) | copy-start | bytes 196612
  14.0 0.8 %copy-start = (f32[8,128,128]{2,1,0:T(8,128)}, f32[8,128,128]{2,1,0:T(8,128)S(1)}, u32[]{:S(2)}) copy-start(f32[8,128,128]{2,1,0:T(8,128)S(1)} %bitcast_dynamic-update-slice_fusion.own_ref) | copy-start | bytes 1572868
  15.2 0.7 %copy-start.1 = (f32[3,128,128]{2,1,0:T(8,128)}, f32[3,128,128]{2,1,0:T(8,128)S(1)}, u32[]{:S(2)}) copy-start(f32[3,128,128]{2,1,0:T(8,128)S(1)} %collective-permute-done.next_ref) | copy-start | bytes 589828
  16.0 9.8 %collective-permute-start.1 = (f32[304,128]{1,0:T(8,128)S(1)}, f32[304,128]{1,0:T(8,128)S(1)}, u32[]{:S(2)}, u32[]{:S(2)}) collective-permute-start(f32[304,128]{1,0:T(8,128)S(1)} %pad_maximum_fusion), channel_id=1, source_target_pairs={{0,1},{1,2},{2,3},{3,4},{4,5},{5,6},{6,7},{7,8},{8,9},{9,10},{10,1... | collective-permute-start | bytes 466952 | tf_op jit(solution)/shard_map/ppermute | solution.py:161
  18.1 8.6 %collective-permute-start.2 = (f32[304,128]{1,0:T(8,128)S(1)}, f32[304,128]{1,0:T(8,128)S(1)}, u32[]{:S(2)}, u32[]{:S(2)}) collective-permute-start(f32[304,128]{1,0:T(8,128)S(1)} %pad_maximum_fusion.1), channel_id=1, source_target_pairs={{0,15},{1,0},{2,1},{3,2},{4,3},{5,4},{6,5},{7,6},{8,7},{9,8},{10,9... | collective-permute-start | bytes 466952 | tf_op jit(solution)/shard_map/ppermute | solution.py:162
  25.8 0.9 %copy-start.3 = (f32[304,128]{1,0:T(8,128)}, f32[304,128]{1,0:T(8,128)S(1)}, u32[]{:S(2)}) copy-start(f32[304,128]{1,0:T(8,128)S(1)} %collective-permute-done.1.left_ref) | copy-start | bytes 466948
  26.7 0.7 %copy-start.4 = (f32[304,128]{1,0:T(8,128)}, f32[304,128]{1,0:T(8,128)S(1)}, u32[]{:S(2)}) copy-start(f32[304,128]{1,0:T(8,128)S(1)} %collective-permute-done.2.right_ref) | copy-start | bytes 466948
  33.9 24.1 %copy-start.2 = (f32[3,128,128]{2,1,0:T(8,128)S(1)}, f32[3,128,128]{2,1,0:T(8,128)}, u32[]{:S(2)}) copy-start(f32[3,128,128]{2,1,0:T(8,128)} %get-tuple-element.7) | copy-start | bytes 589828
  33.9 24.1 %collective-permute-start.3 = (f32[3,128,128]{2,1,0:T(8,128)}, f32[3,128,128]{2,1,0:T(8,128)S(1)}, u32[]{:S(2)}, u32[]{:S(2)}) collective-permute-start(f32[3,128,128]{2,1,0:T(8,128)} %get-tuple-element.6), channel_id=1, source_target_pairs={{0,16},{16,32},{32,48},{48,64},{64,80},{80,96},{96,112},{112,128},... | collective-permute-start | bytes 589832 | tf_op jit(solution)/shard_map/ppermute | solution.py:28

commit v7 on v6

--- a/solution.py
+++ b/solution.py
@@ -38,30 +38,31 @@
     defect_ref, pulled_ref, drag_ref, wide_ref, ahead_ref, stored_ref, *, halo, scale
 ):
     rows, tile = own_ref.shape[-2], own_ref.shape[-1]
-    lanes = wide_ref.shape[-1]
-
-    def circular(middle, right, left):
-        gap = jnp.zeros((tile - right.shape[0] - left.shape[0], rows), jnp.float32)
-        rim = jnp.transpose(jnp.concatenate([right, gap, left], axis=0))
-        return jnp.concatenate([middle, rim], axis=1)
-
+    span = wide_ref.shape[-2]
     fields = own_ref.shape[0]
     wide = 2 * halo
     for field in range(fields):
         strip = slice(field * wide, (field + 1) * wide)
-        wide_ref[field] = circular(own_ref[field], right_ref[strip, :], left_ref[strip, :])
+        wide_ref[field] = jnp.concatenate(
+            [left_ref[strip, :], jnp.transpose(own_ref[field]), right_ref[strip, :]], axis=0
+        )
+    edge = jnp.zeros((halo, rows), jnp.float32)
     for field in range(next_ref.shape[0]):
         strip = slice(fields * wide + field * halo, fields * wide + (field + 1) * halo)
-        ahead_ref[field] = circular(next_ref[field], right_ref[strip, :], left_ref[strip, :])
+        ahead_ref[field] = jnp.concatenate(
+            [edge, left_ref[strip, :], jnp.transpose(next_ref[field]), right_ref[strip, :], edge], axis=0
+        )
 
-    row = lax.broadcasted_iota(jnp.int32, (rows, lanes), 0)
-    first, last = row == 0, row == rows - 1
+    lane = lax.broadcasted_iota(jnp.int32, (span, rows), 1)
+    first, last = lane == 0, lane == rows - 1
+    inner = slice(wide, wide + tile)
+
     def cols_diff(q):
-        return pltpu.roll(q, lanes - 1, 1) - pltpu.roll(q, 1, 1)
+        return pltpu.roll(q, span - 1, 0) - pltpu.roll(q, 1, 0)
 
     def rows_diff(q):
-        upper = jnp.where(last, 0.0, pltpu.roll(q, rows - 1, 0))
-        lower = jnp.where(first, 0.0, pltpu.roll(q, 1, 0))
+        upper = jnp.where(last, 0.0, pltpu.roll(q, rows - 1, 1))
+        lower = jnp.where(first, 0.0, pltpu.roll(q, 1, 1))
         return upper - lower
 
     half_flux, half_press = 0.5 * FLUX_RATE, 0.5 * PRESS_RATE
@@ -78,16 +79,16 @@
             keep * (east - half_press * cols_diff(surface) + rot * north),
             keep * (north - half_press * rows_diff(surface) - rot * east),
         )
-        stored_ref[step, 0] = east[:, :tile]
-        stored_ref[step, 1] = north[:, :tile]
+        stored_ref[step, 0] = east[inner]
+        stored_ref[step, 1] = north[inner]
     height = sea * (height - ahead_ref[0])
     east = sea * (east - ahead_ref[1])
     north = sea * (north - ahead_ref[2])
-    defect_ref[0] = height[:, :tile]
-    defect_ref[1] = east[:, :tile]
-    defect_ref[2] = north[:, :tile]
+    defect_ref[0] = jnp.transpose(height[inner])
+    defect_ref[1] = jnp.transpose(east[inner])
+    defect_ref[2] = jnp.transpose(north[inner])
     half_depth_flux = 0.5 * (FLUX_RATE * depth)
-    drag = jnp.zeros((rows, tile), jnp.float32)
+    drag = jnp.zeros((tile, rows), jnp.float32)
     for back in range(STEPS):
         step = STEPS - 1 - back
         east_part = keep * east
@@ -95,35 +96,33 @@
         height = sea * (height + half_press * (cols_diff(east_part) + rows_diff(north_part)))
         east = east_part - rot * north_part + half_depth_flux * cols_diff(height)
         north = north_part + rot * east_part + half_depth_flux * rows_diff(height)
-        drag = drag - (
-            east_part[:, :tile] * stored_ref[step, 0] + north_part[:, :tile] * stored_ref[step, 1]
-        )
-    sea_tile = sea[:, :tile]
-    pulled_ref[0] = sea_tile * height[:, :tile]
-    pulled_ref[1] = sea_tile * east[:, :tile]
-    pulled_ref[2] = sea_tile * north[:, :tile]
-    drag_ref[...] = drag * scale
+        drag = drag - (east_part[inner] * stored_ref[step, 0] + north_part[inner] * stored_ref[step, 1])
+    sea_tile = sea[inner]
+    pulled_ref[0] = jnp.transpose(sea_tile * height[inner])
+    pulled_ref[1] = jnp.transpose(sea_tile * east[inner])
+    pulled_ref[2] = jnp.transpose(sea_tile * north[inner])
+    drag_ref[...] = jnp.transpose(drag * scale)
 
 
 def shooting(trig, rotation, own, following, from_left, from_right, halo, scale):
     fields, rows, tile = own.shape
     vmem = pl.BlockSpec(memory_space=pltpu.VMEM)
     state = jax.ShapeDtypeStruct((3, rows, tile), jnp.float32)
-    lanes = 2 * tile
+    span = tile + 4 * halo
     return pl.pallas_call(
         functools.partial(shooting_kernel, halo=halo, scale=scale),
         out_shape=(state, state, jax.ShapeDtypeStruct((rows, tile), jnp.float32)),
         in_specs=[pl.BlockSpec(memory_space=pltpu.SMEM)] + [vmem] * 5,
         out_specs=(vmem, vmem, vmem),
         scratch_shapes=[
-            pltpu.VMEM((fields, rows, lanes), jnp.float32),
-            pltpu.VMEM((3, rows, lanes), jnp.float32),
-            pltpu.VMEM((STEPS, 2, rows, tile), jnp.float32),
+            pltpu.VMEM((fields, span, rows), jnp.float32),
+            pltpu.VMEM((3, span, rows), jnp.float32),
+            pltpu.VMEM((STEPS, 2, tile, rows), jnp.float32),
         ],
         cost_estimate=pl.CostEstimate(
-            flops=2 * STEPS * 60 * rows * lanes, transcendentals=0, bytes_accessed=4 * rows * 24 * tile
+            flops=2 * STEPS * 60 * rows * span, transcendentals=0, bytes_accessed=4 * rows * 24 * tile
         ),
-    )(trig, rotation, own, following, from_left, from_right)
+    )(trig, rotation.reshape(1, rows), own, following, from_left, from_right)
 
 
 def reduce_scatter_rows(value, axis):

time: 59.2 us -> 57.9 us (0.978)
  Pallas kernels: 6.49 us -> 5.12 us
    pallas_call x1, Pallas kernels: 6.49 us -> 5.12 us  [shooting(): pl.pallas_call(functools.partial(shooting_kernel, halo=halo, scale=scale)...]
  transfers between devices with their start and end apart: 4 -> 4, of which waited for: 1 -> 1; matrix products, arithmetic and copies ran while one was open for 7% -> 6% of each run, Pallas kernels for 0% -> 0%
where the time goes in v7:
time: 57.9 us; the launch traced here: 57.3 us
  starting transfers between devices  22.1 us (38%)
  blocking collectives  18.5 us (32%)
  local copies, waits for them, and re-layouts  6.88 us (12%)
  Pallas kernels  5.12 us (9%)
  other arithmetic  2.78 us (5%)
  waiting for transfers between devices  1.19 us (2%)
  between operations  0.8 us (1%)
    all_to_all x1, blocking collectives, reduce_scatter_rows(): return jnp.sum(lax.all_to_all(pieces, axis, 0, 0, tiled=True), axis=0)  18.5 us
    ppermute x2, starting transfers between devices, from_behind(): return lax.ppermute(value, axis, ring_pairs(lax.axis_size(axis), steps))  13.9 us
    ppermute x1, starting transfers between devices, local(): from_right = lax.ppermute(strips(False), 'cell', ring_pairs(cells, -1))  6.22 us
    unnamed x25, local copies, waits for them, and re-layouts  6.05 us
    pallas_call x1, Pallas kernels, shooting(): pl.pallas_call(functools.partial(shooting_kernel, halo=halo, scale=scale)...  5.12 us
    ppermute x1, starting transfers between devices, local(): from_left = lax.ppermute(strips(True), 'cell', ring_pairs(cells, 1))  1.92 us
    ppermute x1, waiting for transfers between devices, local(): from_right = lax.ppermute(strips(False), 'cell', ring_pairs(cells, -1))  1.18 us
  transfers between devices with their start and end apart: 4, of which 1 were waited for; matrix products, arithmetic and copies ran while one was open for 6% of the time, Pallas kernels for 0%

profile of v7, /device:TPU:1, one launch (start us, length us, event | category | flops | bytes accessed | tf_op | source)
XLA Modules:
  0.0 57.3 jit_solution(8060060434863725063)
XLA Ops:
  0.6 0.0 copy-start.5
  0.6 8.9 %collective-permute-start = (f32[3,128,128]{2,1,0:T(8,128)}, f32[3,128,128]{2,1,0:T(8,128)S(1)}, u32[]{:S(2)}, u32[]{:S(2)}) collective-permute-start(f32[3,128,128]{2,1,0:T(8,128)} %bitcast.30), channel_id=1, source_target_pairs={{0,496},{16,0},{32,16},{48,32},{64,48},{80,64},{96,80},{112,96},{1... | collective-permute-start | bytes 589832 | tf_op jit(solution)/shard_map/ppermute | solution.py:28
  9.6 0.9 %constant_dynamic-update-slice_fusion = f32[8,128,128]{2,1,0:T(8,128)S(1)} fusion(f32[1,3,128,128]{3,2,1,0:T(8,128)} %param.7), kind=kLoop, calls=%fused_computation.14 | loop fusion | bytes 393216
  10.5 0.0 copy-done.5
  10.5 0.0 copy-start.6
  10.5 0.0 copy-start.10
  10.6 0.8 %copy-done.6 = s32[128,128]{1,0:T(8,128)S(1)} copy-done((s32[128,128]{1,0:T(8,128)S(1)}, s32[128,128]{1,0:T(8,128)}, u32[]{:S(2)}) %copy-start.6) | copy-done | bytes 65560
  11.4 0.0 copy-done.10
  11.4 0.1 select_reduce_fusion
  11.5 0.0 copy-start.7
  11.5 0.8 %copy-done.7 = f32[128,128]{1,0:T(8,128)S(1)} copy-done((f32[128,128]{1,0:T(8,128)S(1)}, f32[128,128]{1,0:T(8,128)}, u32[]{:S(2)}) %copy-start.7) | copy-done | bytes 65560
  12.3 0.0 copy-start.8
  12.3 0.8 %copy-done.8 = f32[128,128]{1,0:T(8,128)S(1)} copy-done((f32[128,128]{1,0:T(8,128)S(1)}, f32[128,128]{1,0:T(8,128)}, u32[]{:S(2)}) %copy-start.8) | copy-done | bytes 65560
  13.2 0.0 copy-start.9
  13.2 0.8 %copy-done.9 = f32[128,128]{1,0:T(8,128)S(1)} copy-done((f32[128,128]{1,0:T(8,128)S(1)}, f32[128,128]{1,0:T(8,128)}, u32[]{:S(2)}) %copy-start.9) | copy-done | bytes 65560
  14.0 0.0 copy-start
  14.0 0.2 slice_bitcast_fusion
  14.2 0.6 %copy-done = f32[8,128,128]{2,1,0:T(8,128)} copy-done((f32[8,128,128]{2,1,0:T(8,128)}, f32[8,128,128]{2,1,0:T(8,128)S(1)}, u32[]{:S(2)}) %copy-start) | copy-done | bytes 524312
  14.8 0.2 copy.14
  15.0 0.2 copy.16
  15.2 0.0 collective-permute-done.next_ref
  15.2 0.0 copy-start.1
  15.2 0.1 slice_bitcast_fusion.2
  15.3 0.6 copy-done.1
  15.9 0.1 copy.15
  16.0 1.9 %collective-permute-start.1 = (f32[304,128]{1,0:T(8,128)S(1)}, f32[304,128]{1,0:T(8,128)S(1)}, u32[]{:S(2)}, u32[]{:S(2)}) collective-permute-start(f32[304,128]{1,0:T(8,128)S(1)} %pad_maximum_fusion), channel_id=1, source_target_pairs={{0,1},{1,2},{2,3},{3,4},{4,5},{5,6},{6,7},{7,8},{8,9},{9,10},{10,1... | collective-permute-start | bytes 466952 | tf_op jit(solution)/shard_map/ppermute | solution.py:160
  17.9 0.1 copy.17
  18.1 6.2 %collective-permute-start.2 = (f32[304,128]{1,0:T(8,128)S(1)}, f32[304,128]{1,0:T(8,128)S(1)}, u32[]{:S(2)}, u32[]{:S(2)}) collective-permute-start(f32[304,128]{1,0:T(8,128)S(1)} %pad_maximum_fusion.1), channel_id=1, source_target_pairs={{0,15},{1,0},{2,1},{3,2},{4,3},{5,4},{6,5},{7,6},{8,7},{9,8},{10,9... | collective-permute-start | bytes 466952 | tf_op jit(solution)/shard_map/ppermute | solution.py:161
  24.3 0.6 %sine_multiply_fusion.rot_ref = f32[1,128]{1,0:T(1,128)} fusion(), kind=kLoop, calls=%fused_computation.16 | loop fusion | flops 640 | bytes 512 | tf_op jit(solution)/shard_map/mul | solution.py:33
  24.9 0.6 %pad_maximum_fusion.2.trig_ref = f32[16]{0:T(128)} fusion(f32[8]{0:T(128)S(1)} %get-tuple-element.13, f32[8]{0:T(128)S(1)} %get-tuple-element.14), kind=kLoop, calls=%fused_computation.15 | loop fusion | flops 16 | bytes 128 | tf_op jit(solution)/shard_map/concatenate | solution.py:164
  25.5 0.0 collective-permute-done.1.left_ref
  25.5 0.0 copy-start.3
  25.5 1.2 %collective-permute-done.2.right_ref = f32[304,128]{1,0:T(8,128)S(1)} collective-permute-done((f32[304,128]{1,0:T(8,128)S(1)}, f32[304,128]{1,0:T(8,128)S(1)}, u32[]{:S(2)}, u32[]{:S(2)}) %collective-permute-start.2) | collective-permute-done | bytes 155680 | tf_op jit(solution)/shard_map/ppermute | solution.py:161
  26.7 0.0 copy-done.3
  26.7 0.0 copy-start.4
  26.7 0.7 %copy-done.4 = f32[304,128]{1,0:T(8,128)} copy-done((f32[304,128]{1,0:T(8,128)}, f32[304,128]{1,0:T(8,128)S(1)}, u32[]{:S(2)}) %copy-start.4) | copy-done | bytes 155672
  27.4 5.1 %shard_map.94 = (f32[3,128,128]{2,1,0:T(8,128)}, f32[3,128,128]{2,1,0:T(8,128)}, f32[128,128]{1,0:T(8,128)}) custom-call(f32[16]{0:T(128)} %pad_maximum_fusion.2.trig_ref, f32[1,128]{1,0:T(1,128)} %sine_multiply_fusion.rot_ref, f32[8,128,128]{2,1,0:T(8,128)} %copy-done, f32[3,128,128]{2,1,0:T(8,128)} %copy-done.1, f32[304,128]{1,0:T(8,128)} %copy-done.3, ...), custom_call_target="tpu_custom_call" | custom-call | flops 23592960 | bytes 1572864 | tf_op jit(solution)/shard_map/pallas_call | solution.py:112
  32.5 0.0 copy-start.2
  32.5 5.0 %collective-permute-start.3 = (f32[3,128,128]{2,1,0:T(8,128)}, f32[3,128,128]{2,1,0:T(8,128)S(1)}, u32[]{:S(2)}, u32[]{:S(2)}) collective-permute-start(f32[3,128,128]{2,1,0:T(8,128)} %get-tuple-element.6), channel_id=1, source_target_pairs={{0,16},{16,32},{32,48},{48,64},{64,80},{80,96},{96,112},{112,128},... | collective-permute-start | bytes 589832 | tf_op jit(solution)/shard_map/ppermute | solution.py:28
  37.5 18.5 %all_to_all.5 = f32[32,4,128]{2,1,0:T(4,128)S(1)} all-to-all(f32[32,4,128]{2,1,0:T(4,128)} %bitcast.33), channel_id=1, replica_groups=mesh['tm'=32,'cell'=16] {'tm'}, dimensions={0} | all-to-all | bytes 131072 | tf_op jit(solution)/shard_map/all_to_all | solution.py:131
  56.0 0.6 %reduce_sum.19 = f32[4,128]{1,0:T(4,128)} reduce(f32[32,4,128]{2,1,0:T(4,128)S(1)} %all_to_all.5, f32[]{:T(128)} %constant.23.clone.1), dimensions={0}, to_apply=%region_1.2 | reduce | flops 15872 | bytes 67588 | tf_op jit(solution)/shard_map/reduce_sum | solution.py:131
  56.6 0.0 collective-permute-done.3
  56.6 0.0 copy-done.2
  56.6 0.7 %subtract_bitcast_fusion = f32[1,3,128,128]{3,2,1,0:T(8,128)} fusion(f32[3,128,128]{2,1,0:T(8,128)S(1)} %copy-done.2, f32[3,128,128]{2,1,0:T(8,128)S(1)} %collective-permute-done.3), kind=kLoop, calls=%fused_computation.6 | loop fusion | flops 49152 | bytes 589824 | tf_op jit(solution)/shard_map/broadcast_in_dim | solution.py:171
  (8 shorter events, 0.2 us)
Async XLA Ops:
  0.6 9.9 %copy-start.5 = (s32[128,128]{1,0:T(8,128)S(1)}, s32[128,128]{1,0:T(8,128)}, u32[]{:S(2)}) copy-start(s32[128,128]{1,0:T(8,128)} %param.8) | copy-start | bytes 196612
  0.6 14.6 %collective-permute-start = (f32[3,128,128]{2,1,0:T(8,128)}, f32[3,128,128]{2,1,0:T(8,128)S(1)}, u32[]{:S(2)}, u32[]{:S(2)}) collective-permute-start(f32[3,128,128]{2,1,0:T(8,128)} %bitcast.30), channel_id=1, source_target_pairs={{0,496},{16,0},{32,16},{48,32},{64,48},{80,64},{96,80},{112,96},{1... | collective-permute-start | bytes 589832 | tf_op jit(solution)/shard_map/ppermute | solution.py:28
  10.5 0.8 %copy-start.6 = (s32[128,128]{1,0:T(8,128)S(1)}, s32[128,128]{1,0:T(8,128)}, u32[]{:S(2)}) copy-start(s32[128,128]{1,0:T(8,128)} %param.9) | copy-start | bytes 196612
  10.5 0.8 %copy-start.10 = (f32[8]{0:T(128)S(1)}, f32[8]{0:T(128)}, u32[]{:S(2)}) copy-start(f32[8]{0:T(128)} %param.10) | copy-start | bytes 100
  11.5 0.8 %copy-start.7 = (f32[128,128]{1,0:T(8,128)S(1)}, f32[128,128]{1,0:T(8,128)}, u32[]{:S(2)}) copy-start(f32[128,128]{1,0:T(8,128)} %param.11) | copy-start | bytes 196612
  12.3 0.8 %copy-start.8 = (f32[128,128]{1,0:T(8,128)S(1)}, f32[128,128]{1,0:T(8,128)}, u32[]{:S(2)}) copy-start(f32[128,128]{1,0:T(8,128)} %param.12) | copy-start | bytes 196612
  13.2 0.8 %copy-start.9 = (f32[128,128]{1,0:T(8,128)S(1)}, f32[128,128]{1,0:T(8,128)}, u32[]{:S(2)}) copy-start(f32[128,128]{1,0:T(8,128)} %param.13) | copy-start | bytes 196612
  14.0 0.8 %copy-start = (f32[8,128,128]{2,1,0:T(8,128)}, f32[8,128,128]{2,1,0:T(8,128)S(1)}, u32[]{:S(2)}) copy-start(f32[8,128,128]{2,1,0:T(8,128)S(1)} %bitcast_dynamic-update-slice_fusion.own_ref) | copy-start | bytes 1572868
  15.2 0.7 %copy-start.1 = (f32[3,128,128]{2,1,0:T(8,128)}, f32[3,128,128]{2,1,0:T(8,128)S(1)}, u32[]{:S(2)}) copy-start(f32[3,128,128]{2,1,0:T(8,128)S(1)} %collective-permute-done.next_ref) | copy-start | bytes 589828
  16.0 9.5 %collective-permute-start.1 = (f32[304,128]{1,0:T(8,128)S(1)}, f32[304,128]{1,0:T(8,128)S(1)}, u32[]{:S(2)}, u32[]{:S(2)}) collective-permute-start(f32[304,128]{1,0:T(8,128)S(1)} %pad_maximum_fusion), channel_id=1, source_target_pairs={{0,1},{1,2},{2,3},{3,4},{4,5},{5,6},{6,7},{7,8},{8,9},{9,10},{10,1... | collective-permute-start | bytes 466952 | tf_op jit(solution)/shard_map/ppermute | solution.py:160
  18.1 8.6 %collective-permute-start.2 = (f32[304,128]{1,0:T(8,128)S(1)}, f32[304,128]{1,0:T(8,128)S(1)}, u32[]{:S(2)}, u32[]{:S(2)}) collective-permute-start(f32[304,128]{1,0:T(8,128)S(1)} %pad_maximum_fusion.1), channel_id=1, source_target_pairs={{0,15},{1,0},{2,1},{3,2},{4,3},{5,4},{6,5},{7,6},{8,7},{9,8},{10,9... | collective-permute-start | bytes 466952 | tf_op jit(solution)/shard_map/ppermute | solution.py:161
  25.5 1.2 %copy-start.3 = (f32[304,128]{1,0:T(8,128)}, f32[304,128]{1,0:T(8,128)S(1)}, u32[]{:S(2)}) copy-start(f32[304,128]{1,0:T(8,128)S(1)} %collective-permute-done.1.left_ref) | copy-start | bytes 466948
  26.7 0.7 %copy-start.4 = (f32[304,128]{1,0:T(8,128)}, f32[304,128]{1,0:T(8,128)S(1)}, u32[]{:S(2)}) copy-start(f32[304,128]{1,0:T(8,128)S(1)} %collective-permute-done.2.right_ref) | copy-start | bytes 466948
  32.5 24.1 %copy-start.2 = (f32[3,128,128]{2,1,0:T(8,128)S(1)}, f32[3,128,128]{2,1,0:T(8,128)}, u32[]{:S(2)}) copy-start(f32[3,128,128]{2,1,0:T(8,128)} %get-tuple-element.7) | copy-start | bytes 589828
  32.5 24.1 %collective-permute-start.3 = (f32[3,128,128]{2,1,0:T(8,128)}, f32[3,128,128]{2,1,0:T(8,128)S(1)}, u32[]{:S(2)}, u32[]{:S(2)}) collective-permute-start(f32[3,128,128]{2,1,0:T(8,128)} %get-tuple-element.6), channel_id=1, source_target_pairs={{0,16},{16,32},{32,48},{48,64},{64,80},{80,96},{96,112},{112,128},... | collective-permute-start | bytes 589832 | tf_op jit(solution)/shard_map/ppermute | solution.py:28

commit v8 on v7

--- a/solution.py
+++ b/solution.py
@@ -34,17 +34,18 @@
 
 
 def shooting_kernel(
-    trig_ref, rot_ref, own_ref, next_ref, left_ref, right_ref,
+    trig_ref, rot_ref, start_ref, sea_ref, depth_ref, retain_ref, cos_ref, sin_ref, next_ref, left_ref, right_ref,
     defect_ref, pulled_ref, drag_ref, wide_ref, ahead_ref, stored_ref, *, halo, scale
 ):
-    rows, tile = own_ref.shape[-2], own_ref.shape[-1]
+    rows, tile = sea_ref.shape[-2], sea_ref.shape[-1]
     span = wide_ref.shape[-2]
-    fields = own_ref.shape[0]
+    own = [start_ref.at[0], start_ref.at[1], start_ref.at[2], sea_ref, depth_ref, retain_ref, cos_ref, sin_ref]
+    fields = len(own)
     wide = 2 * halo
     for field in range(fields):
         strip = slice(field * wide, (field + 1) * wide)
         wide_ref[field] = jnp.concatenate(
-            [left_ref[strip, :], jnp.transpose(own_ref[field]), right_ref[strip, :]], axis=0
+            [left_ref[strip, :], jnp.transpose(own[field][...]), right_ref[strip, :]], axis=0
         )
     edge = jnp.zeros((halo, rows), jnp.float32)
     for field in range(next_ref.shape[0]):
@@ -104,15 +105,15 @@
     drag_ref[...] = jnp.transpose(drag * scale)
 
 
-def shooting(trig, rotation, own, following, from_left, from_right, halo, scale):
-    fields, rows, tile = own.shape
+def shooting(trig, rotation, start, statics, following, from_left, from_right, halo, scale):
+    fields, (rows, tile) = 3 + len(statics), statics[0].shape
     vmem = pl.BlockSpec(memory_space=pltpu.VMEM)
     state = jax.ShapeDtypeStruct((3, rows, tile), jnp.float32)
     span = tile + 4 * halo
     return pl.pallas_call(
         functools.partial(shooting_kernel, halo=halo, scale=scale),
         out_shape=(state, state, jax.ShapeDtypeStruct((rows, tile), jnp.float32)),
-        in_specs=[pl.BlockSpec(memory_space=pltpu.SMEM)] + [vmem] * 5,
+        in_specs=[pl.BlockSpec(memory_space=pltpu.SMEM)] + [vmem] * (5 + len(statics)),
         out_specs=(vmem, vmem, vmem),
         scratch_shapes=[
             pltpu.VMEM((fields, span, rows), jnp.float32),
@@ -122,7 +123,7 @@
         cost_estimate=pl.CostEstimate(
             flops=2 * STEPS * 60 * rows * span, transcendentals=0, bytes_accessed=4 * rows * 24 * tile
         ),
-    )(trig, rotation.reshape(1, rows), own, following, from_left, from_right)
+    )(trig, rotation.reshape(1, rows), start, *statics, following, from_left, from_right)
 
 
 def reduce_scatter_rows(value, axis):
@@ -144,17 +145,16 @@
     retain = 1.0 / (1.0 + drag_rate)
     initial = start_states[0]
     cells = lax.axis_size("cell")
-    own = jnp.concatenate(
-        [initial, jnp.stack([sea_mask, depth_field, retain, tide_cos, tide_sin])], axis=0
-    )
-    fields, rows, width = own.shape
+    statics = [sea_mask, depth_field, retain, tide_cos, tide_sin]
+    own = [initial[0], initial[1], initial[2]] + statics
+    rows, width = sea_mask.shape
     following = from_behind(initial, "tm", -1)
 
     def strips(at_right):
-        mine = own[..., width - 2 * halo :] if at_right else own[..., : 2 * halo]
+        mine = [field[:, width - 2 * halo :] if at_right else field[:, : 2 * halo] for field in own]
         theirs = following[..., width - halo :] if at_right else following[..., :halo]
         return jnp.concatenate(
-            [lane_dense(mine).reshape(-1, rows), lane_dense(theirs).reshape(-1, rows)], axis=0
+            [lane_dense(field) for field in mine] + [lane_dense(theirs).reshape(-1, rows)], axis=0
         )
 
     from_left = lax.ppermute(strips(True), "cell", ring_pairs(cells, 1))
@@ -163,7 +163,7 @@
     phases = (slice_index * STEPS + jnp.arange(STEPS)).astype(jnp.float32) * phase_unit
     trig = jnp.concatenate([jnp.cos(phases), jnp.sin(phases)])
     defect, pulled, drag_grad = shooting(
-        trig, coriolis(rows), own, following, from_left, from_right, halo, 1.0 / slice_count
+        trig, coriolis(rows), initial, statics, following, from_left, from_right, halo, 1.0 / slice_count
     )
     behind = from_behind(defect, "tm", 1)
     state_grad = pulled - behind

time: 57.9 us -> 63.6 us (1.098)
  local copies, waits for them, and re-layouts: 6.88 us -> 9.39 us
  waiting for transfers between devices: 1.19 us -> 3.55 us
    ppermute x1, waiting for transfers between devices: 0.01 us -> 3.54 us  [local(): from_left = lax.ppermute(strips(True), 'cell', ring_pairs(cells, 1))]
    ppermute x1, waiting for transfers between devices: 1.18 us -> 0.01 us  [local(): from_right = lax.ppermute(strips(False), 'cell', ring_pairs(cells, -1))]
    slice x0 -> x4, local copies, waits for them, and re-layouts: none -> 1.16 us  [the longest x1 0.92 us: local(): own = [initial[0], initial[1], initial[2]] + statics]
    div x0 -> x1, local copies, waits for them, and re-layouts: none -> 0.72 us  [local(): retain = 1.0 / (1.0 + drag_rate)]
    convert_element_type x0 -> x1, local copies, waits for them, and re-layouts: none -> 0.72 us  [local(): sea_mask = ocean_mask.astype(jnp.float32)]
    unnamed x25 -> x43, local copies, waits for them, and re-layouts: 6.05 us -> 6.51 us
  transfers between devices with their start and end apart: 4 -> 4, of which waited for: 1 -> 1; matrix products, arithmetic and copies ran while one was open for 6% -> 9% of each run, Pallas kernels for 0% -> 0%
where the time goes in v8:
time: 63.6 us; the launch traced here: 63 us
  starting transfers between devices  22.5 us (35%)
  blocking collectives  18.7 us (29%)
  local copies, waits for them, and re-layouts  9.39 us (15%)
  Pallas kernels  5.23 us (8%)
  waiting for transfers between devices  3.55 us (6%)
  other arithmetic  2.69 us (4%)
  between operations  0.9 us (1%)
    all_to_all x1, blocking collectives, reduce_scatter_rows(): return jnp.sum(lax.all_to_all(pieces, axis, 0, 0, tiled=True), axis=0)  18.7 us
    ppermute x2, starting transfers between devices, from_behind(): return lax.ppermute(value, axis, ring_pairs(lax.axis_size(axis), steps))  14.4 us
    unnamed x43, local copies, waits for them, and re-layouts  6.51 us
    ppermute x1, starting transfers between devices, local(): from_right = lax.ppermute(strips(False), 'cell', ring_pairs(cells, -1))  6.23 us
    pallas_call x1, Pallas kernels, shooting(): pl.pallas_call(functools.partial(shooting_kernel, halo=halo, scale=scale)...  5.23 us
    ppermute x1, waiting for transfers between devices, local(): from_left = lax.ppermute(strips(True), 'cell', ring_pairs(cells, 1))  3.54 us
    ppermute x1, starting transfers between devices, local(): from_left = lax.ppermute(strips(True), 'cell', ring_pairs(cells, 1))  1.93 us
  transfers between devices with their start and end apart: 4, of which 1 were waited for; matrix products, arithmetic and copies ran while one was open for 9% of the time, Pallas kernels for 0%

profile of v8, /device:TPU:1, one launch (start us, length us, event | category | flops | bytes accessed | tf_op | source)
XLA Modules:
  0.0 63.0 jit_solution(12495781929511188223)
XLA Ops:
  0.6 8.8 %collective-permute-start = (f32[3,128,128]{2,1,0:T(8,128)}, f32[3,128,128]{2,1,0:T(8,128)S(1)}, u32[]{:S(2)}, u32[]{:S(2)}) collective-permute-start(f32[3,128,128]{2,1,0:T(8,128)} %bitcast.66), channel_id=1, source_target_pairs={{0,496},{16,0},{32,16},{48,32},{64,48},{80,64},{96,80},{112,96},{1... | collective-permute-start | bytes 589832 | tf_op jit(solution)/shard_map/ppermute | solution.py:28
  9.4 0.9 %fusion.2 = (f32[1,1,128,128]{3,2,1,0:T(8,128)S(1)}, f32[1,1,128,128]{3,2,1,0:T(8,128)S(1)}, f32[1,1,128,128]{3,2,1,0:T(8,128)S(1)}) fusion(f32[1,3,128,128]{3,2,1,0:T(8,128)} %param.7), kind=kLoop, calls=%fused_computation.39 | loop fusion | bytes 393216 | tf_op jit(solution)/shard_map/slice | solution.py:149
  10.4 0.1 copy.39
  10.5 0.1 copy.40
  10.6 0.0 copy-start.7
  10.6 0.1 copy.41
  10.7 0.7 %copy-done.7 = s32[128,128]{1,0:T(8,128)S(1)} copy-done((s32[128,128]{1,0:T(8,128)S(1)}, s32[128,128]{1,0:T(8,128)}, u32[]{:S(2)}) %copy-start.7) | copy-done | bytes 65560
  11.4 0.1 copy.24
  11.5 0.0 copy-start.8
  11.5 0.0 copy-start.10
  11.5 0.8 %copy-done.8 = s32[128,128]{1,0:T(8,128)S(1)} copy-done((s32[128,128]{1,0:T(8,128)S(1)}, s32[128,128]{1,0:T(8,128)}, u32[]{:S(2)}) %copy-start.8) | copy-done | bytes 65560
  12.3 0.1 select_reduce_fusion.depth_ref
  12.5 0.1 fusion.5
  12.6 0.5 copy-done.1
  13.1 0.1 copy.42
  13.2 0.1 copy.45
  13.2 0.7 %copy-done.9 = f32[128,128]{1,0:T(8,128)S(1)} copy-done((f32[128,128]{1,0:T(8,128)S(1)}, f32[128,128]{1,0:T(8,128)}, u32[]{:S(2)}) %copy-start.9) | copy-done | bytes 65560
  13.9 0.1 copy.25
  14.0 0.0 copy-start.2
  14.1 0.8 %copy-done.2 = f32[128,128]{1,0:T(8,128)S(1)} copy-done((f32[128,128]{1,0:T(8,128)S(1)}, f32[128,128]{1,0:T(8,128)}, u32[]{:S(2)}) %copy-start.2) | copy-done | bytes 65560
  14.9 0.1 fusion.4
  15.0 0.1 copy.46
  15.0 0.8 %copy-done.3 = f32[128,128]{1,0:T(8,128)S(1)} copy-done((f32[128,128]{1,0:T(8,128)S(1)}, f32[128,128]{1,0:T(8,128)}, u32[]{:S(2)}) %copy-start.3) | copy-done | bytes 65560
  15.8 0.1 fusion.3
  15.9 0.1 copy.47
  15.9 0.1 copy.43
  16.0 0.1 copy.44
  16.1 0.1 fusion
  16.3 0.0 collective-permute-done.next_ref
  16.3 0.0 copy-start
  16.3 0.1 slice_bitcast_fusion
  16.4 0.6 copy-done
  17.0 0.1 copy.36
  17.1 6.2 %collective-permute-start.2 = (f32[304,128]{1,0:T(8,128)S(1)}, f32[304,128]{1,0:T(8,128)S(1)}, u32[]{:S(2)}, u32[]{:S(2)}) collective-permute-start(f32[304,128]{1,0:T(8,128)S(1)} %constant_dynamic-update-slice_fusion.9), channel_id=1, source_target_pairs={{0,15},{1,0},{2,1},{3,2},{4,3},{5,4},{6,5},{7,6},{8,7},{9,8},{10,9... | collective-permute-start | bytes 466952 | tf_op jit(solution)/shard_map/ppermute | solution.py:161
  23.3 0.1 copy.32
  23.4 1.9 %collective-permute-start.1 = (f32[304,128]{1,0:T(8,128)S(1)}, f32[304,128]{1,0:T(8,128)S(1)}, u32[]{:S(2)}, u32[]{:S(2)}) collective-permute-start(f32[304,128]{1,0:T(8,128)S(1)} %constant_dynamic-update-slice_fusion), channel_id=1, source_target_pairs={{0,1},{1,2},{2,3},{3,4},{4,5},{5,6},{6,7},{7,8},{8,9},{9,10},{10,1... | collective-permute-start | bytes 466952 | tf_op jit(solution)/shard_map/ppermute | solution.py:160
  25.3 0.6 sine_multiply_fusion.rot_ref
  25.9 0.7 %copy.37.sea_ref = f32[128,128]{1,0:T(8,128)} copy(f32[128,128]{0,1:T(8,128)S(1)} %convert_element_type.7) | data formatting | bytes 131072 | tf_op jit(solution)/shard_map/convert_element_type | solution.py:139
  26.6 0.7 %copy.38.retain_ref = f32[128,128]{1,0:T(8,128)} copy(f32[128,128]{0,1:T(8,128)S(1)} %add_divide_fusion) | data formatting | bytes 131072 | tf_op jit(solution)/shard_map/div | solution.py:145
  27.4 0.6 pad_maximum_fusion.trig_ref
  27.9 0.0 collective-permute-done.2.right_ref
  27.9 3.5 %collective-permute-done.1.left_ref = f32[304,128]{1,0:T(8,128)S(1)} collective-permute-done((f32[304,128]{1,0:T(8,128)S(1)}, f32[304,128]{1,0:T(8,128)S(1)}, u32[]{:S(2)}, u32[]{:S(2)}) %collective-permute-start.1) | collective-permute-done | bytes 155680 | tf_op jit(solution)/shard_map/ppermute | solution.py:160
  31.5 0.7 %copy-done.6 = f32[304,128]{1,0:T(8,128)} copy-done((f32[304,128]{1,0:T(8,128)}, f32[304,128]{1,0:T(8,128)S(1)}, u32[]{:S(2)}) %copy-start.6) | copy-done | bytes 155672
  32.1 5.2 %shard_map.94 = (f32[3,128,128]{2,1,0:T(8,128)}, f32[3,128,128]{2,1,0:T(8,128)}, f32[128,128]{1,0:T(8,128)}) custom-call(f32[16]{0:T(128)} %pad_maximum_fusion.trig_ref, f32[1,128]{1,0:T(1,128)} %sine_multiply_fusion.rot_ref, f32[3,128,128]{2,1,0:T(8,128)} %bitcast.67, f32[128,128]{1,0:T(8,128)} %copy.37.sea_ref, f32[128,128]{1,0:T(8,128)} %copy-done.1, ...), custom_call_target="tpu_custom_call" | custom-call | flops 23592960 | bytes 1572864 | tf_op jit(solution)/shard_map/pallas_call | solution.py:113
  37.4 5.6 %collective-permute-start.3 = (f32[3,128,128]{2,1,0:T(8,128)}, f32[3,128,128]{2,1,0:T(8,128)S(1)}, u32[]{:S(2)}, u32[]{:S(2)}) collective-permute-start(f32[3,128,128]{2,1,0:T(8,128)} %get-tuple-element.6), channel_id=1, source_target_pairs={{0,16},{16,32},{32,48},{48,64},{64,80},{80,96},{96,112},{112,128},... | collective-permute-start | bytes 589832 | tf_op jit(solution)/shard_map/ppermute | solution.py:28
  43.0 18.7 %all_to_all.5 = f32[32,4,128]{2,1,0:T(4,128)S(1)} all-to-all(f32[32,4,128]{2,1,0:T(4,128)} %bitcast.73), channel_id=1, replica_groups=mesh['tm'=32,'cell'=16] {'tm'}, dimensions={0} | all-to-all | bytes 131072 | tf_op jit(solution)/shard_map/all_to_all | solution.py:132
  61.7 0.6 reduce_sum.19
  62.3 0.7 %subtract_bitcast_fusion = f32[1,3,128,128]{3,2,1,0:T(8,128)} fusion(f32[3,128,128]{2,1,0:T(8,128)S(1)} %copy-done.4, f32[3,128,128]{2,1,0:T(8,128)S(1)} %collective-permute-done.3), kind=kLoop, calls=%fused_computation.4 | loop fusion | flops 49152 | bytes 589824 | tf_op jit(solution)/shard_map/broadcast_in_dim | solution.py:171
  (24 shorter events, 0.1 us)
Async XLA Ops:
  0.6 15.7 %collective-permute-start = (f32[3,128,128]{2,1,0:T(8,128)}, f32[3,128,128]{2,1,0:T(8,128)S(1)}, u32[]{:S(2)}, u32[]{:S(2)}) collective-permute-start(f32[3,128,128]{2,1,0:T(8,128)} %bitcast.66), channel_id=1, source_target_pairs={{0,496},{16,0},{32,16},{48,32},{64,48},{80,64},{96,80},{112,96},{1... | collective-permute-start | bytes 589832 | tf_op jit(solution)/shard_map/ppermute | solution.py:28
  10.6 0.8 %copy-start.7 = (s32[128,128]{1,0:T(8,128)S(1)}, s32[128,128]{1,0:T(8,128)}, u32[]{:S(2)}) copy-start(s32[128,128]{1,0:T(8,128)} %param.8) | copy-start | bytes 196612
  11.5 0.8 %copy-start.8 = (s32[128,128]{1,0:T(8,128)S(1)}, s32[128,128]{1,0:T(8,128)}, u32[]{:S(2)}) copy-start(s32[128,128]{1,0:T(8,128)} %param.9) | copy-start | bytes 196612
  11.5 0.8 %copy-start.10 = (f32[8]{0:T(128)S(1)}, f32[8]{0:T(128)}, u32[]{:S(2)}) copy-start(f32[8]{0:T(128)} %param.10) | copy-start | bytes 100
  12.5 0.6 %copy-start.1 = (f32[128,128]{1,0:T(8,128)}, f32[128,128]{1,0:T(8,128)S(1)}, u32[]{:S(2)}) copy-start(f32[128,128]{1,0:T(8,128)S(1)} %select_reduce_fusion.depth_ref) | copy-start | bytes 196612
  13.1 0.8 %copy-start.9 = (f32[128,128]{1,0:T(8,128)S(1)}, f32[128,128]{1,0:T(8,128)}, u32[]{:S(2)}) copy-start(f32[128,128]{1,0:T(8,128)} %param.11) | copy-start | bytes 196612
  14.0 0.8 %copy-start.2 = (f32[128,128]{1,0:T(8,128)S(1)}, f32[128,128]{1,0:T(8,128)}, u32[]{:S(2)}) copy-start(f32[128,128]{1,0:T(8,128)} %cos_ref.1) | copy-start | bytes 196612
  15.0 0.8 %copy-start.3 = (f32[128,128]{1,0:T(8,128)S(1)}, f32[128,128]{1,0:T(8,128)}, u32[]{:S(2)}) copy-start(f32[128,128]{1,0:T(8,128)} %sin_ref.1) | copy-start | bytes 196612
  16.3 0.7 %copy-start = (f32[3,128,128]{2,1,0:T(8,128)}, f32[3,128,128]{2,1,0:T(8,128)S(1)}, u32[]{:S(2)}) copy-start(f32[3,128,128]{2,1,0:T(8,128)S(1)} %collective-permute-done.next_ref) | copy-start | bytes 589828
  17.1 10.9 %collective-permute-start.2 = (f32[304,128]{1,0:T(8,128)S(1)}, f32[304,128]{1,0:T(8,128)S(1)}, u32[]{:S(2)}, u32[]{:S(2)}) collective-permute-start(f32[304,128]{1,0:T(8,128)S(1)} %constant_dynamic-update-slice_fusion.9), channel_id=1, source_target_pairs={{0,15},{1,0},{2,1},{3,2},{4,3},{5,4},{6,5},{7,6},{8,7},{9,8},{10,9... | collective-permute-start | bytes 466952 | tf_op jit(solution)/shard_map/ppermute | solution.py:161
  23.4 8.1 %collective-permute-start.1 = (f32[304,128]{1,0:T(8,128)S(1)}, f32[304,128]{1,0:T(8,128)S(1)}, u32[]{:S(2)}, u32[]{:S(2)}) collective-permute-start(f32[304,128]{1,0:T(8,128)S(1)} %constant_dynamic-update-slice_fusion), channel_id=1, source_target_pairs={{0,1},{1,2},{2,3},{3,4},{4,5},{5,6},{6,7},{7,8},{8,9},{9,10},{10,1... | collective-permute-start | bytes 466952 | tf_op jit(solution)/shard_map/ppermute | solution.py:160
  27.9 3.5 %copy-start.5 = (f32[304,128]{1,0:T(8,128)}, f32[304,128]{1,0:T(8,128)S(1)}, u32[]{:S(2)}) copy-start(f32[304,128]{1,0:T(8,128)S(1)} %collective-permute-done.2.right_ref) | copy-start | bytes 466948
  31.5 0.7 %copy-start.6 = (f32[304,128]{1,0:T(8,128)}, f32[304,128]{1,0:T(8,128)S(1)}, u32[]{:S(2)}) copy-start(f32[304,128]{1,0:T(8,128)S(1)} %collective-permute-done.1.left_ref) | copy-start | bytes 466948
  37.4 24.9 %copy-start.4 = (f32[3,128,128]{2,1,0:T(8,128)S(1)}, f32[3,128,128]{2,1,0:T(8,128)}, u32[]{:S(2)}) copy-start(f32[3,128,128]{2,1,0:T(8,128)} %get-tuple-element.7) | copy-start | bytes 589828
  37.4 24.9 %collective-permute-start.3 = (f32[3,128,128]{2,1,0:T(8,128)}, f32[3,128,128]{2,1,0:T(8,128)S(1)}, u32[]{:S(2)}, u32[]{:S(2)}) collective-permute-start(f32[3,128,128]{2,1,0:T(8,128)} %get-tuple-element.6), channel_id=1, source_target_pairs={{0,16},{16,32},{32,48},{48,64},{64,80},{80,96},{96,112},{112,128},... | collective-permute-start | bytes 589832 | tf_op jit(solution)/shard_map/ppermute | solution.py:28

commit v9 on v7

--- a/solution.py
+++ b/solution.py
@@ -125,6 +125,59 @@
     )(trig, rotation.reshape(1, rows), own, following, from_left, from_right)
 
 
+def pack_kernel(
+    depths_ref, start_hbm, mask_hbm, classes_hbm, drag_hbm, cos_hbm, sin_hbm,
+    own_ref, low_ref, high_ref, start_v, mask_v, classes_v, drag_v, cos_v, sin_v, sems, *, width
+):
+    copies = [
+        pltpu.make_async_copy(source, target, sems.at[index])
+        for index, (source, target) in enumerate(
+            [(start_hbm, start_v), (mask_hbm, mask_v), (classes_hbm, classes_v), (drag_hbm, drag_v),
+             (cos_hbm, cos_v), (sin_hbm, sin_v)]
+        )
+    ]
+    for copy in copies:
+        copy.start()
+    for copy in copies:
+        copy.wait()
+    classes = classes_v[...]
+    depth = jnp.zeros(classes.shape, jnp.float32)
+    for index in range(depths_ref.shape[0]):
+        depth = jnp.where(classes == index, depths_ref[index], depth)
+    fields = [
+        start_v[0, 0], start_v[0, 1], start_v[0, 2], mask_v[...].astype(jnp.float32), depth,
+        1.0 / (1.0 + drag_v[...]), cos_v[...], sin_v[...],
+    ]
+    tile = own_ref.shape[-1]
+    for index, field in enumerate(fields):
+        own_ref[index] = field
+        turned = jnp.transpose(field)
+        low_ref[index * width : (index + 1) * width, :] = turned[:width]
+        high_ref[index * width : (index + 1) * width, :] = turned[tile - width :]
+
+
+def pack(start_states, ocean_mask, depth_class, class_depth, drag_rate, tide_cos, tide_sin, width):
+    rows, tile = ocean_mask.shape
+    hbm = pl.BlockSpec(memory_space=pl.ANY)
+    vmem = pl.BlockSpec(memory_space=pltpu.VMEM)
+    strips = jax.ShapeDtypeStruct((8 * width, rows), jnp.float32)
+    return pl.pallas_call(
+        functools.partial(pack_kernel, width=width),
+        out_shape=(jax.ShapeDtypeStruct((8, rows, tile), jnp.float32), strips, strips),
+        in_specs=[pl.BlockSpec(memory_space=pltpu.SMEM)] + [hbm] * 6,
+        out_specs=(vmem, vmem, vmem),
+        scratch_shapes=[
+            pltpu.VMEM(start_states.shape, jnp.float32),
+            pltpu.VMEM((rows, tile), jnp.int32),
+            pltpu.VMEM((rows, tile), jnp.int32),
+            pltpu.VMEM((rows, tile), jnp.float32),
+            pltpu.VMEM((rows, tile), jnp.float32),
+            pltpu.VMEM((rows, tile), jnp.float32),
+            pltpu.SemaphoreType.DMA((6,)),
+        ],
+    )(class_depth, start_states, ocean_mask, depth_class, drag_rate, tide_cos, tide_sin)
+
+
 def reduce_scatter_rows(value, axis):
     count = lax.axis_size(axis)
     pieces = value.reshape((count, value.shape[0] // count, value.shape[1]))
@@ -135,27 +188,18 @@
     halo = 2 * STEPS
     slice_count = lax.axis_size("tm")
     slice_index = lax.axis_index("tm")
-    sea_mask = ocean_mask.astype(jnp.float32)
-    classes = jnp.arange(class_depth.shape[0], dtype=jnp.int32)
-    depth_field = jnp.sum(
-        jnp.where(depth_class[None] == classes[:, None, None], class_depth[:, None, None], 0.0),
-        axis=0,
-    )
-    retain = 1.0 / (1.0 + drag_rate)
     initial = start_states[0]
     cells = lax.axis_size("cell")
-    own = jnp.concatenate(
-        [initial, jnp.stack([sea_mask, depth_field, retain, tide_cos, tide_sin])], axis=0
+    own, low, high = pack(
+        start_states, ocean_mask, depth_class, class_depth, drag_rate, tide_cos, tide_sin, 2 * halo
     )
     fields, rows, width = own.shape
     following = from_behind(initial, "tm", -1)
 
     def strips(at_right):
-        mine = own[..., width - 2 * halo :] if at_right else own[..., : 2 * halo]
+        mine = high if at_right else low
         theirs = following[..., width - halo :] if at_right else following[..., :halo]
-        return jnp.concatenate(
-            [lane_dense(mine).reshape(-1, rows), lane_dense(theirs).reshape(-1, rows)], axis=0
-        )
+        return jnp.concatenate([mine, lane_dense(theirs).reshape(-1, rows)], axis=0)
 
     from_left = lax.ppermute(strips(True), "cell", ring_pairs(cells, 1))
     from_right = lax.ppermute(strips(False), "cell", ring_pairs(cells, -1))

time: 57.9 us -> 61.5 us (1.062)
  local copies, waits for them, and re-layouts: 6.88 us -> 2.34 us
  waiting for transfers between devices: 1.19 us -> 4.98 us
  Pallas kernels: 5.12 us -> 7.82 us
  starting transfers between devices: 22.1 us -> 23.7 us
    ppermute x1, waiting for transfers between devices: 0.01 us -> 4.97 us  [local(): from_left = lax.ppermute(strips(True), 'cell', ring_pairs(cells, 1))]
    unnamed x25 -> x12, local copies, waits for them, and re-layouts: 6.05 us -> 2.05 us
    pallas_call x0 -> x1, Pallas kernels: none -> 2.69 us  [pack(): pl.pallas_call(functools.partial(pack_kernel, width=width), out_shape=(ja...]
    ppermute x1, starting transfers between devices: 6.22 us -> 8.32 us  [local(): from_right = lax.ppermute(strips(False), 'cell', ring_pairs(cells, -1))]
    ppermute x1, waiting for transfers between devices: 1.18 us -> 0.01 us  [local(): from_right = lax.ppermute(strips(False), 'cell', ring_pairs(cells, -1))]
  transfers between devices with their start and end apart: 4 -> 4, of which waited for: 1 -> 1; matrix products, arithmetic and copies ran while one was open for 6% -> 3% of each run, Pallas kernels for 0% -> 4%
where the time goes in v9:
time: 61.5 us; the launch traced here: 61.1 us
  starting transfers between devices  23.7 us (39%)
  blocking collectives  19 us (31%)
  Pallas kernels  7.82 us (13%)
  waiting for transfers between devices  4.98 us (8%)
  other arithmetic  2.57 us (4%)
  local copies, waits for them, and re-layouts  2.34 us (4%)
  between operations  0.73 us (1%)
    all_to_all x1, blocking collectives, reduce_scatter_rows(): return jnp.sum(lax.all_to_all(pieces, axis, 0, 0, tiled=True), axis=0)  19 us
    ppermute x2, starting transfers between devices, from_behind(): return lax.ppermute(value, axis, ring_pairs(lax.axis_size(axis), steps))  13.4 us
    ppermute x1, starting transfers between devices, local(): from_right = lax.ppermute(strips(False), 'cell', ring_pairs(cells, -1))  8.32 us
    pallas_call x1, Pallas kernels, shooting(): pl.pallas_call(functools.partial(shooting_kernel, halo=halo, scale=scale)...  5.13 us
    ppermute x1, waiting for transfers between devices, local(): from_left = lax.ppermute(strips(True), 'cell', ring_pairs(cells, 1))  4.97 us
    pallas_call x1, Pallas kernels, pack(): pl.pallas_call(functools.partial(pack_kernel, width=width), out_shape=(ja...  2.69 us
    unnamed x12, local copies, waits for them, and re-layouts  2.05 us
    ppermute x1, starting transfers between devices, local(): from_left = lax.ppermute(strips(True), 'cell', ring_pairs(cells, 1))  1.92 us
  transfers between devices with their start and end apart: 4, of which 1 were waited for; matrix products, arithmetic and copies ran while one was open for 3% of the time, Pallas kernels for 4%

profile of v9, /device:TPU:1, one launch (start us, length us, event | category | flops | bytes accessed | tf_op | source)
XLA Modules:
  0.0 61.1 jit_solution(8487545833973110917)
XLA Ops:
  0.6 8.8 %collective-permute-start = (f32[3,128,128]{2,1,0:T(8,128)}, f32[3,128,128]{2,1,0:T(8,128)S(1)}, u32[]{:S(2)}, u32[]{:S(2)}) collective-permute-start(f32[3,128,128]{2,1,0:T(8,128)} %bitcast.11), channel_id=1, source_target_pairs={{0,496},{16,0},{32,16},{48,32},{64,48},{80,64},{96,80},{112,96},{1... | collective-permute-start | bytes 589832 | tf_op jit(solution)/shard_map/ppermute | solution.py:28
  9.4 2.7 %shard_map.94 = (f32[8,128,128]{2,1,0:T(8,128)}, f32[256,128]{1,0:T(8,128)}, f32[256,128]{1,0:T(8,128)}) custom-call(f32[8]{0:T(128)} %depths_ref.1, f32[1,3,128,128]{3,2,1,0:T(8,128)} %start_hbm.1, s32[128,128]{1,0:T(8,128)} %mask_hbm.1, s32[128,128]{1,0:T(8,128)} %classes_hbm.1, f32[128,128]{1,0:T(8,128)} %drag_hbm.1, f32[128,128]{1,0:T(8,128)} %cos_hbm.1, ...), custom_call_target="tpu_custom_call" | custom-call | tf_op jit(solution)/shard_map/pallas_call | solution.py:164
  12.2 0.0 collective-permute-done.next_ref
  12.2 0.0 copy-start
  12.2 0.1 slice_bitcast_fusion
  12.3 0.6 copy-done
  12.9 0.1 copy.11
  12.9 0.0 copy-start.5
  12.9 0.1 copy.10
  13.1 0.8 %copy-done.5 = f32[256,128]{1,0:T(8,128)S(1)} copy-done((f32[256,128]{1,0:T(8,128)S(1)}, f32[256,128]{1,0:T(8,128)}, u32[]{:S(2)}) %copy-start.5) | copy-done | bytes 131096
  13.9 0.0 copy-start.4
  13.9 8.3 %collective-permute-start.2 = (f32[304,128]{1,0:T(8,128)S(1)}, f32[304,128]{1,0:T(8,128)S(1)}, u32[]{:S(2)}, u32[]{:S(2)}) collective-permute-start(f32[304,128]{1,0:T(8,128)S(1)} %pad_maximum_fusion.1), channel_id=1, source_target_pairs={{0,15},{1,0},{2,1},{3,2},{4,3},{5,4},{6,5},{7,6},{8,7},{9,8},{10,9... | collective-permute-start | bytes 466952 | tf_op jit(solution)/shard_map/ppermute | solution.py:205
  22.2 0.0 copy-done.4
  22.3 1.9 %collective-permute-start.1 = (f32[304,128]{1,0:T(8,128)S(1)}, f32[304,128]{1,0:T(8,128)S(1)}, u32[]{:S(2)}, u32[]{:S(2)}) collective-permute-start(f32[304,128]{1,0:T(8,128)S(1)} %pad_maximum_fusion), channel_id=1, source_target_pairs={{0,1},{1,2},{2,3},{3,4},{4,5},{5,6},{6,7},{7,8},{8,9},{9,10},{10,1... | collective-permute-start | bytes 466952 | tf_op jit(solution)/shard_map/ppermute | solution.py:204
  24.2 0.6 sine_multiply_fusion.rot_ref
  24.8 0.6 pad_maximum_fusion.2.trig_ref
  25.4 0.0 collective-permute-done.2.right_ref
  25.4 0.0 copy-start.2
  25.4 5.0 %collective-permute-done.1.left_ref = f32[304,128]{1,0:T(8,128)S(1)} collective-permute-done((f32[304,128]{1,0:T(8,128)S(1)}, f32[304,128]{1,0:T(8,128)S(1)}, u32[]{:S(2)}, u32[]{:S(2)}) %collective-permute-start.1) | collective-permute-done | bytes 155680 | tf_op jit(solution)/shard_map/ppermute | solution.py:204
  30.3 0.0 copy-start.3
  30.3 0.0 copy-done.2
  30.3 0.7 %copy-done.3 = f32[304,128]{1,0:T(8,128)} copy-done((f32[304,128]{1,0:T(8,128)}, f32[304,128]{1,0:T(8,128)S(1)}, u32[]{:S(2)}) %copy-start.3) | copy-done | bytes 155672
  31.0 5.1 %shard_map.95 = (f32[3,128,128]{2,1,0:T(8,128)}, f32[3,128,128]{2,1,0:T(8,128)}, f32[128,128]{1,0:T(8,128)}) custom-call(f32[16]{0:T(128)} %pad_maximum_fusion.2.trig_ref, f32[1,128]{1,0:T(1,128)} %sine_multiply_fusion.rot_ref, f32[8,128,128]{2,1,0:T(8,128)} %get-tuple-element.9.own_ref, f32[3,128,128]{2,1,0:T(8,128)} %copy-done, f32[304,128]{1,0:T(8,128)} %copy-done.3, ...), custom_call_target="tpu_custom_call" | custom-call | flops 23592960 | bytes 1572864 | tf_op jit(solution)/shard_map/pallas_call | solution.py:112
  36.1 0.0 copy-start.1
  36.1 4.6 %collective-permute-start.3 = (f32[3,128,128]{2,1,0:T(8,128)}, f32[3,128,128]{2,1,0:T(8,128)S(1)}, u32[]{:S(2)}, u32[]{:S(2)}) collective-permute-start(f32[3,128,128]{2,1,0:T(8,128)} %get-tuple-element.12), channel_id=1, source_target_pairs={{0,16},{16,32},{32,48},{48,64},{64,80},{80,96},{96,112},{112,128},... | collective-permute-start | bytes 589832 | tf_op jit(solution)/shard_map/ppermute | solution.py:28
  40.8 19.0 %all_to_all.5 = f32[32,4,128]{2,1,0:T(4,128)S(1)} all-to-all(f32[32,4,128]{2,1,0:T(4,128)} %bitcast.14), channel_id=1, replica_groups=mesh['tm'=32,'cell'=16] {'tm'}, dimensions={0} | all-to-all | bytes 131072 | tf_op jit(solution)/shard_map/all_to_all | solution.py:184
  59.8 0.6 %reduce_sum.9 = f32[4,128]{1,0:T(4,128)} reduce(f32[32,4,128]{2,1,0:T(4,128)S(1)} %all_to_all.5, f32[]{:T(128)} %constant.22.clone.1), dimensions={0}, to_apply=%region_0.0 | reduce | flops 15872 | bytes 67588 | tf_op jit(solution)/shard_map/reduce_sum | solution.py:184
  60.4 0.0 collective-permute-done.3
  60.4 0.0 copy-done.1
  60.4 0.7 %subtract_bitcast_fusion = f32[1,3,128,128]{3,2,1,0:T(8,128)} fusion(f32[3,128,128]{2,1,0:T(8,128)S(1)} %copy-done.1, f32[3,128,128]{2,1,0:T(8,128)S(1)} %collective-permute-done.3), kind=kLoop, calls=%fused_computation.2 | loop fusion | flops 49152 | bytes 589824 | tf_op jit(solution)/shard_map/broadcast_in_dim | solution.py:215
  (3 shorter events, 0.1 us)
Async XLA Ops:
  0.6 11.5 %collective-permute-start = (f32[3,128,128]{2,1,0:T(8,128)}, f32[3,128,128]{2,1,0:T(8,128)S(1)}, u32[]{:S(2)}, u32[]{:S(2)}) collective-permute-start(f32[3,128,128]{2,1,0:T(8,128)} %bitcast.11), channel_id=1, source_target_pairs={{0,496},{16,0},{32,16},{48,32},{64,48},{80,64},{96,80},{112,96},{1... | collective-permute-start | bytes 589832 | tf_op jit(solution)/shard_map/ppermute | solution.py:28
  12.2 0.7 %copy-start = (f32[3,128,128]{2,1,0:T(8,128)}, f32[3,128,128]{2,1,0:T(8,128)S(1)}, u32[]{:S(2)}) copy-start(f32[3,128,128]{2,1,0:T(8,128)S(1)} %collective-permute-done.next_ref) | copy-start | bytes 589828
  12.9 0.9 %copy-start.5 = (f32[256,128]{1,0:T(8,128)S(1)}, f32[256,128]{1,0:T(8,128)}, u32[]{:S(2)}) copy-start(f32[256,128]{1,0:T(8,128)} %get-tuple-element.11) | copy-start | bytes 393220
  13.9 8.3 %copy-start.4 = (f32[256,128]{1,0:T(8,128)S(1)}, f32[256,128]{1,0:T(8,128)}, u32[]{:S(2)}) copy-start(f32[256,128]{1,0:T(8,128)} %get-tuple-element.10) | copy-start | bytes 393220
  13.9 11.5 %collective-permute-start.2 = (f32[304,128]{1,0:T(8,128)S(1)}, f32[304,128]{1,0:T(8,128)S(1)}, u32[]{:S(2)}, u32[]{:S(2)}) collective-permute-start(f32[304,128]{1,0:T(8,128)S(1)} %pad_maximum_fusion.1), channel_id=1, source_target_pairs={{0,15},{1,0},{2,1},{3,2},{4,3},{5,4},{6,5},{7,6},{8,7},{9,8},{10,9... | collective-permute-start | bytes 466952 | tf_op jit(solution)/shard_map/ppermute | solution.py:205
  22.3 8.1 %collective-permute-start.1 = (f32[304,128]{1,0:T(8,128)S(1)}, f32[304,128]{1,0:T(8,128)S(1)}, u32[]{:S(2)}, u32[]{:S(2)}) collective-permute-start(f32[304,128]{1,0:T(8,128)S(1)} %pad_maximum_fusion), channel_id=1, source_target_pairs={{0,1},{1,2},{2,3},{3,4},{4,5},{5,6},{6,7},{7,8},{8,9},{9,10},{10,1... | collective-permute-start | bytes 466952 | tf_op jit(solution)/shard_map/ppermute | solution.py:204
  25.4 5.0 %copy-start.2 = (f32[304,128]{1,0:T(8,128)}, f32[304,128]{1,0:T(8,128)S(1)}, u32[]{:S(2)}) copy-start(f32[304,128]{1,0:T(8,128)S(1)} %collective-permute-done.2.right_ref) | copy-start | bytes 466948
  30.3 0.7 %copy-start.3 = (f32[304,128]{1,0:T(8,128)}, f32[304,128]{1,0:T(8,128)S(1)}, u32[]{:S(2)}) copy-start(f32[304,128]{1,0:T(8,128)S(1)} %collective-permute-done.1.left_ref) | copy-start | bytes 466948
  36.1 24.3 %copy-start.1 = (f32[3,128,128]{2,1,0:T(8,128)S(1)}, f32[3,128,128]{2,1,0:T(8,128)}, u32[]{:S(2)}) copy-start(f32[3,128,128]{2,1,0:T(8,128)} %get-tuple-element.13) | copy-start | bytes 589828
  36.1 24.3 %collective-permute-start.3 = (f32[3,128,128]{2,1,0:T(8,128)}, f32[3,128,128]{2,1,0:T(8,128)S(1)}, u32[]{:S(2)}, u32[]{:S(2)}) collective-permute-start(f32[3,128,128]{2,1,0:T(8,128)} %get-tuple-element.12), channel_id=1, source_target_pairs={{0,16},{16,32},{32,48},{48,64},{64,80},{80,96},{96,112},{112,128},... | collective-permute-start | bytes 589832 | tf_op jit(solution)/shard_map/ppermute | solution.py:28

commit v10 on v7

--- a/solution.py
+++ b/solution.py
@@ -163,11 +163,11 @@
     phases = (slice_index * STEPS + jnp.arange(STEPS)).astype(jnp.float32) * phase_unit
     trig = jnp.concatenate([jnp.cos(phases), jnp.sin(phases)])
     defect, pulled, drag_grad = shooting(
-        trig, coriolis(rows), own, following, from_left, from_right, halo, 1.0 / slice_count
+        trig, coriolis(rows), own, following, from_left, from_right, halo, 1.0
     )
     behind = from_behind(defect, "tm", 1)
     state_grad = pulled - behind
-    drag_grad = reduce_scatter_rows(drag_grad, "tm")
+    drag_grad = reduce_scatter_rows(drag_grad, "tm") / slice_count
     return (defect[None], state_grad[None], drag_grad)
 
 

time: 57.9 us -> 55.3 us (0.955)
  blocking collectives: 18.5 us -> 0 us
  starting transfers between devices: 22.1 us -> 32 us
  waiting for transfers between devices: 1.19 us -> 7.26 us
    all_to_all x1 -> x0, blocking collectives: 18.5 us -> none  [reduce_scatter_rows(): return jnp.sum(lax.all_to_all(pieces, axis, 0, 0, tiled=True), axis=0)]
    all_to_all x0 -> x1, starting transfers between devices: none -> 11.4 us  [reduce_scatter_rows(): return jnp.sum(lax.all_to_all(pieces, axis, 0, 0, tiled=True), axis=0)]
    all_to_all x0 -> x1, waiting for transfers between devices: none -> 6.03 us  [reduce_scatter_rows(): return jnp.sum(lax.all_to_all(pieces, axis, 0, 0, tiled=True), axis=0)]
    ppermute x2, starting transfers between devices: 13.9 us -> 12.5 us  [from_behind(): return lax.ppermute(value, axis, ring_pairs(lax.axis_size(axis), steps))]
    div x0 -> x1, other arithmetic: none -> 0.58 us  [local(): drag_grad = reduce_scatter_rows(drag_grad, 'tm') / slice_count]
  transfers between devices with their start and end apart: 4 -> 5, of which waited for: 1 -> 2; matrix products, arithmetic and copies ran while one was open for 6% -> 7% of each run, Pallas kernels for 0% -> 0%
where the time goes in v10:
time: 55.3 us; the launch traced here: 54.8 us
  starting transfers between devices  32 us (58%)
  waiting for transfers between devices  7.26 us (13%)
  local copies, waits for them, and re-layouts  6.87 us (12%)
  Pallas kernels  5.11 us (9%)
  other arithmetic  2.75 us (5%)
  between operations  0.81 us (1%)
    ppermute x2, starting transfers between devices, from_behind(): return lax.ppermute(value, axis, ring_pairs(lax.axis_size(axis), steps))  12.5 us
    all_to_all x1, starting transfers between devices, reduce_scatter_rows(): return jnp.sum(lax.all_to_all(pieces, axis, 0, 0, tiled=True), axis=0)  11.4 us
    ppermute x1, starting transfers between devices, local(): from_right = lax.ppermute(strips(False), 'cell', ring_pairs(cells, -1))  6.22 us
    unnamed x25, local copies, waits for them, and re-layouts  6.05 us
    all_to_all x1, waiting for transfers between devices, reduce_scatter_rows(): return jnp.sum(lax.all_to_all(pieces, axis, 0, 0, tiled=True), axis=0)  6.03 us
    pallas_call x1, Pallas kernels, shooting(): pl.pallas_call(functools.partial(shooting_kernel, halo=halo, scale=scale)...  5.11 us
    ppermute x1, starting transfers between devices, local(): from_left = lax.ppermute(strips(True), 'cell', ring_pairs(cells, 1))  1.92 us
    ppermute x1, waiting for transfers between devices, local(): from_right = lax.ppermute(strips(False), 'cell', ring_pairs(cells, -1))  1.22 us
  transfers between devices with their start and end apart: 5, of which 2 were waited for; matrix products, arithmetic and copies ran while one was open for 7% of the time, Pallas kernels for 0%

profile of v10, /device:TPU:1, one launch (start us, length us, event | category | flops | bytes accessed | tf_op | source)
XLA Modules:
  0.0 54.8 jit_solution(5027073213560345314)
XLA Ops:
  0.6 0.0 copy-start.5
  0.6 8.9 %collective-permute-start = (f32[3,128,128]{2,1,0:T(8,128)}, f32[3,128,128]{2,1,0:T(8,128)S(1)}, u32[]{:S(2)}, u32[]{:S(2)}) collective-permute-start(f32[3,128,128]{2,1,0:T(8,128)} %bitcast.30), channel_id=1, source_target_pairs={{0,496},{16,0},{32,16},{48,32},{64,48},{80,64},{96,80},{112,96},{1... | collective-permute-start | bytes 589832 | tf_op jit(solution)/shard_map/ppermute | solution.py:28
  9.6 0.9 %constant_dynamic-update-slice_fusion = f32[8,128,128]{2,1,0:T(8,128)S(1)} fusion(f32[1,3,128,128]{3,2,1,0:T(8,128)} %param.7), kind=kLoop, calls=%fused_computation.14 | loop fusion | bytes 393216
  10.5 0.0 copy-done.5
  10.5 0.0 copy-start.6
  10.5 0.0 copy-start.10
  10.6 0.8 %copy-done.6 = s32[128,128]{1,0:T(8,128)S(1)} copy-done((s32[128,128]{1,0:T(8,128)S(1)}, s32[128,128]{1,0:T(8,128)}, u32[]{:S(2)}) %copy-start.6) | copy-done | bytes 65560
  11.4 0.0 copy-done.10
  11.4 0.1 select_reduce_fusion
  11.5 0.0 copy-start.7
  11.5 0.8 %copy-done.7 = f32[128,128]{1,0:T(8,128)S(1)} copy-done((f32[128,128]{1,0:T(8,128)S(1)}, f32[128,128]{1,0:T(8,128)}, u32[]{:S(2)}) %copy-start.7) | copy-done | bytes 65560
  12.3 0.0 copy-start.8
  12.3 0.8 %copy-done.8 = f32[128,128]{1,0:T(8,128)S(1)} copy-done((f32[128,128]{1,0:T(8,128)S(1)}, f32[128,128]{1,0:T(8,128)}, u32[]{:S(2)}) %copy-start.8) | copy-done | bytes 65560
  13.2 0.0 copy-start.9
  13.2 0.8 %copy-done.9 = f32[128,128]{1,0:T(8,128)S(1)} copy-done((f32[128,128]{1,0:T(8,128)S(1)}, f32[128,128]{1,0:T(8,128)}, u32[]{:S(2)}) %copy-start.9) | copy-done | bytes 65560
  14.0 0.0 copy-start
  14.0 0.2 slice_bitcast_fusion
  14.2 0.6 %copy-done = f32[8,128,128]{2,1,0:T(8,128)} copy-done((f32[8,128,128]{2,1,0:T(8,128)}, f32[8,128,128]{2,1,0:T(8,128)S(1)}, u32[]{:S(2)}) %copy-start) | copy-done | bytes 524312
  14.8 0.2 copy.14
  15.0 0.2 copy.16
  15.2 0.0 collective-permute-done.next_ref
  15.2 0.0 copy-start.1
  15.2 0.1 slice_bitcast_fusion.2
  15.3 0.6 %copy-done.1 = f32[3,128,128]{2,1,0:T(8,128)} copy-done((f32[3,128,128]{2,1,0:T(8,128)}, f32[3,128,128]{2,1,0:T(8,128)S(1)}, u32[]{:S(2)}) %copy-start.1) | copy-done | bytes 196632
  15.9 0.1 copy.15
  16.0 1.9 %collective-permute-start.1 = (f32[304,128]{1,0:T(8,128)S(1)}, f32[304,128]{1,0:T(8,128)S(1)}, u32[]{:S(2)}, u32[]{:S(2)}) collective-permute-start(f32[304,128]{1,0:T(8,128)S(1)} %pad_maximum_fusion), channel_id=1, source_target_pairs={{0,1},{1,2},{2,3},{3,4},{4,5},{5,6},{6,7},{7,8},{8,9},{9,10},{10,1... | collective-permute-start | bytes 466952 | tf_op jit(solution)/shard_map/ppermute | solution.py:160
  17.9 0.1 copy.17
  18.1 6.2 %collective-permute-start.2 = (f32[304,128]{1,0:T(8,128)S(1)}, f32[304,128]{1,0:T(8,128)S(1)}, u32[]{:S(2)}, u32[]{:S(2)}) collective-permute-start(f32[304,128]{1,0:T(8,128)S(1)} %pad_maximum_fusion.1), channel_id=1, source_target_pairs={{0,15},{1,0},{2,1},{3,2},{4,3},{5,4},{6,5},{7,6},{8,7},{9,8},{10,9... | collective-permute-start | bytes 466952 | tf_op jit(solution)/shard_map/ppermute | solution.py:161
  24.3 0.6 %sine_multiply_fusion.rot_ref = f32[1,128]{1,0:T(1,128)} fusion(), kind=kLoop, calls=%fused_computation.17 | loop fusion | flops 640 | bytes 512 | tf_op jit(solution)/shard_map/mul | solution.py:33
  24.9 0.6 %pad_maximum_fusion.2.trig_ref = f32[16]{0:T(128)} fusion(f32[8]{0:T(128)S(1)} %get-tuple-element.13, f32[8]{0:T(128)S(1)} %get-tuple-element.14), kind=kLoop, calls=%fused_computation.16 | loop fusion | flops 16 | bytes 128 | tf_op jit(solution)/shard_map/concatenate | solution.py:164
  25.5 0.0 collective-permute-done.1.left_ref
  25.5 0.0 copy-start.3
  25.5 1.2 %collective-permute-done.2.right_ref = f32[304,128]{1,0:T(8,128)S(1)} collective-permute-done((f32[304,128]{1,0:T(8,128)S(1)}, f32[304,128]{1,0:T(8,128)S(1)}, u32[]{:S(2)}, u32[]{:S(2)}) %collective-permute-start.2) | collective-permute-done | bytes 155680 | tf_op jit(solution)/shard_map/ppermute | solution.py:161
  26.7 0.0 copy-done.3
  26.7 0.0 copy-start.4
  26.7 0.7 %copy-done.4 = f32[304,128]{1,0:T(8,128)} copy-done((f32[304,128]{1,0:T(8,128)}, f32[304,128]{1,0:T(8,128)S(1)}, u32[]{:S(2)}) %copy-start.4) | copy-done | bytes 155672
  27.4 5.1 %shard_map.94 = (f32[3,128,128]{2,1,0:T(8,128)}, f32[3,128,128]{2,1,0:T(8,128)}, f32[128,128]{1,0:T(8,128)}) custom-call(f32[16]{0:T(128)} %pad_maximum_fusion.2.trig_ref, f32[1,128]{1,0:T(1,128)} %sine_multiply_fusion.rot_ref, f32[8,128,128]{2,1,0:T(8,128)} %copy-done, f32[3,128,128]{2,1,0:T(8,128)} %copy-done.1, f32[304,128]{1,0:T(8,128)} %copy-done.3, ...), custom_call_target="tpu_custom_call" | custom-call | flops 23592960 | bytes 1572864 | tf_op jit(solution)/shard_map/pallas_call | solution.py:112
  32.5 0.0 copy-start.2
  32.5 11.4 %all-to-all-start = ((f32[32,4,128]{2,1,0:T(4,128)}), f32[32,4,128]{2,1,0:T(4,128)S(1)}, u32[]{:S(2)}, u32[]{:S(2)}) async-start(f32[32,4,128]{2,1,0:T(4,128)} %bitcast.33), calls=%async_computation | async-start | bytes 131072 | tf_op jit(solution)/shard_map/all_to_all | solution.py:131
  43.8 3.5 %collective-permute-start.3 = (f32[3,128,128]{2,1,0:T(8,128)}, f32[3,128,128]{2,1,0:T(8,128)S(1)}, u32[]{:S(2)}, u32[]{:S(2)}) collective-permute-start(f32[3,128,128]{2,1,0:T(8,128)} %get-tuple-element.6), channel_id=1, source_target_pairs={{0,16},{16,32},{32,48},{48,64},{64,80},{80,96},{96,112},{112,128},... | collective-permute-start | bytes 589832 | tf_op jit(solution)/shard_map/ppermute | solution.py:28
  47.4 6.0 %all-to-all-done = f32[32,4,128]{2,1,0:T(4,128)S(1)} async-done(((f32[32,4,128]{2,1,0:T(4,128)}), f32[32,4,128]{2,1,0:T(4,128)S(1)}, u32[]{:S(2)}, u32[]{:S(2)}) %all-to-all-start) | async-done | bytes 65568 | tf_op jit(solution)/shard_map/all_to_all | solution.py:131
  53.5 0.6 %broadcast_multiply_fusion = f32[4,128]{1,0:T(4,128)} fusion(f32[4,128]{1,0:T(4,128)S(1)} %reduce_sum.19), kind=kLoop, calls=%fused_computation.15 | loop fusion | flops 512 | bytes 4096 | tf_op jit(solution)/shard_map/div | solution.py:170
  54.1 0.0 collective-permute-done.3
  54.1 0.0 copy-done.2
  54.1 0.7 %subtract_bitcast_fusion = f32[1,3,128,128]{3,2,1,0:T(8,128)} fusion(f32[3,128,128]{2,1,0:T(8,128)S(1)} %copy-done.2, f32[3,128,128]{2,1,0:T(8,128)S(1)} %collective-permute-done.3), kind=kLoop, calls=%fused_computation.6 | loop fusion | flops 49152 | bytes 589824 | tf_op jit(solution)/shard_map/broadcast_in_dim | solution.py:171
  (9 shorter events, 0.2 us)
Async XLA Ops:
  0.6 9.9 %copy-start.5 = (s32[128,128]{1,0:T(8,128)S(1)}, s32[128,128]{1,0:T(8,128)}, u32[]{:S(2)}) copy-start(s32[128,128]{1,0:T(8,128)} %param.8) | copy-start | bytes 196612
  0.6 14.6 %collective-permute-start = (f32[3,128,128]{2,1,0:T(8,128)}, f32[3,128,128]{2,1,0:T(8,128)S(1)}, u32[]{:S(2)}, u32[]{:S(2)}) collective-permute-start(f32[3,128,128]{2,1,0:T(8,128)} %bitcast.30), channel_id=1, source_target_pairs={{0,496},{16,0},{32,16},{48,32},{64,48},{80,64},{96,80},{112,96},{1... | collective-permute-start | bytes 589832 | tf_op jit(solution)/shard_map/ppermute | solution.py:28
  10.5 0.8 %copy-start.6 = (s32[128,128]{1,0:T(8,128)S(1)}, s32[128,128]{1,0:T(8,128)}, u32[]{:S(2)}) copy-start(s32[128,128]{1,0:T(8,128)} %param.9) | copy-start | bytes 196612
  10.5 0.8 %copy-start.10 = (f32[8]{0:T(128)S(1)}, f32[8]{0:T(128)}, u32[]{:S(2)}) copy-start(f32[8]{0:T(128)} %param.10) | copy-start | bytes 100
  11.5 0.8 %copy-start.7 = (f32[128,128]{1,0:T(8,128)S(1)}, f32[128,128]{1,0:T(8,128)}, u32[]{:S(2)}) copy-start(f32[128,128]{1,0:T(8,128)} %param.11) | copy-start | bytes 196612
  12.3 0.8 %copy-start.8 = (f32[128,128]{1,0:T(8,128)S(1)}, f32[128,128]{1,0:T(8,128)}, u32[]{:S(2)}) copy-start(f32[128,128]{1,0:T(8,128)} %param.12) | copy-start | bytes 196612
  13.2 0.8 %copy-start.9 = (f32[128,128]{1,0:T(8,128)S(1)}, f32[128,128]{1,0:T(8,128)}, u32[]{:S(2)}) copy-start(f32[128,128]{1,0:T(8,128)} %param.13) | copy-start | bytes 196612
  14.0 0.8 %copy-start = (f32[8,128,128]{2,1,0:T(8,128)}, f32[8,128,128]{2,1,0:T(8,128)S(1)}, u32[]{:S(2)}) copy-start(f32[8,128,128]{2,1,0:T(8,128)S(1)} %bitcast_dynamic-update-slice_fusion.own_ref) | copy-start | bytes 1572868
  15.2 0.7 %copy-start.1 = (f32[3,128,128]{2,1,0:T(8,128)}, f32[3,128,128]{2,1,0:T(8,128)S(1)}, u32[]{:S(2)}) copy-start(f32[3,128,128]{2,1,0:T(8,128)S(1)} %collective-permute-done.next_ref) | copy-start | bytes 589828
  16.0 9.5 %collective-permute-start.1 = (f32[304,128]{1,0:T(8,128)S(1)}, f32[304,128]{1,0:T(8,128)S(1)}, u32[]{:S(2)}, u32[]{:S(2)}) collective-permute-start(f32[304,128]{1,0:T(8,128)S(1)} %pad_maximum_fusion), channel_id=1, source_target_pairs={{0,1},{1,2},{2,3},{3,4},{4,5},{5,6},{6,7},{7,8},{8,9},{9,10},{10,1... | collective-permute-start | bytes 466952 | tf_op jit(solution)/shard_map/ppermute | solution.py:160
  18.1 8.6 %collective-permute-start.2 = (f32[304,128]{1,0:T(8,128)S(1)}, f32[304,128]{1,0:T(8,128)S(1)}, u32[]{:S(2)}, u32[]{:S(2)}) collective-permute-start(f32[304,128]{1,0:T(8,128)S(1)} %pad_maximum_fusion.1), channel_id=1, source_target_pairs={{0,15},{1,0},{2,1},{3,2},{4,3},{5,4},{6,5},{7,6},{8,7},{9,8},{10,9... | collective-permute-start | bytes 466952 | tf_op jit(solution)/shard_map/ppermute | solution.py:161
  25.5 1.2 %copy-start.3 = (f32[304,128]{1,0:T(8,128)}, f32[304,128]{1,0:T(8,128)S(1)}, u32[]{:S(2)}) copy-start(f32[304,128]{1,0:T(8,128)S(1)} %collective-permute-done.1.left_ref) | copy-start | bytes 466948
  26.7 0.7 %copy-start.4 = (f32[304,128]{1,0:T(8,128)}, f32[304,128]{1,0:T(8,128)S(1)}, u32[]{:S(2)}) copy-start(f32[304,128]{1,0:T(8,128)S(1)} %collective-permute-done.2.right_ref) | copy-start | bytes 466948
  32.5 21.6 %copy-start.2 = (f32[3,128,128]{2,1,0:T(8,128)S(1)}, f32[3,128,128]{2,1,0:T(8,128)}, u32[]{:S(2)}) copy-start(f32[3,128,128]{2,1,0:T(8,128)} %get-tuple-element.7) | copy-start | bytes 589828
  32.5 21.0 %all-to-all-start = ((f32[32,4,128]{2,1,0:T(4,128)}), f32[32,4,128]{2,1,0:T(4,128)S(1)}, u32[]{:S(2)}, u32[]{:S(2)}) async-start(f32[32,4,128]{2,1,0:T(4,128)} %bitcast.33), calls=%async_computation | async-start | bytes 131072 | tf_op jit(solution)/shard_map/all_to_all | solution.py:131
  43.8 10.2 %collective-permute-start.3 = (f32[3,128,128]{2,1,0:T(8,128)}, f32[3,128,128]{2,1,0:T(8,128)S(1)}, u32[]{:S(2)}, u32[]{:S(2)}) collective-permute-start(f32[3,128,128]{2,1,0:T(8,128)} %get-tuple-element.6), channel_id=1, source_target_pairs={{0,16},{16,32},{32,48},{48,64},{64,80},{80,96},{96,112},{112,128},... | collective-permute-start | bytes 589832 | tf_op jit(solution)/shard_map/ppermute | solution.py:28

commit v11 on v10

--- a/solution.py
+++ b/solution.py
@@ -53,25 +53,42 @@
             [edge, left_ref[strip, :], jnp.transpose(next_ref[field]), right_ref[strip, :], edge], axis=0
         )
 
-    lane = lax.broadcasted_iota(jnp.int32, (span, rows), 1)
-    first, last = lane == 0, lane == rows - 1
-    inner = slice(wide, wide + tile)
+    masks = {}
 
     def cols_diff(q):
-        return pltpu.roll(q, span - 1, 0) - pltpu.roll(q, 1, 0)
+        count = q.shape[0]
+        return pltpu.roll(q, count - 1, 0) - pltpu.roll(q, 1, 0)
 
     def rows_diff(q):
+        count = q.shape[0]
+        if count not in masks:
+            lane = lax.broadcasted_iota(jnp.int32, (count, rows), 1)
+            masks[count] = (lane == 0, lane == rows - 1)
+        first, last = masks[count]
         upper = jnp.where(last, 0.0, pltpu.roll(q, rows - 1, 1))
         lower = jnp.where(first, 0.0, pltpu.roll(q, 1, 1))
         return upper - lower
 
+    def statics_at(low, high):
+        return [wide_ref[index, low:high, :] for index in range(3, 8)]
+
+    def cropped(values, cut):
+        return [value[cut : value.shape[0] - cut] for value in values]
+
+    cut = 2 * (STEPS // 2)
     half_flux, half_press = 0.5 * FLUX_RATE, 0.5 * PRESS_RATE
-    sea, depth, retain = wide_ref[3], wide_ref[4], wide_ref[5]
     rot = rot_ref[...]
+    low, high = 0, span
+    sea, depth, retain, cosine, sine = statics_at(low, high)
     keep = sea * retain
     height, east, north = wide_ref[0] * sea, wide_ref[1] * sea, wide_ref[2] * sea
     for step in range(STEPS):
-        force = trig_ref[step] * wide_ref[6] + trig_ref[STEPS + step] * wide_ref[7]
+        if step == STEPS // 2:
+            height, east, north = cropped((height, east, north), cut)
+            low, high = low + cut, high - cut
+            sea, depth, retain, cosine, sine = statics_at(low, high)
+            keep = sea * retain
+        force = trig_ref[step] * cosine + trig_ref[STEPS + step] * sine
         spread = cols_diff(depth * east) + rows_diff(depth * north)
         height = sea * (height - half_flux * spread)
         surface = height + force
@@ -79,17 +96,27 @@
             keep * (east - half_press * cols_diff(surface) + rot * north),
             keep * (north - half_press * rows_diff(surface) - rot * east),
         )
+        inner = slice(wide - low, wide - low + tile)
         stored_ref[step, 0] = east[inner]
         stored_ref[step, 1] = north[inner]
-    height = sea * (height - ahead_ref[0])
-    east = sea * (east - ahead_ref[1])
-    north = sea * (north - ahead_ref[2])
+    height = sea * (height - ahead_ref[0, low:high, :])
+    east = sea * (east - ahead_ref[1, low:high, :])
+    north = sea * (north - ahead_ref[2, low:high, :])
     defect_ref[0] = jnp.transpose(height[inner])
     defect_ref[1] = jnp.transpose(east[inner])
     defect_ref[2] = jnp.transpose(north[inner])
-    half_depth_flux = 0.5 * (FLUX_RATE * depth)
+    height, east, north = cropped((height, east, north), halo - low)
+    low, high = halo, span - halo
     drag = jnp.zeros((tile, rows), jnp.float32)
     for back in range(STEPS):
+        if back % (STEPS // 2) == 0:
+            if back:
+                height, east, north = cropped((height, east, north), cut)
+                low, high = low + cut, high - cut
+            sea, depth, retain, _, _ = statics_at(low, high)
+            keep = sea * retain
+            half_depth_flux = 0.5 * (FLUX_RATE * depth)
+            inner = slice(wide - low, wide - low + tile)
         step = STEPS - 1 - back
         east_part = keep * east
         north_part = keep * north

time: 55.3 us -> 55.2 us (level)
  no operation moved by 1% of the time
where the time goes in v11:
time: 55.2 us; the launch traced here: 54.7 us
  starting transfers between devices  32 us (58%)
  waiting for transfers between devices  7.26 us (13%)
  local copies, waits for them, and re-layouts  6.87 us (12%)
  Pallas kernels  5.04 us (9%)
  other arithmetic  2.75 us (5%)
  between operations  0.81 us (1%)
    ppermute x2, starting transfers between devices, from_behind(): return lax.ppermute(value, axis, ring_pairs(lax.axis_size(axis), steps))  12.5 us
    all_to_all x1, starting transfers between devices, reduce_scatter_rows(): return jnp.sum(lax.all_to_all(pieces, axis, 0, 0, tiled=True), axis=0)  11.4 us
    ppermute x1, starting transfers between devices, local(): from_right = lax.ppermute(strips(False), 'cell', ring_pairs(cells, -1))  6.22 us
    unnamed x25, local copies, waits for them, and re-layouts  6.05 us
    all_to_all x1, waiting for transfers between devices, reduce_scatter_rows(): return jnp.sum(lax.all_to_all(pieces, axis, 0, 0, tiled=True), axis=0)  6.03 us
    pallas_call x1, Pallas kernels, shooting(): pl.pallas_call(functools.partial(shooting_kernel, halo=halo, scale=scale)...  5.04 us
    ppermute x1, starting transfers between devices, local(): from_left = lax.ppermute(strips(True), 'cell', ring_pairs(cells, 1))  1.92 us
    ppermute x1, waiting for transfers between devices, local(): from_right = lax.ppermute(strips(False), 'cell', ring_pairs(cells, -1))  1.22 us
  transfers between devices with their start and end apart: 5, of which 2 were waited for; matrix products, arithmetic and copies ran while one was open for 7% of the time, Pallas kernels for 0%

profile of v11, /device:TPU:1, one launch (start us, length us, event | category | flops | bytes accessed | tf_op | source)
XLA Modules:
  0.0 54.7 jit_solution(8459369591893730116)
XLA Ops:
  0.6 0.0 copy-start.5
  0.6 8.9 %collective-permute-start = (f32[3,128,128]{2,1,0:T(8,128)}, f32[3,128,128]{2,1,0:T(8,128)S(1)}, u32[]{:S(2)}, u32[]{:S(2)}) collective-permute-start(f32[3,128,128]{2,1,0:T(8,128)} %bitcast.30), channel_id=1, source_target_pairs={{0,496},{16,0},{32,16},{48,32},{64,48},{80,64},{96,80},{112,96},{1... | collective-permute-start | bytes 589832 | tf_op jit(solution)/shard_map/ppermute | solution.py:28
  9.6 0.9 %constant_dynamic-update-slice_fusion = f32[8,128,128]{2,1,0:T(8,128)S(1)} fusion(f32[1,3,128,128]{3,2,1,0:T(8,128)} %param.7), kind=kLoop, calls=%fused_computation.14 | loop fusion | bytes 393216
  10.5 0.0 copy-done.5
  10.5 0.0 copy-start.6
  10.5 0.0 copy-start.10
  10.6 0.8 %copy-done.6 = s32[128,128]{1,0:T(8,128)S(1)} copy-done((s32[128,128]{1,0:T(8,128)S(1)}, s32[128,128]{1,0:T(8,128)}, u32[]{:S(2)}) %copy-start.6) | copy-done | bytes 65560
  11.4 0.0 copy-done.10
  11.4 0.1 select_reduce_fusion
  11.5 0.0 copy-start.7
  11.5 0.8 %copy-done.7 = f32[128,128]{1,0:T(8,128)S(1)} copy-done((f32[128,128]{1,0:T(8,128)S(1)}, f32[128,128]{1,0:T(8,128)}, u32[]{:S(2)}) %copy-start.7) | copy-done | bytes 65560
  12.3 0.0 copy-start.8
  12.3 0.8 %copy-done.8 = f32[128,128]{1,0:T(8,128)S(1)} copy-done((f32[128,128]{1,0:T(8,128)S(1)}, f32[128,128]{1,0:T(8,128)}, u32[]{:S(2)}) %copy-start.8) | copy-done | bytes 65560
  13.2 0.0 copy-start.9
  13.2 0.8 %copy-done.9 = f32[128,128]{1,0:T(8,128)S(1)} copy-done((f32[128,128]{1,0:T(8,128)S(1)}, f32[128,128]{1,0:T(8,128)}, u32[]{:S(2)}) %copy-start.9) | copy-done | bytes 65560
  14.0 0.0 copy-start
  14.0 0.2 slice_bitcast_fusion
  14.2 0.6 %copy-done = f32[8,128,128]{2,1,0:T(8,128)} copy-done((f32[8,128,128]{2,1,0:T(8,128)}, f32[8,128,128]{2,1,0:T(8,128)S(1)}, u32[]{:S(2)}) %copy-start) | copy-done | bytes 524312
  14.8 0.2 copy.14
  15.0 0.2 copy.16
  15.2 0.0 collective-permute-done.next_ref
  15.2 0.0 copy-start.1
  15.2 0.1 slice_bitcast_fusion.2
  15.3 0.6 %copy-done.1 = f32[3,128,128]{2,1,0:T(8,128)} copy-done((f32[3,128,128]{2,1,0:T(8,128)}, f32[3,128,128]{2,1,0:T(8,128)S(1)}, u32[]{:S(2)}) %copy-start.1) | copy-done | bytes 196632
  15.9 0.1 copy.15
  16.0 1.9 %collective-permute-start.1 = (f32[304,128]{1,0:T(8,128)S(1)}, f32[304,128]{1,0:T(8,128)S(1)}, u32[]{:S(2)}, u32[]{:S(2)}) collective-permute-start(f32[304,128]{1,0:T(8,128)S(1)} %pad_maximum_fusion), channel_id=1, source_target_pairs={{0,1},{1,2},{2,3},{3,4},{4,5},{5,6},{6,7},{7,8},{8,9},{9,10},{10,1... | collective-permute-start | bytes 466952 | tf_op jit(solution)/shard_map/ppermute | solution.py:187
  17.9 0.1 copy.17
  18.1 6.2 %collective-permute-start.2 = (f32[304,128]{1,0:T(8,128)S(1)}, f32[304,128]{1,0:T(8,128)S(1)}, u32[]{:S(2)}, u32[]{:S(2)}) collective-permute-start(f32[304,128]{1,0:T(8,128)S(1)} %pad_maximum_fusion.1), channel_id=1, source_target_pairs={{0,15},{1,0},{2,1},{3,2},{4,3},{5,4},{6,5},{7,6},{8,7},{9,8},{10,9... | collective-permute-start | bytes 466952 | tf_op jit(solution)/shard_map/ppermute | solution.py:188
  24.3 0.6 %sine_multiply_fusion.rot_ref = f32[1,128]{1,0:T(1,128)} fusion(), kind=kLoop, calls=%fused_computation.17 | loop fusion | flops 640 | bytes 512 | tf_op jit(solution)/shard_map/mul | solution.py:33
  24.9 0.6 %pad_maximum_fusion.2.trig_ref = f32[16]{0:T(128)} fusion(f32[8]{0:T(128)S(1)} %get-tuple-element.13, f32[8]{0:T(128)S(1)} %get-tuple-element.14), kind=kLoop, calls=%fused_computation.16 | loop fusion | flops 16 | bytes 128 | tf_op jit(solution)/shard_map/concatenate | solution.py:191
  25.5 0.0 collective-permute-done.1.left_ref
  25.5 0.0 copy-start.3
  25.5 1.2 %collective-permute-done.2.right_ref = f32[304,128]{1,0:T(8,128)S(1)} collective-permute-done((f32[304,128]{1,0:T(8,128)S(1)}, f32[304,128]{1,0:T(8,128)S(1)}, u32[]{:S(2)}, u32[]{:S(2)}) %collective-permute-start.2) | collective-permute-done | bytes 155680 | tf_op jit(solution)/shard_map/ppermute | solution.py:188
  26.7 0.0 copy-done.3
  26.7 0.0 copy-start.4
  26.7 0.7 %copy-done.4 = f32[304,128]{1,0:T(8,128)} copy-done((f32[304,128]{1,0:T(8,128)}, f32[304,128]{1,0:T(8,128)S(1)}, u32[]{:S(2)}) %copy-start.4) | copy-done | bytes 155672
  27.4 5.0 %shard_map.94 = (f32[3,128,128]{2,1,0:T(8,128)}, f32[3,128,128]{2,1,0:T(8,128)}, f32[128,128]{1,0:T(8,128)}) custom-call(f32[16]{0:T(128)} %pad_maximum_fusion.2.trig_ref, f32[1,128]{1,0:T(1,128)} %sine_multiply_fusion.rot_ref, f32[8,128,128]{2,1,0:T(8,128)} %copy-done, f32[3,128,128]{2,1,0:T(8,128)} %copy-done.1, f32[304,128]{1,0:T(8,128)} %copy-done.3, ...), custom_call_target="tpu_custom_call" | custom-call | flops 23592960 | bytes 1572864 | tf_op jit(solution)/shard_map/pallas_call | solution.py:139
  32.4 0.0 copy-start.2
  32.4 11.4 %all-to-all-start = ((f32[32,4,128]{2,1,0:T(4,128)}), f32[32,4,128]{2,1,0:T(4,128)S(1)}, u32[]{:S(2)}, u32[]{:S(2)}) async-start(f32[32,4,128]{2,1,0:T(4,128)} %bitcast.33), calls=%async_computation | async-start | bytes 131072 | tf_op jit(solution)/shard_map/all_to_all | solution.py:158
  43.8 3.5 %collective-permute-start.3 = (f32[3,128,128]{2,1,0:T(8,128)}, f32[3,128,128]{2,1,0:T(8,128)S(1)}, u32[]{:S(2)}, u32[]{:S(2)}) collective-permute-start(f32[3,128,128]{2,1,0:T(8,128)} %get-tuple-element.6), channel_id=1, source_target_pairs={{0,16},{16,32},{32,48},{48,64},{64,80},{80,96},{96,112},{112,128},... | collective-permute-start | bytes 589832 | tf_op jit(solution)/shard_map/ppermute | solution.py:28
  47.3 6.0 %all-to-all-done = f32[32,4,128]{2,1,0:T(4,128)S(1)} async-done(((f32[32,4,128]{2,1,0:T(4,128)}), f32[32,4,128]{2,1,0:T(4,128)S(1)}, u32[]{:S(2)}, u32[]{:S(2)}) %all-to-all-start) | async-done | bytes 65568 | tf_op jit(solution)/shard_map/all_to_all | solution.py:158
  53.4 0.6 %broadcast_multiply_fusion = f32[4,128]{1,0:T(4,128)} fusion(f32[4,128]{1,0:T(4,128)S(1)} %reduce_sum.19), kind=kLoop, calls=%fused_computation.15 | loop fusion | flops 512 | bytes 4096 | tf_op jit(solution)/shard_map/div | solution.py:197
  54.0 0.0 collective-permute-done.3
  54.0 0.0 copy-done.2
  54.0 0.7 %subtract_bitcast_fusion = f32[1,3,128,128]{3,2,1,0:T(8,128)} fusion(f32[3,128,128]{2,1,0:T(8,128)S(1)} %copy-done.2, f32[3,128,128]{2,1,0:T(8,128)S(1)} %collective-permute-done.3), kind=kLoop, calls=%fused_computation.6 | loop fusion | flops 49152 | bytes 589824 | tf_op jit(solution)/shard_map/broadcast_in_dim | solution.py:198
  (9 shorter events, 0.2 us)
Async XLA Ops:
  0.6 9.9 %copy-start.5 = (s32[128,128]{1,0:T(8,128)S(1)}, s32[128,128]{1,0:T(8,128)}, u32[]{:S(2)}) copy-start(s32[128,128]{1,0:T(8,128)} %param.8) | copy-start | bytes 196612
  0.6 14.6 %collective-permute-start = (f32[3,128,128]{2,1,0:T(8,128)}, f32[3,128,128]{2,1,0:T(8,128)S(1)}, u32[]{:S(2)}, u32[]{:S(2)}) collective-permute-start(f32[3,128,128]{2,1,0:T(8,128)} %bitcast.30), channel_id=1, source_target_pairs={{0,496},{16,0},{32,16},{48,32},{64,48},{80,64},{96,80},{112,96},{1... | collective-permute-start | bytes 589832 | tf_op jit(solution)/shard_map/ppermute | solution.py:28
  10.5 0.8 %copy-start.6 = (s32[128,128]{1,0:T(8,128)S(1)}, s32[128,128]{1,0:T(8,128)}, u32[]{:S(2)}) copy-start(s32[128,128]{1,0:T(8,128)} %param.9) | copy-start | bytes 196612
  10.5 0.8 %copy-start.10 = (f32[8]{0:T(128)S(1)}, f32[8]{0:T(128)}, u32[]{:S(2)}) copy-start(f32[8]{0:T(128)} %param.10) | copy-start | bytes 100
  11.5 0.8 %copy-start.7 = (f32[128,128]{1,0:T(8,128)S(1)}, f32[128,128]{1,0:T(8,128)}, u32[]{:S(2)}) copy-start(f32[128,128]{1,0:T(8,128)} %param.11) | copy-start | bytes 196612
  12.3 0.8 %copy-start.8 = (f32[128,128]{1,0:T(8,128)S(1)}, f32[128,128]{1,0:T(8,128)}, u32[]{:S(2)}) copy-start(f32[128,128]{1,0:T(8,128)} %param.12) | copy-start | bytes 196612
  13.2 0.8 %copy-start.9 = (f32[128,128]{1,0:T(8,128)S(1)}, f32[128,128]{1,0:T(8,128)}, u32[]{:S(2)}) copy-start(f32[128,128]{1,0:T(8,128)} %param.13) | copy-start | bytes 196612
  14.0 0.8 %copy-start = (f32[8,128,128]{2,1,0:T(8,128)}, f32[8,128,128]{2,1,0:T(8,128)S(1)}, u32[]{:S(2)}) copy-start(f32[8,128,128]{2,1,0:T(8,128)S(1)} %bitcast_dynamic-update-slice_fusion.own_ref) | copy-start | bytes 1572868
  15.2 0.7 %copy-start.1 = (f32[3,128,128]{2,1,0:T(8,128)}, f32[3,128,128]{2,1,0:T(8,128)S(1)}, u32[]{:S(2)}) copy-start(f32[3,128,128]{2,1,0:T(8,128)S(1)} %collective-permute-done.next_ref) | copy-start | bytes 589828
  16.0 9.5 %collective-permute-start.1 = (f32[304,128]{1,0:T(8,128)S(1)}, f32[304,128]{1,0:T(8,128)S(1)}, u32[]{:S(2)}, u32[]{:S(2)}) collective-permute-start(f32[304,128]{1,0:T(8,128)S(1)} %pad_maximum_fusion), channel_id=1, source_target_pairs={{0,1},{1,2},{2,3},{3,4},{4,5},{5,6},{6,7},{7,8},{8,9},{9,10},{10,1... | collective-permute-start | bytes 466952 | tf_op jit(solution)/shard_map/ppermute | solution.py:187
  18.1 8.6 %collective-permute-start.2 = (f32[304,128]{1,0:T(8,128)S(1)}, f32[304,128]{1,0:T(8,128)S(1)}, u32[]{:S(2)}, u32[]{:S(2)}) collective-permute-start(f32[304,128]{1,0:T(8,128)S(1)} %pad_maximum_fusion.1), channel_id=1, source_target_pairs={{0,15},{1,0},{2,1},{3,2},{4,3},{5,4},{6,5},{7,6},{8,7},{9,8},{10,9... | collective-permute-start | bytes 466952 | tf_op jit(solution)/shard_map/ppermute | solution.py:188
  25.5 1.2 %copy-start.3 = (f32[304,128]{1,0:T(8,128)}, f32[304,128]{1,0:T(8,128)S(1)}, u32[]{:S(2)}) copy-start(f32[304,128]{1,0:T(8,128)S(1)} %collective-permute-done.1.left_ref) | copy-start | bytes 466948
  26.7 0.7 %copy-start.4 = (f32[304,128]{1,0:T(8,128)}, f32[304,128]{1,0:T(8,128)S(1)}, u32[]{:S(2)}) copy-start(f32[304,128]{1,0:T(8,128)S(1)} %collective-permute-done.2.right_ref) | copy-start | bytes 466948
  32.4 21.6 %copy-start.2 = (f32[3,128,128]{2,1,0:T(8,128)S(1)}, f32[3,128,128]{2,1,0:T(8,128)}, u32[]{:S(2)}) copy-start(f32[3,128,128]{2,1,0:T(8,128)} %get-tuple-element.7) | copy-start | bytes 589828
  32.4 21.0 %all-to-all-start = ((f32[32,4,128]{2,1,0:T(4,128)}), f32[32,4,128]{2,1,0:T(4,128)S(1)}, u32[]{:S(2)}, u32[]{:S(2)}) async-start(f32[32,4,128]{2,1,0:T(4,128)} %bitcast.33), calls=%async_computation | async-start | bytes 131072 | tf_op jit(solution)/shard_map/all_to_all | solution.py:158
  43.8 10.2 %collective-permute-start.3 = (f32[3,128,128]{2,1,0:T(8,128)}, f32[3,128,128]{2,1,0:T(8,128)S(1)}, u32[]{:S(2)}, u32[]{:S(2)}) collective-permute-start(f32[3,128,128]{2,1,0:T(8,128)} %get-tuple-element.6), channel_id=1, source_target_pairs={{0,16},{16,32},{32,48},{48,64},{64,80},{80,96},{96,112},{112,128},... | collective-permute-start | bytes 589832 | tf_op jit(solution)/shard_map/ppermute | solution.py:28

commit v12 on v11

--- a/solution.py
+++ b/solution.py
@@ -152,10 +152,11 @@
     )(trig, rotation.reshape(1, rows), own, following, from_left, from_right)
 
 
-def reduce_scatter_rows(value, axis):
+def reduce_scatter_rows(value, axis, beside):
     count = lax.axis_size(axis)
     pieces = value.reshape((count, value.shape[0] // count, value.shape[1]))
-    return jnp.sum(lax.all_to_all(pieces, axis, 0, 0, tiled=True), axis=0)
+    gathered, beside = lax.optimization_barrier((lax.all_to_all(pieces, axis, 0, 0, tiled=True), beside))
+    return jnp.sum(gathered, axis=0), beside
 
 
 def local(start_states, ocean_mask, depth_class, class_depth, drag_rate, tide_cos, tide_sin):
@@ -193,8 +194,8 @@
         trig, coriolis(rows), own, following, from_left, from_right, halo, 1.0
     )
     behind = from_behind(defect, "tm", 1)
-    state_grad = pulled - behind
-    drag_grad = reduce_scatter_rows(drag_grad, "tm") / slice_count
+    drag_grad, state_grad = reduce_scatter_rows(drag_grad, "tm", pulled - behind)
+    drag_grad = drag_grad / slice_count
     return (defect[None], state_grad[None], drag_grad)
 
 

time: 55.2 us -> 57 us (1.033)
  waiting for transfers between devices: 7.26 us -> 9.19 us
  starting transfers between devices: 32 us -> 30.9 us
  other arithmetic: 2.75 us -> 3.65 us
    all_to_all x1, starting transfers between devices: 11.4 us -> 8.9 us  [reduce_scatter_rows(): lax.all_to_all(pieces, axis, 0, 0, tiled=True)]
    all_to_all x1, waiting for transfers between devices: 6.03 us -> 7.94 us  [reduce_scatter_rows(): lax.all_to_all(pieces, axis, 0, 0, tiled=True)]
    sub x0 -> x1, other arithmetic: none -> 1.63 us  [local(): pulled - behind]
    ppermute x2, starting transfers between devices: 12.5 us -> 13.8 us  [from_behind(): return lax.ppermute(value, axis, ring_pairs(lax.axis_size(axis), steps))]
    broadcast_in_dim x1 -> x0, other arithmetic: 0.7 us -> none  [local(): return (defect[None], state_grad[None], drag_grad)]
    unnamed x25 -> x23, local copies, waits for them, and re-layouts: 6.05 us -> 6.04 us
  transfers between devices with their start and end apart: 5 -> 5, of which waited for: 2 -> 2; matrix products, arithmetic and copies ran while one was open for 7% -> 8% of each run, Pallas kernels for 0% -> 0%
where the time goes in v12:
time: 57 us; the launch traced here: 56.4 us
  starting transfers between devices  30.9 us (54%)
  waiting for transfers between devices  9.19 us (16%)
  local copies, waits for them, and re-layouts  6.86 us (12%)
  Pallas kernels  5.04 us (9%)
  other arithmetic  3.65 us (6%)
  between operations  0.81 us (1%)
    ppermute x2, starting transfers between devices, from_behind(): return lax.ppermute(value, axis, ring_pairs(lax.axis_size(axis), steps))  13.8 us
    all_to_all x1, starting transfers between devices, reduce_scatter_rows(): lax.all_to_all(pieces, axis, 0, 0, tiled=True)  8.9 us
    all_to_all x1, waiting for transfers between devices, reduce_scatter_rows(): lax.all_to_all(pieces, axis, 0, 0, tiled=True)  7.94 us
    ppermute x1, starting transfers between devices, local(): from_right = lax.ppermute(strips(False), 'cell', ring_pairs(cells, -1))  6.22 us
    unnamed x23, local copies, waits for them, and re-layouts  6.04 us
    pallas_call x1, Pallas kernels, shooting(): pl.pallas_call(functools.partial(shooting_kernel, halo=halo, scale=scale)...  5.04 us
    ppermute x1, starting transfers between devices, local(): from_left = lax.ppermute(strips(True), 'cell', ring_pairs(cells, 1))  1.92 us
    sub x1, other arithmetic, local(): pulled - behind  1.63 us
  transfers between devices with their start and end apart: 5, of which 2 were waited for; matrix products, arithmetic and copies ran while one was open for 8% of the time, Pallas kernels for 0%

profile of v12, /device:TPU:1, one launch (start us, length us, event | category | flops | bytes accessed | tf_op | source)
XLA Modules:
  0.0 56.4 jit_solution(18270923764911538694)
XLA Ops:
  0.6 0.0 copy-start.4
  0.6 8.9 %collective-permute-start = (f32[3,128,128]{2,1,0:T(8,128)}, f32[3,128,128]{2,1,0:T(8,128)S(1)}, u32[]{:S(2)}, u32[]{:S(2)}) collective-permute-start(f32[3,128,128]{2,1,0:T(8,128)} %bitcast.29), channel_id=1, source_target_pairs={{0,496},{16,0},{32,16},{48,32},{64,48},{80,64},{96,80},{112,96},{1... | collective-permute-start | bytes 589832 | tf_op jit(solution)/shard_map/ppermute | solution.py:28
  9.6 0.9 %constant_dynamic-update-slice_fusion = f32[8,128,128]{2,1,0:T(8,128)S(1)} fusion(f32[1,3,128,128]{3,2,1,0:T(8,128)} %param.7), kind=kLoop, calls=%fused_computation.13 | loop fusion | bytes 393216
  10.5 0.0 copy-done.4
  10.5 0.0 copy-start.5
  10.5 0.0 copy-start.9
  10.6 0.8 %copy-done.5 = s32[128,128]{1,0:T(8,128)S(1)} copy-done((s32[128,128]{1,0:T(8,128)S(1)}, s32[128,128]{1,0:T(8,128)}, u32[]{:S(2)}) %copy-start.5) | copy-done | bytes 65560
  11.4 0.0 copy-done.9
  11.4 0.1 select_reduce_fusion
  11.5 0.0 copy-start.6
  11.5 0.8 %copy-done.6 = f32[128,128]{1,0:T(8,128)S(1)} copy-done((f32[128,128]{1,0:T(8,128)S(1)}, f32[128,128]{1,0:T(8,128)}, u32[]{:S(2)}) %copy-start.6) | copy-done | bytes 65560
  12.3 0.0 copy-start.7
  12.3 0.8 %copy-done.7 = f32[128,128]{1,0:T(8,128)S(1)} copy-done((f32[128,128]{1,0:T(8,128)S(1)}, f32[128,128]{1,0:T(8,128)}, u32[]{:S(2)}) %copy-start.7) | copy-done | bytes 65560
  13.2 0.0 copy-start.8
  13.2 0.8 %copy-done.8 = f32[128,128]{1,0:T(8,128)S(1)} copy-done((f32[128,128]{1,0:T(8,128)S(1)}, f32[128,128]{1,0:T(8,128)}, u32[]{:S(2)}) %copy-start.8) | copy-done | bytes 65560
  14.0 0.0 copy-start
  14.0 0.2 slice_bitcast_fusion
  14.2 0.6 %copy-done = f32[8,128,128]{2,1,0:T(8,128)} copy-done((f32[8,128,128]{2,1,0:T(8,128)}, f32[8,128,128]{2,1,0:T(8,128)S(1)}, u32[]{:S(2)}) %copy-start) | copy-done | bytes 524312
  14.8 0.2 copy.14
  15.0 0.2 copy.16
  15.2 0.0 collective-permute-done.next_ref
  15.2 0.0 copy-start.1
  15.2 0.1 slice_bitcast_fusion.2
  15.3 0.6 copy-done.1
  15.9 0.1 copy.15
  16.0 1.9 %collective-permute-start.1 = (f32[304,128]{1,0:T(8,128)S(1)}, f32[304,128]{1,0:T(8,128)S(1)}, u32[]{:S(2)}, u32[]{:S(2)}) collective-permute-start(f32[304,128]{1,0:T(8,128)S(1)} %pad_maximum_fusion), channel_id=1, source_target_pairs={{0,1},{1,2},{2,3},{3,4},{4,5},{5,6},{6,7},{7,8},{8,9},{9,10},{10,1... | collective-permute-start | bytes 466952 | tf_op jit(solution)/shard_map/ppermute | solution.py:188
  17.9 0.1 copy.17
  18.1 6.2 %collective-permute-start.2 = (f32[304,128]{1,0:T(8,128)S(1)}, f32[304,128]{1,0:T(8,128)S(1)}, u32[]{:S(2)}, u32[]{:S(2)}) collective-permute-start(f32[304,128]{1,0:T(8,128)S(1)} %pad_maximum_fusion.1), channel_id=1, source_target_pairs={{0,15},{1,0},{2,1},{3,2},{4,3},{5,4},{6,5},{7,6},{8,7},{9,8},{10,9... | collective-permute-start | bytes 466952 | tf_op jit(solution)/shard_map/ppermute | solution.py:189
  24.3 0.6 %sine_multiply_fusion.rot_ref = f32[1,128]{1,0:T(1,128)} fusion(), kind=kLoop, calls=%fused_computation.16 | loop fusion | flops 640 | bytes 512 | tf_op jit(solution)/shard_map/mul | solution.py:33
  24.9 0.6 %pad_maximum_fusion.2.trig_ref = f32[16]{0:T(128)} fusion(f32[8]{0:T(128)S(1)} %get-tuple-element.17, f32[8]{0:T(128)S(1)} %get-tuple-element.18), kind=kLoop, calls=%fused_computation.15 | loop fusion | flops 16 | bytes 128 | tf_op jit(solution)/shard_map/concatenate | solution.py:192
  25.4 0.0 collective-permute-done.1.left_ref
  25.5 0.0 copy-start.2
  25.5 1.2 %collective-permute-done.2.right_ref = f32[304,128]{1,0:T(8,128)S(1)} collective-permute-done((f32[304,128]{1,0:T(8,128)S(1)}, f32[304,128]{1,0:T(8,128)S(1)}, u32[]{:S(2)}, u32[]{:S(2)}) %collective-permute-start.2) | collective-permute-done | bytes 155680 | tf_op jit(solution)/shard_map/ppermute | solution.py:189
  26.7 0.0 copy-done.2
  26.7 0.0 copy-start.3
  26.7 0.7 %copy-done.3 = f32[304,128]{1,0:T(8,128)} copy-done((f32[304,128]{1,0:T(8,128)}, f32[304,128]{1,0:T(8,128)S(1)}, u32[]{:S(2)}) %copy-start.3) | copy-done | bytes 155672
  27.4 5.0 %shard_map.94 = (f32[3,128,128]{2,1,0:T(8,128)}, f32[3,128,128]{2,1,0:T(8,128)}, f32[128,128]{1,0:T(8,128)}) custom-call(f32[16]{0:T(128)} %pad_maximum_fusion.2.trig_ref, f32[1,128]{1,0:T(1,128)} %sine_multiply_fusion.rot_ref, f32[8,128,128]{2,1,0:T(8,128)} %copy-done, f32[3,128,128]{2,1,0:T(8,128)} %copy-done.1, f32[304,128]{1,0:T(8,128)} %copy-done.2, ...), custom_call_target="tpu_custom_call" | custom-call | flops 23592960 | bytes 1572864 | tf_op jit(solution)/shard_map/pallas_call | solution.py:139
  32.4 4.9 %collective-permute-start.3 = (f32[3,128,128]{2,1,0:T(8,128)}, f32[3,128,128]{2,1,0:T(8,128)S(1)}, u32[]{:S(2)}, u32[]{:S(2)}) collective-permute-start(f32[3,128,128]{2,1,0:T(8,128)} %get-tuple-element.8), channel_id=1, source_target_pairs={{0,16},{16,32},{32,48},{48,64},{64,80},{80,96},{96,112},{112,128},... | collective-permute-start | bytes 589832 | tf_op jit(solution)/shard_map/ppermute | solution.py:28
  37.3 8.9 %all-to-all-start = ((f32[32,4,128]{2,1,0:T(4,128)}), f32[32,4,128]{2,1,0:T(4,128)S(1)}, u32[]{:S(2)}, u32[]{:S(2)}) async-start(f32[32,4,128]{2,1,0:T(4,128)} %bitcast.33), calls=%async_computation | async-start | bytes 131072 | tf_op jit(solution)/shard_map/all_to_all | solution.py:158
  46.2 0.0 collective-permute-done.3
  46.2 1.6 %sub.7 = f32[3,128,128]{2,1,0:T(8,128)} subtract(f32[3,128,128]{2,1,0:T(8,128)} %get-tuple-element.10, f32[3,128,128]{2,1,0:T(8,128)S(1)} %collective-permute-done.3) | non-fusion elementwise | flops 49152 | bytes 589824 | tf_op jit(solution)/shard_map/sub | solution.py:197
  47.8 7.9 %all-to-all-done = f32[32,4,128]{2,1,0:T(4,128)S(1)} async-done(((f32[32,4,128]{2,1,0:T(4,128)}), f32[32,4,128]{2,1,0:T(4,128)S(1)}, u32[]{:S(2)}, u32[]{:S(2)}) %all-to-all-start) | async-done | bytes 65568 | tf_op jit(solution)/shard_map/all_to_all | solution.py:158
  55.8 0.6 %broadcast_multiply_fusion = f32[4,128]{1,0:T(4,128)} fusion(f32[4,128]{1,0:T(4,128)S(1)} %reduce_sum.19), kind=kLoop, calls=%fused_computation.14 | loop fusion | flops 512 | bytes 4096 | tf_op jit(solution)/shard_map/div | solution.py:198
  (9 shorter events, 0.2 us)
Async XLA Ops:
  0.6 9.9 %copy-start.4 = (s32[128,128]{1,0:T(8,128)S(1)}, s32[128,128]{1,0:T(8,128)}, u32[]{:S(2)}) copy-start(s32[128,128]{1,0:T(8,128)} %param.8) | copy-start | bytes 196612
  0.6 14.6 %collective-permute-start = (f32[3,128,128]{2,1,0:T(8,128)}, f32[3,128,128]{2,1,0:T(8,128)S(1)}, u32[]{:S(2)}, u32[]{:S(2)}) collective-permute-start(f32[3,128,128]{2,1,0:T(8,128)} %bitcast.29), channel_id=1, source_target_pairs={{0,496},{16,0},{32,16},{48,32},{64,48},{80,64},{96,80},{112,96},{1... | collective-permute-start | bytes 589832 | tf_op jit(solution)/shard_map/ppermute | solution.py:28
  10.5 0.8 %copy-start.5 = (s32[128,128]{1,0:T(8,128)S(1)}, s32[128,128]{1,0:T(8,128)}, u32[]{:S(2)}) copy-start(s32[128,128]{1,0:T(8,128)} %param.9) | copy-start | bytes 196612
  10.5 0.8 %copy-start.9 = (f32[8]{0:T(128)S(1)}, f32[8]{0:T(128)}, u32[]{:S(2)}) copy-start(f32[8]{0:T(128)} %param.10) | copy-start | bytes 100
  11.5 0.8 %copy-start.6 = (f32[128,128]{1,0:T(8,128)S(1)}, f32[128,128]{1,0:T(8,128)}, u32[]{:S(2)}) copy-start(f32[128,128]{1,0:T(8,128)} %param.11) | copy-start | bytes 196612
  12.3 0.8 %copy-start.7 = (f32[128,128]{1,0:T(8,128)S(1)}, f32[128,128]{1,0:T(8,128)}, u32[]{:S(2)}) copy-start(f32[128,128]{1,0:T(8,128)} %param.12) | copy-start | bytes 196612
  13.2 0.8 %copy-start.8 = (f32[128,128]{1,0:T(8,128)S(1)}, f32[128,128]{1,0:T(8,128)}, u32[]{:S(2)}) copy-start(f32[128,128]{1,0:T(8,128)} %param.13) | copy-start | bytes 196612
  14.0 0.8 %copy-start = (f32[8,128,128]{2,1,0:T(8,128)}, f32[8,128,128]{2,1,0:T(8,128)S(1)}, u32[]{:S(2)}) copy-start(f32[8,128,128]{2,1,0:T(8,128)S(1)} %bitcast_dynamic-update-slice_fusion.own_ref) | copy-start | bytes 1572868
  15.2 0.7 %copy-start.1 = (f32[3,128,128]{2,1,0:T(8,128)}, f32[3,128,128]{2,1,0:T(8,128)S(1)}, u32[]{:S(2)}) copy-start(f32[3,128,128]{2,1,0:T(8,128)S(1)} %collective-permute-done.next_ref) | copy-start | bytes 589828
  16.0 9.4 %collective-permute-start.1 = (f32[304,128]{1,0:T(8,128)S(1)}, f32[304,128]{1,0:T(8,128)S(1)}, u32[]{:S(2)}, u32[]{:S(2)}) collective-permute-start(f32[304,128]{1,0:T(8,128)S(1)} %pad_maximum_fusion), channel_id=1, source_target_pairs={{0,1},{1,2},{2,3},{3,4},{4,5},{5,6},{6,7},{7,8},{8,9},{9,10},{10,1... | collective-permute-start | bytes 466952 | tf_op jit(solution)/shard_map/ppermute | solution.py:188
  18.1 8.6 %collective-permute-start.2 = (f32[304,128]{1,0:T(8,128)S(1)}, f32[304,128]{1,0:T(8,128)S(1)}, u32[]{:S(2)}, u32[]{:S(2)}) collective-permute-start(f32[304,128]{1,0:T(8,128)S(1)} %pad_maximum_fusion.1), channel_id=1, source_target_pairs={{0,15},{1,0},{2,1},{3,2},{4,3},{5,4},{6,5},{7,6},{8,7},{9,8},{10,9... | collective-permute-start | bytes 466952 | tf_op jit(solution)/shard_map/ppermute | solution.py:189
  25.5 1.2 %copy-start.2 = (f32[304,128]{1,0:T(8,128)}, f32[304,128]{1,0:T(8,128)S(1)}, u32[]{:S(2)}) copy-start(f32[304,128]{1,0:T(8,128)S(1)} %collective-permute-done.1.left_ref) | copy-start | bytes 466948
  26.7 0.7 %copy-start.3 = (f32[304,128]{1,0:T(8,128)}, f32[304,128]{1,0:T(8,128)S(1)}, u32[]{:S(2)}) copy-start(f32[304,128]{1,0:T(8,128)S(1)} %collective-permute-done.2.right_ref) | copy-start | bytes 466948
  32.4 13.8 %collective-permute-start.3 = (f32[3,128,128]{2,1,0:T(8,128)}, f32[3,128,128]{2,1,0:T(8,128)S(1)}, u32[]{:S(2)}, u32[]{:S(2)}) collective-permute-start(f32[3,128,128]{2,1,0:T(8,128)} %get-tuple-element.8), channel_id=1, source_target_pairs={{0,16},{16,32},{32,48},{48,64},{64,80},{80,96},{96,112},{112,128},... | collective-permute-start | bytes 589832 | tf_op jit(solution)/shard_map/ppermute | solution.py:28
  37.3 18.5 %all-to-all-start = ((f32[32,4,128]{2,1,0:T(4,128)}), f32[32,4,128]{2,1,0:T(4,128)S(1)}, u32[]{:S(2)}, u32[]{:S(2)}) async-start(f32[32,4,128]{2,1,0:T(4,128)} %bitcast.33), calls=%async_computation | async-start | bytes 131072 | tf_op jit(solution)/shard_map/all_to_all | solution.py:158
